TPU v7x, 32 devices: a whole 2x2x4 slice. The times are simulated.
32 devices in a mesh: req: 4 (over z), seq: 2 (over x), tp: 4 (over y, core).
Axes of the slice: x: 2, y: 2, z: 4, core: 2. Of those that a mesh axis runs over, the one named last changes fastest.
Arguments:
- tokens: bfloat16 [8, 256, 2048], P('req', 'seq'), may hold values from -6 to 6
- w_query: bfloat16 [2048, 2048], P(('req', 'seq'), 'tp'), may hold values from -0.125 to 0.125
- w_key: bfloat16 [2048, 2048], P(('req', 'seq'), 'tp'), may hold values from -0.125 to 0.125
- w_value: bfloat16 [2048, 2048], P(('req', 'seq'), 'tp'), may hold values from -0.125 to 0.125
- q_gain: float32 [2048], P('tp'), may hold values from 1 to 4
- k_gain: float32 [2048], P('tp'), may hold values from 1 to 4
- cache_keys: bfloat16 [8, 4096, 2048], P('req', 'seq', 'tp'), may hold values from -140 to 140
- cache_values: bfloat16 [8, 4096, 2048], P('req', 'seq', 'tp'), may hold values from -6 to 6
- sink_keys: bfloat16 [8, 4, 2048], P('req', None, 'tp'), may hold values from -16 to 16
- sink_values: bfloat16 [8, 4, 2048], P('req', None, 'tp'), may hold values from -6 to 6
- sink_pos: int32 [8, 4], P('req'), may hold values from 0 to 8191
- cache_len: int32 [8], P('req'), may hold values from 0 to 32768
- span_len: int32 [8], P('req'), may hold values from 1 to 256, as said below
- window_len: int32 [8], P('req'), may hold values from 2048 to 4096, as said below
Outputs:
- attended: bfloat16 [8, 256, 2048], P('req', 'seq', 'tp')
Inputs may be any that keep to these rules, and one draw needn't show every extreme that they name: `span_len`: some request's span has exactly 256 live tokens. `window_len`: some request's window is exactly 4096.
All inputs are finite; a program needn't handle non-finite values.
Results may differ from a plain program's by a relative error of at most 0.022.
Values may be sent and summed in bfloat16 or wider, within the bound.
No kernel may reach another device: no remote copies, remote signals or barrier semaphores. Data moves between devices by JAX's collectives and lax.ppermute only.
A program may use at most 128 MiB of HBM per device.

v0:
```python
import jax
import jax.numpy as jnp
from jax import lax
from jax.sharding import PartitionSpec as P

D = 2048
HEAD_DIM = 128
WINDOW = 4096
SINKS = 4


rope_base = 500000.0
epsilon = 1e-06
lowest = -1e30


def rotate_heads(vectors, positions):
    half_dim = vectors.shape[-1] // 2
    powers = jnp.arange(half_dim, dtype=jnp.float32) * (2.0 / vectors.shape[-1])
    inverse = rope_base ** (-powers)
    angles = positions.astype(jnp.float32)[:, None] * inverse[None, :]
    cosine = jnp.cos(angles)[:, None, :]
    sine_part = jnp.sin(angles)[:, None, :]
    leading = vectors[..., :half_dim]
    trailing = vectors[..., half_dim:]
    return jnp.concatenate(
        [leading * cosine - trailing * sine_part, trailing * cosine + leading * sine_part], axis=-1
    )


def normalize_rotate(projected, squares, feature_gain, positions, model_width, head_size):
    factor = lax.rsqrt(squares / model_width + epsilon)
    normed = projected * factor[:, None] * feature_gain[None, :]
    shaped = normed.reshape(projected.shape[0], projected.shape[1] // head_size, head_size)
    return rotate_heads(shaped, positions).reshape(projected.shape).astype(jnp.bfloat16)


def partial_head(query_head, key_head, value_head, allowed, scaling):
    scores = (
        jnp.einsum("qd,kd->qk", query_head, key_head, preferred_element_type=jnp.float32) * scaling
    )
    highest = jnp.max(jnp.where(allowed, scores, lowest), axis=1)
    weights = jnp.where(allowed, jnp.exp(scores - highest[:, None]), 0.0)
    totals = jnp.sum(weights, axis=1)
    summed = jnp.dot(weights.astype(jnp.bfloat16), value_head, preferred_element_type=jnp.float32)
    return (summed, highest, totals)


def on_device(
    tokens,
    w_query,
    w_key,
    w_value,
    q_gain,
    k_gain,
    cache_keys,
    cache_values,
    sink_keys,
    sink_values,
    sink_pos,
    cache_len,
    span_len,
    window_len,
):
    req_local, span_local, model_width = tokens.shape
    local_cols = w_query.shape[1]
    heads_local = local_cols // HEAD_DIM
    seq_count = lax.axis_size("seq")
    seq_index = lax.axis_index("seq")
    span_total = span_local * seq_count
    slot_local = cache_keys.shape[1]
    scaling = HEAD_DIM ** (-0.5)
    token_rows = tokens.reshape(req_local * span_local, model_width)
    q_proj = jnp.dot(
        token_rows,
        lax.all_gather(w_query, ("req", "seq"), axis=0, tiled=True),
        preferred_element_type=jnp.float32,
    )
    k_proj = jnp.dot(
        token_rows,
        lax.all_gather(w_key, ("req", "seq"), axis=0, tiled=True),
        preferred_element_type=jnp.float32,
    )
    v_proj = jnp.dot(
        token_rows,
        lax.all_gather(w_value, ("req", "seq"), axis=0, tiled=True),
        preferred_element_type=jnp.float32,
    )
    q_squares, k_squares = lax.psum(
        (jnp.sum(q_proj * q_proj, axis=1), jnp.sum(k_proj * k_proj, axis=1)), "tp"
    )
    offsets = seq_index * span_local + jnp.arange(span_local, dtype=jnp.int32)
    positions = (cache_len[:, None] + offsets[None, :]).reshape(-1)
    q_local = normalize_rotate(q_proj, q_squares, q_gain, positions, D, HEAD_DIM).reshape(
        req_local, span_local, local_cols
    )
    k_rot = normalize_rotate(k_proj, k_squares, k_gain, positions, D, HEAD_DIM).reshape(
        req_local, span_local, local_cols
    )
    v_new = v_proj.astype(jnp.bfloat16).reshape(req_local, span_local, local_cols)
    q_whole = lax.all_gather(q_local, "seq", axis=1, tiled=True)
    block_rows = min(512, span_total)
    slot_index = seq_index * slot_local + jnp.arange(slot_local, dtype=jnp.int32)
    query_index = jnp.arange(span_total, dtype=jnp.int32)
    parts_sum, parts_high, parts_total = ([], [], [])
    for request in range(req_local):
        length_now = cache_len[request]
        window_now = window_len[request]
        slot_pos = length_now - 1 - jnp.mod(length_now - 1 - slot_index, WINDOW)
        keys_here = jnp.concatenate([cache_keys[request], k_rot[request]], axis=0)
        values_here = jnp.concatenate([cache_values[request], v_new[request]], axis=0)
        key_heads = keys_here.reshape(-1, heads_local, HEAD_DIM).transpose(1, 0, 2)
        value_heads = values_here.reshape(-1, heads_local, HEAD_DIM).transpose(1, 0, 2)
        query_heads = q_whole[request].reshape(span_total, heads_local, HEAD_DIM).transpose(1, 0, 2)
        block_sum, block_high, block_total = ([], [], [])
        for block_id in range(span_total // block_rows):
            first_row = block_id * block_rows
            rows_here = query_index[first_row : first_row + block_rows]
            edge_pos = length_now + rows_here - window_now
            allowed = jnp.concatenate(
                [
                    (slot_pos[None, :] >= 0) & (slot_pos[None, :] > edge_pos[:, None]),
                    offsets[None, :] <= rows_here[:, None],
                ],
                axis=1,
            )
            queries_block = query_heads[:, first_row : first_row + block_rows]

            def run_heads(unused, queries_block=queries_block, allowed=allowed):
                return lax.map(
                    lambda operands: partial_head(
                        operands[0], operands[1], operands[2], allowed, scaling
                    ),
                    (queries_block, key_heads, value_heads),
                )

            summed, highest, totals = run_heads(0)
            block_sum.append(summed)
            block_high.append(highest)
            block_total.append(totals)
        parts_sum.append(jnp.concatenate(block_sum, axis=1))
        parts_high.append(jnp.concatenate(block_high, axis=1))
        parts_total.append(jnp.concatenate(block_total, axis=1))
    part_sum = jnp.stack(parts_sum)[:, None]
    part_high = jnp.stack(parts_high)[:, None]
    part_total = jnp.stack(parts_total)[:, None]
    got_sum, got_high, got_total = (
        lax.all_to_all(part_sum, "seq", split_axis=3, concat_axis=1, tiled=True),
        lax.all_to_all(part_high, "seq", split_axis=3, concat_axis=1, tiled=True),
        lax.all_to_all(part_total, "seq", split_axis=3, concat_axis=1, tiled=True),
    )
    own_heads = q_local.reshape(req_local, span_local, heads_local, HEAD_DIM)
    sink_heads = sink_keys.reshape(req_local, SINKS, heads_local, HEAD_DIM)
    sink_vheads = sink_values.reshape(req_local, SINKS, heads_local, HEAD_DIM)
    sink_scores = (
        jnp.einsum("rqhd,rshd->rhqs", own_heads, sink_heads, preferred_element_type=jnp.float32)
        * scaling
    )
    sink_edge = cache_len[:, None] + offsets[None, :] - window_len[:, None]
    sink_allowed = sink_pos[:, None, None, :] <= sink_edge[:, None, :, None]
    sink_high = jnp.max(jnp.where(sink_allowed, sink_scores, lowest), axis=3)
    sink_weights = jnp.where(sink_allowed, jnp.exp(sink_scores - sink_high[..., None]), 0.0)
    sink_total = jnp.sum(sink_weights, axis=3)
    sink_sum = jnp.einsum(
        "rhqs,rshd->rhqd",
        sink_weights.astype(jnp.bfloat16),
        sink_vheads,
        preferred_element_type=jnp.float32,
    )
    all_high = jnp.concatenate([got_high, sink_high[:, None]], axis=1)
    all_total = jnp.concatenate([got_total, sink_total[:, None]], axis=1)
    all_parts = jnp.concatenate([got_sum, sink_sum[:, None]], axis=1)
    peak_value = jnp.max(all_high, axis=1, keepdims=True)
    factor = jnp.exp(all_high - peak_value)
    denominator = jnp.sum(all_total * factor, axis=1)
    numerator = jnp.sum(all_parts * factor[..., None], axis=1)
    live_rows = (offsets[None, :] < span_len[:, None])[:, None, :]
    safe_total = jnp.where(live_rows, denominator, 1.0)
    mixed = jnp.where(live_rows[..., None], numerator / safe_total[..., None], 0.0)
    return (
        mixed.transpose(0, 2, 1, 3).reshape(req_local, span_local, local_cols).astype(jnp.bfloat16)
    )


def solution(mesh):
    placed = (
        P("req", "seq", None),
        P(("req", "seq"), "tp"),
        P(("req", "seq"), "tp"),
        P(("req", "seq"), "tp"),
        P("tp"),
        P("tp"),
        P("req", "seq", "tp"),
        P("req", "seq", "tp"),
        P("req", None, "tp"),
        P("req", None, "tp"),
        P("req", None),
        P("req"),
        P("req"),
        P("req"),
    )
    return jax.shard_map(
        on_device, mesh=mesh, in_specs=placed, out_specs=P("req", "seq", "tp"), check_vma=False
    )
```

profile of v0, /device:TPU:0, one launch (start us, length us, event | category | flops | bytes accessed | tf_op | source)
XLA Modules:
  0.0 291.4 jit_solution(3076069375159025954)
XLA Ops:
  13.7 4.0 %fusion.57 = (bf16[1,2048,512]{2,1,0:T(8,128)(2,1)S(1)}, bf16[1,2048,512]{2,1,0:T(8,128)(2,1)}) fusion(bf16[2,2048,512]{2,1,0:T(8,128)(2,1)} %param.24), kind=kLoop, calls=%fused_computation.116 | loop fusion | bytes 8388608 | tf_op jit(solution)/shard_map/slice | solution.py:110
  19.0 2.3 fusion.56
  23.6 2.5 copy.166
  26.0 2.9 %copy.167 = bf16[1,2048,512]{1,2,0:T(8,128)(2,1)S(1)} copy(bf16[1,2048,512]{2,1,0:T(8,128)(2,1)} %get-tuple-element.201) | data formatting | bytes 4194304
  29.0 4.0 %copy.168 = bf16[1,2048,512]{1,2,0:T(8,128)(2,1)} copy(bf16[1,2048,512]{2,1,0:T(8,128)(2,1)} %get-tuple-element.204) | data formatting | bytes 4194304
  33.0 4.0 %copy.169 = bf16[1,2048,512]{1,2,0:T(8,128)(2,1)} copy(bf16[1,2048,512]{2,1,0:T(8,128)(2,1)} %get-tuple-element.202) | data formatting | bytes 4194304
  38.9 22.9 %all-gather.4.cloned.1.call-done = bf16[2048,512]{1,0:T(8,128)(2,1)} async-done(((bf16[256,512]{1,0:T(8,128)(2,1)}), bf16[2048,512]{1,0:T(8,128)(2,1)}) %all-gather.4.cloned.1.call-update) | async-done | bytes 2097168 | tf_op jit(solution)/shard_map/all_gather | solution.py:76
  61.9 3.1 %multiply_reduce_fusion.1 = (f32[256]{0:T(256)S(1)}, f32[256,512]{1,0:T(8,128)}) fusion(bf16[256,2048]{1,0:T(8,128)(2,1)S(1)} %bitcast.160, bf16[2048,512]{1,0:T(8,128)(2,1)} %all-gather.4.cloned.1.call-done), kind=kOutput, calls=%fused_computation.61 | convolution fusion | flops 537132800 | bytes 3671040 | tf_op jit(solution)/shard_map/dot_general | solution.py:74
  64.9 46.9 %all-gather.6.cloned.1.call-done = bf16[2048,512]{1,0:T(8,128)(2,1)} async-done(((bf16[256,512]{1,0:T(8,128)(2,1)}), bf16[2048,512]{1,0:T(8,128)(2,1)}) %all-gather.6.cloned.1.call-update) | async-done | bytes 2097168 | tf_op jit(solution)/shard_map/all_gather | solution.py:81
  111.8 3.1 %multiply_reduce_fusion = (f32[256]{0:T(256)S(1)}, f32[256,512]{1,0:T(8,128)}) fusion(bf16[256,2048]{1,0:T(8,128)(2,1)S(1)} %bitcast.161, bf16[2048,512]{1,0:T(8,128)(2,1)} %all-gather.6.cloned.1.call-done), kind=kOutput, calls=%fused_computation.59 | convolution fusion | flops 537132800 | bytes 3671040 | tf_op jit(solution)/shard_map/dot_general | solution.py:79
  114.9 5.6 %all-reduce = (f32[256]{0:T(256)S(1)}, f32[256]{0:T(256)S(1)}) all-reduce(f32[256]{0:T(256)S(1)} %get-tuple-element.225, f32[256]{0:T(256)S(1)} %get-tuple-element.227), channel_id=1, replica_groups=mesh['req'=4,'seq'=2,'tp'=4] {'tp'}, use_global_device_ids=true, to_apply=%region_1.0 | all-reduce | flops 512 | bytes 4096 | tf_op jit(solution)/shard_map/psum | solution.py:89
  120.6 2.0 multiply_multiply_fusion.1
  122.6 2.1 copy.154
  127.4 2.0 multiply_multiply_fusion
  129.3 2.1 copy.155
  132.6 9.3 %all_gather.13 = bf16[2,256,512]{2,1,0:T(8,128)(2,1)S(1)} all-gather(bf16[2,128,512]{2,1,0:T(8,128)(2,1)S(1)} %copy.151), channel_id=1, replica_groups=mesh['req'=4,'seq'=2,'tp'=4] {'seq'}, dimensions={1}, use_global_device_ids=true | all-gather | bytes 786432 | tf_op jit(solution)/shard_map/all_gather | solution.py:101
  144.6 17.2 %all-gather.8.cloned.1.call-done = bf16[2048,512]{1,0:T(8,128)(2,1)} async-done(((bf16[256,512]{1,0:T(8,128)(2,1)}), bf16[2048,512]{1,0:T(8,128)(2,1)}) %all-gather.8.cloned.1.call-update) | async-done | bytes 2097168 | tf_op jit(solution)/shard_map/all_gather | solution.py:86
  161.8 2.3 convolution_convert_fusion
  165.5 3.2 %maximum_bitcast_fusion = bf16[4,2176,128]{1,2,0:T(8,128)(2,1)} fusion(bf16[128,4,128]{0,2,1:T(8,128)(2,1)S(1)} %fusion.39, bf16[2048,4,128]{0,2,1:T(8,128)(2,1)} %bitcast.168), kind=kLoop, calls=%fused_computation.42 | loop fusion | flops 4456448 | bytes 4456448 | tf_op jit(solution)/shard_map/transpose | solution.py:112
  171.3 36.7 %while.28 = (s32[]{:T(128)}, f32[4,256,128]{2,0,1:T(4,128)}, f32[4,256]{1,0:T(4,128)S(1)}, f32[4,256]{1,0:T(4,128)S(1)}, bf16[4,256,128]{1,2,0:T(8,128)(2,1)}, /...) while((s32[]{:T(128)}, f32[4,256,128]{2,0,1:T(4,128)}, ...), condition=%wide.region_7.8_spmd, body=%wide.region_4.7_spmd.sunk | while | flops 290225664 | bytes 12166797 | solution.py:130
  171.3 2.0 select_reduce_fusion.5
  175.8 4.6 %dynamic_update_slice.26 = f32[4,256,128]{2,0,1:T(4,128)} dynamic-update-slice(f32[4,256,128]{2,0,1:T(4,128)} %get-tuple-element.384, f32[1,256,128]{2,0,1:T(1,128)S(1)} %bitcast.163, s32[]{:T(128)} %get-tuple-element.383, s32[]{:T(128)} %constant.86.clone.1..sunk, s32[]{:T(128)} %constant.86.clone.1..sunk) | dynamic-update-slice | bytes 262148 | tf_op jit(solution)/shard_map/while/body/jit(dynamic_update_index_in_dim)/dynamic_update_slice | solution.py:130
  180.4 2.0 select_reduce_fusion.5
  183.1 1.8 fusion.78
  185.0 4.6 %dynamic_update_slice.26 = f32[4,256,128]{2,0,1:T(4,128)} dynamic-update-slice(f32[4,256,128]{2,0,1:T(4,128)} %get-tuple-element.384, f32[1,256,128]{2,0,1:T(1,128)S(1)} %bitcast.163, s32[]{:T(128)} %get-tuple-element.383, s32[]{:T(128)} %constant.86.clone.1..sunk, s32[]{:T(128)} %constant.86.clone.1..sunk) | dynamic-update-slice | bytes 262148 | tf_op jit(solution)/shard_map/while/body/jit(dynamic_update_index_in_dim)/dynamic_update_slice | solution.py:130
  189.6 2.0 select_reduce_fusion.5
  192.3 1.8 fusion.78
  194.2 4.6 %dynamic_update_slice.26 = f32[4,256,128]{2,0,1:T(4,128)} dynamic-update-slice(f32[4,256,128]{2,0,1:T(4,128)} %get-tuple-element.384, f32[1,256,128]{2,0,1:T(1,128)S(1)} %bitcast.163, s32[]{:T(128)} %get-tuple-element.383, s32[]{:T(128)} %constant.86.clone.1..sunk, s32[]{:T(128)} %constant.86.clone.1..sunk) | dynamic-update-slice | bytes 262148 | tf_op jit(solution)/shard_map/while/body/jit(dynamic_update_index_in_dim)/dynamic_update_slice | solution.py:130
  198.8 2.0 select_reduce_fusion.5
  203.3 4.6 %dynamic_update_slice.26 = f32[4,256,128]{2,0,1:T(4,128)} dynamic-update-slice(f32[4,256,128]{2,0,1:T(4,128)} %get-tuple-element.384, f32[1,256,128]{2,0,1:T(1,128)S(1)} %bitcast.163, s32[]{:T(128)} %get-tuple-element.383, s32[]{:T(128)} %constant.86.clone.1..sunk, s32[]{:T(128)} %constant.86.clone.1..sunk) | dynamic-update-slice | bytes 262148 | tf_op jit(solution)/shard_map/while/body/jit(dynamic_update_index_in_dim)/dynamic_update_slice | solution.py:130
  208.0 3.4 %fusion.34 = bf16[4,2176,128]{1,2,0:T(8,128)(2,1)} fusion(bf16[256,4,64]{0,2,1:T(8,128)(2,1)} %copy-done.7, bf16[256,4,64]{0,2,1:T(8,128)(2,1)S(1)} %get-tuple-element.205, bf16[2048,4,128]{0,2,1:T(8,128)(2,1)} %bitcast.166), kind=kLoop, calls=%fused_computation.41 | loop fusion | flops 10027008 | bytes 4587520 | tf_op jit(solution)/shard_map/transpose | solution.py:112
  215.7 36.7 %while.29 = (s32[]{:T(128)}, f32[4,256,128]{2,0,1:T(4,128)}, f32[4,256]{1,0:T(4,128)S(1)}, f32[4,256]{1,0:T(4,128)S(1)}, bf16[4,256,128]{1,2,0:T(8,128)(2,1)}, /...) while((s32[]{:T(128)}, f32[4,256,128]{2,0,1:T(4,128)}, ...), condition=%wide.region_11.12_spmd, body=%wide.region_8.11_spmd.sunk | while | flops 290225664 | bytes 12166797 | solution.py:130
  215.7 2.0 select_reduce_fusion.6
  220.3 4.6 %dynamic_update_slice.29 = f32[4,256,128]{2,0,1:T(4,128)} dynamic-update-slice(f32[4,256,128]{2,0,1:T(4,128)} %get-tuple-element.354, f32[1,256,128]{2,0,1:T(1,128)S(1)} %bitcast.164, s32[]{:T(128)} %get-tuple-element.353, s32[]{:T(128)} %constant.86.clone.1..sunk.1, s32[]{:T(128)} %constant.86.clone.1..sunk.1) | dynamic-update-slice | bytes 262148 | tf_op jit(solution)/shard_map/while/body/jit(dynamic_update_index_in_dim)/dynamic_update_slice | solution.py:130
  224.9 2.0 select_reduce_fusion.6
  227.6 1.8 fusion.82
  229.4 4.6 %dynamic_update_slice.29 = f32[4,256,128]{2,0,1:T(4,128)} dynamic-update-slice(f32[4,256,128]{2,0,1:T(4,128)} %get-tuple-element.354, f32[1,256,128]{2,0,1:T(1,128)S(1)} %bitcast.164, s32[]{:T(128)} %get-tuple-element.353, s32[]{:T(128)} %constant.86.clone.1..sunk.1, s32[]{:T(128)} %constant.86.clone.1..sunk.1) | dynamic-update-slice | bytes 262148 | tf_op jit(solution)/shard_map/while/body/jit(dynamic_update_index_in_dim)/dynamic_update_slice | solution.py:130
  234.1 2.0 select_reduce_fusion.6
  236.8 1.8 fusion.82
  238.6 4.6 %dynamic_update_slice.29 = f32[4,256,128]{2,0,1:T(4,128)} dynamic-update-slice(f32[4,256,128]{2,0,1:T(4,128)} %get-tuple-element.354, f32[1,256,128]{2,0,1:T(1,128)S(1)} %bitcast.164, s32[]{:T(128)} %get-tuple-element.353, s32[]{:T(128)} %constant.86.clone.1..sunk.1, s32[]{:T(128)} %constant.86.clone.1..sunk.1) | dynamic-update-slice | bytes 262148 | tf_op jit(solution)/shard_map/while/body/jit(dynamic_update_index_in_dim)/dynamic_update_slice | solution.py:130
  243.2 2.0 select_reduce_fusion.6
  245.9 1.8 fusion.82
  247.8 4.6 %dynamic_update_slice.29 = f32[4,256,128]{2,0,1:T(4,128)} dynamic-update-slice(f32[4,256,128]{2,0,1:T(4,128)} %get-tuple-element.354, f32[1,256,128]{2,0,1:T(1,128)S(1)} %bitcast.164, s32[]{:T(128)} %get-tuple-element.353, s32[]{:T(128)} %constant.86.clone.1..sunk.1, s32[]{:T(128)} %constant.86.clone.1..sunk.1) | dynamic-update-slice | bytes 262148 | tf_op jit(solution)/shard_map/while/body/jit(dynamic_update_index_in_dim)/dynamic_update_slice | solution.py:130
  253.6 3.2 %all-to-all-start.1 = ((f32[2,1,1024]{2,1,0:T(1,128)}), f32[2,1,1024]{2,1,0:T(1,128)S(1)}, u32[]{:S(2)}, u32[]{:S(2)}) async-start(f32[2,1,1024]{2,1,0:T(1,128)} %reshape.312), calls=%async_computation.1 | async-start | bytes 16384 | tf_op jit(solution)/shard_map/all_to_all | solution.py:149
  260.6 3.2 %all-to-all-start.2 = ((f32[2,1,1024]{2,1,0:T(1,128)}), f32[2,1,1024]{2,1,0:T(1,128)S(1)}, u32[]{:S(2)}, u32[]{:S(2)}) async-start(f32[2,1,1024]{2,1,0:T(1,128)} %reshape.314), calls=%async_computation.2 | async-start | bytes 16384 | tf_op jit(solution)/shard_map/all_to_all | solution.py:150
  265.6 2.0 all-to-all-done.2
  267.7 3.6 %all-to-all-start = ((f32[2,1,4,256,128]{4,2,0,1,3:T(4,128)}), f32[2,1,4,256,128]{4,2,0,1,3:T(4,128)S(1)}, u32[]{:S(2)}, u32[]{:S(2)}) async-start(f32[2,1,4,256,128]{4,2,0,1,3:T(4,128)} %maximum_bitcast_fusion.3), calls=%async_computation | async-start | bytes 2097152 | tf_op jit(solution)/shard_map/all_to_all | solution.py:148
  272.6 10.3 %all-to-all-done = f32[2,1,4,256,128]{4,2,0,1,3:T(4,128)S(1)} async-done(((f32[2,1,4,256,128]{4,2,0,1,3:T(4,128)}), f32[2,1,4,256,128]{4,2,0,1,3:T(4,128)S(1)}, u32[]{:S(2)}, u32[]{:S(2)}) %all-to-all-start) | async-done | bytes 1048608 | tf_op jit(solution)/shard_map/all_to_all | solution.py:148
  (152 shorter events, 47.5 us)
Async XLA Ops:
  6.5 55.3 %copy-start = (bf16[2,128,2048]{2,1,0:T(8,128)(2,1)S(1)}, bf16[2,128,2048]{2,1,0:T(8,128)(2,1)}, u32[]{:S(2)}) copy-start(bf16[2,128,2048]{2,1,0:T(8,128)(2,1)} %param.18) | copy-start | bytes 3145732
  6.5 55.3 %all-gather.4.cloned.1.call-start = ((), (), s32[]{:S(2)}) async-start(), calls=%async_computation.3 | async-start | bytes 2359296 | tf_op jit(solution)/shard_map/all_gather | solution.py:76
  7.3 104.6 %all-gather.6.cloned.1.call-start = ((), (), s32[]{:S(2)}) async-start(), calls=%async_computation.4 | async-start | bytes 2359296 | tf_op jit(solution)/shard_map/all_gather | solution.py:81
  8.0 153.8 %all-gather.8.cloned.1.call-start = ((), (), s32[]{:S(2)}) async-start(), calls=%async_computation.5 | async-start | bytes 2359296 | tf_op jit(solution)/shard_map/all_gather | solution.py:86
  13.6 5.3 %copy-start.4 = (bf16[2,2048,512]{2,1,0:T(8,128)(2,1)S(1)}, bf16[2,2048,512]{2,1,0:T(8,128)(2,1)}, u32[]{:S(2)}) copy-start(bf16[2,2048,512]{2,1,0:T(8,128)(2,1)} %param.25) | copy-start | bytes 12582916
  19.0 2.3 copy-start.19
  19.0 3.3 %copy-start.17 = (s32[2,4]{1,0:T(2,128)S(1)}, s32[2,4]{1,0:T(2,128)}, u32[]{:S(2)}) copy-start(s32[2,4]{1,0:T(2,128)} %param.28) | copy-start | bytes 100
  22.2 102.4 %copy-start.9 = (f32[256,64]{0,1:T(8,128)}, f32[256,64]{0,1:T(8,128)S(1)}, u32[]{:S(2)}) copy-start(f32[256,64]{0,1:T(8,128)S(1)} %get-tuple-element.217) | copy-start | bytes 196612
  22.3 102.4 %copy-start.10 = (f32[256,64]{0,1:T(8,128)}, f32[256,64]{0,1:T(8,128)S(1)}, u32[]{:S(2)}) copy-start(f32[256,64]{0,1:T(8,128)S(1)} %get-tuple-element.218) | copy-start | bytes 196612
  64.9 55.6 %copy-start.14 = (f32[512]{0:T(512)S(1)}, f32[512]{0:T(512)}, u32[]{:S(2)}) copy-start(f32[512]{0:T(512)} %param.22) | copy-start | bytes 6148
  120.6 6.8 %copy-start.15 = (f32[512]{0:T(512)S(1)}, f32[512]{0:T(512)}, u32[]{:S(2)}) copy-start(f32[512]{0:T(512)} %param.23) | copy-start | bytes 6148
  144.6 20.9 %copy-start.7 = (bf16[256,4,64]{0,2,1:T(8,128)(2,1)}, bf16[256,4,64]{0,2,1:T(8,128)(2,1)S(1)}, u32[]{:S(2)}) copy-start(bf16[256,4,64]{0,2,1:T(8,128)(2,1)S(1)} %get-tuple-element.206) | copy-start | bytes 393220
  165.5 3.2 %copy-start.11 = (bf16[128,512]{0,1:T(8,128)(2,1)S(1)}, bf16[128,512]{0,1:T(8,128)(2,1)}, u32[]{:S(2)}) copy-start(bf16[128,512]{0,1:T(8,128)(2,1)} %copy.152) | copy-start | bytes 393220
  171.3 2.0 copy-start.2
  180.4 2.0 copy-start.2
  189.6 2.0 copy-start.2
  198.8 2.0 copy-start.2
  207.9 3.4 %copy-start.8 = (bf16[1,256,512]{2,1,0:T(8,128)(2,1)S(1)}, bf16[1,256,512]{2,1,0:T(8,128)(2,1)}, u32[]{:S(2)}) copy-start(bf16[1,256,512]{2,1,0:T(8,128)(2,1)} %get-tuple-element.210) | copy-start | bytes 786436
  207.9 5.3 %copy-start.3 = (bf16[1,2048,512]{1,2,0:T(8,128)(2,1)S(1)}, bf16[1,2048,512]{1,2,0:T(8,128)(2,1)}, u32[]{:S(2)}) copy-start(bf16[1,2048,512]{1,2,0:T(8,128)(2,1)} %copy.169) | copy-start | bytes 6291460
  215.7 2.0 copy-start.1
  224.9 2.0 copy-start.1
  234.1 2.0 copy-start.1
  243.2 2.0 copy-start.1
  252.4 4.7 %copy-start.5 = (f32[4,256,128]{2,0,1:T(4,128)S(1)}, f32[4,256,128]{2,0,1:T(4,128)}, u32[]{:S(2)}) copy-start(f32[4,256,128]{2,0,1:T(4,128)} %get-tuple-element.94) | copy-start | bytes 1572868
  252.4 4.7 %copy-start.6 = (f32[4,256,128]{2,0,1:T(4,128)S(1)}, f32[4,256,128]{2,0,1:T(4,128)}, u32[]{:S(2)}) copy-start(f32[4,256,128]{2,0,1:T(4,128)} %get-tuple-element.93) | copy-start | bytes 1572868
  252.4 5.9 %copy-start.12 = (bf16[256,4,128]{2,0,1:T(8,128)(2,1)S(1)}, bf16[256,4,128]{2,0,1:T(8,128)(2,1)}, u32[]{:S(2)}) copy-start(bf16[256,4,128]{2,0,1:T(8,128)(2,1)} %copy.140) | copy-start | bytes 786436
  252.4 5.9 %copy-start.18 = (bf16[2,4,512]{2,1,0:T(4,128)(2,1)S(1)}, bf16[2,4,512]{2,1,0:T(4,128)(2,1)}, u32[]{:S(2)}) copy-start(bf16[2,4,512]{2,1,0:T(4,128)(2,1)} %param.26) | copy-start | bytes 24580
  252.4 6.1 %copy-start.13 = (bf16[2,4,512]{2,1,0:T(4,128)(2,1)S(1)}, bf16[2,4,512]{2,1,0:T(4,128)(2,1)}, u32[]{:S(2)}) copy-start(bf16[2,4,512]{2,1,0:T(4,128)(2,1)} %param.27) | copy-start | bytes 24580
  253.6 7.0 %all-to-all-start.1 = ((f32[2,1,1024]{2,1,0:T(1,128)}), f32[2,1,1024]{2,1,0:T(1,128)S(1)}, u32[]{:S(2)}, u32[]{:S(2)}) async-start(f32[2,1,1024]{2,1,0:T(1,128)} %reshape.312), calls=%async_computation.1 | async-start | bytes 16384 | tf_op jit(solution)/shard_map/all_to_all | solution.py:149
  258.3 14.3 %copy-start.16 = (pred[2,128]{1,0:T(4,128)(4,1)S(1)}, pred[2,128]{1,0:T(4,128)(4,1)}, u32[]{:S(2)}) copy-start(pred[2,128]{1,0:T(4,128)(4,1)} %broadcast_compare_fusion.3) | copy-start | bytes 772
  260.6 7.0 %all-to-all-start.2 = ((f32[2,1,1024]{2,1,0:T(1,128)}), f32[2,1,1024]{2,1,0:T(1,128)S(1)}, u32[]{:S(2)}, u32[]{:S(2)}) async-start(f32[2,1,1024]{2,1,0:T(1,128)} %reshape.314), calls=%async_computation.2 | async-start | bytes 16384 | tf_op jit(solution)/shard_map/all_to_all | solution.py:150
  267.7 15.3 %all-to-all-start = ((f32[2,1,4,256,128]{4,2,0,1,3:T(4,128)}), f32[2,1,4,256,128]{4,2,0,1,3:T(4,128)S(1)}, u32[]{:S(2)}, u32[]{:S(2)}) async-start(f32[2,1,4,256,128]{4,2,0,1,3:T(4,128)} %maximum_bitcast_fusion.3), calls=%async_computation | async-start | bytes 2097152 | tf_op jit(solution)/shard_map/all_to_all | solution.py:148
Sparse Core Ops, SparseCore 0:
  9.5 52.3 all-gather.3
  64.0 47.7 all-gather.5
  114.0 47.7 all-gather.7
where the time goes:
time: 293 us; the launch traced here: 291 us
  waiting for transfers between devices  102 us (35%)
  local copies, waits for them, and re-layouts  78.6 us (27%)
  matrix products  39.6 us (14%)
  other arithmetic  31 us (11%)
  blocking collectives  15 us (5%)
  between operations  14.8 us (5%)
  starting transfers between devices  10.1 us (3%)
    all_gather x1, waiting for transfers between devices, on_device(): lax.all_gather(w_key, ('req', 'seq'), axis=0, tiled=True)  46.9 us
    dynamic_update_slice x24, local copies, waits for them, and re-layouts, run_heads(): lax.map(lambda operands: partial_head(operands[0], operands[1], operands[...  37.3 us
    all_gather x1, waiting for transfers between devices, on_device(): lax.all_gather(w_query, ('req', 'seq'), axis=0, tiled=True)  22.9 us
    all_gather x1, waiting for transfers between devices, on_device(): lax.all_gather(w_value, ('req', 'seq'), axis=0, tiled=True)  17.2 us
    unnamed x46, local copies, waits for them, and re-layouts  16.3 us
    dot_general x8, matrix products, partial_head(): jnp.einsum('qd,kd->qk', query_head, key_head, preferred_element_type=jnp....  15.9 us
    dot_general x8, matrix products, partial_head(): jnp.dot(weights.astype(jnp.bfloat16), value_head, preferred_element_type=...  14.6 us
    all_to_all x1, waiting for transfers between devices, on_device(): lax.all_to_all(part_sum, 'seq', split_axis=3, concat_axis=1, tiled=True)  10.3 us
  transfers between devices with their start and end apart: 6, of which 6 were waited for; matrix products, arithmetic and copies ran while one was open for 19% of the time, Pallas kernels for 0%

commit v1 on v0

v1 whole, which is shorter than its diff:
```python
import functools

import jax
import jax.numpy as jnp
from jax import lax
from jax.experimental import pallas as pl
from jax.experimental.pallas import tpu as pltpu
from jax.sharding import PartitionSpec as P

D = 2048
HEAD_DIM = 128
WINDOW = 4096
SINKS = 4


rope_base = 500000.0
epsilon = 1e-06
lowest = -1e30


def rotate_heads(vectors, positions):
    half_dim = vectors.shape[-1] // 2
    powers = jnp.arange(half_dim, dtype=jnp.float32) * (2.0 / vectors.shape[-1])
    inverse = rope_base ** (-powers)
    angles = positions.astype(jnp.float32)[:, None] * inverse[None, :]
    cosine = jnp.cos(angles)[:, None, :]
    sine_part = jnp.sin(angles)[:, None, :]
    leading = vectors[..., :half_dim]
    trailing = vectors[..., half_dim:]
    return jnp.concatenate(
        [leading * cosine - trailing * sine_part, trailing * cosine + leading * sine_part], axis=-1
    )


def normalize_rotate(projected, squares, feature_gain, positions, model_width, head_size):
    factor = lax.rsqrt(squares / model_width + epsilon)
    normed = projected * factor[:, None] * feature_gain[None, :]
    shaped = normed.reshape(projected.shape[0], projected.shape[1] // head_size, head_size)
    return rotate_heads(shaped, positions).reshape(projected.shape).astype(jnp.bfloat16)


def attention_kernel(
    len_ref, win_ref, seq_ref, q_ref, ck_ref, cv_ref, nk_ref, nv_ref, o_ref, m_ref, l_ref, *, scaling
):
    r = pl.program_id(0)
    length_now = len_ref[r]
    window_now = win_ref[r]
    seq_index = seq_ref[0]
    queries = q_ref[0]
    rows, slots, span_local = queries.shape[0], ck_ref.shape[1], nk_ref.shape[1]
    dims = (((1,), (1,)), ((), ()))
    cache_scores = (
        lax.dot_general(queries, ck_ref[0], dims, preferred_element_type=jnp.float32) * scaling
    )
    span_scores = (
        lax.dot_general(queries, nk_ref[0], dims, preferred_element_type=jnp.float32) * scaling
    )
    row_c = lax.broadcasted_iota(jnp.int32, (rows, slots), 0)
    slot = lax.broadcasted_iota(jnp.int32, (rows, slots), 1) + seq_index * slots
    edge = length_now + row_c - window_now
    slot_pos = length_now - 1 - ((length_now - 1 - slot) & (WINDOW - 1))
    cache_ok = (slot_pos >= 0) & (slot_pos > edge)
    row_s = lax.broadcasted_iota(jnp.int32, (rows, span_local), 0)
    key_s = lax.broadcasted_iota(jnp.int32, (rows, span_local), 1) + seq_index * span_local
    span_ok = key_s <= row_s
    highest = jnp.maximum(
        jnp.max(jnp.where(cache_ok, cache_scores, lowest), axis=1, keepdims=True),
        jnp.max(jnp.where(span_ok, span_scores, lowest), axis=1, keepdims=True),
    )
    cache_w = jnp.where(cache_ok, jnp.exp(cache_scores - highest), 0.0)
    span_w = jnp.where(span_ok, jnp.exp(span_scores - highest), 0.0)
    totals = jnp.sum(cache_w, axis=1, keepdims=True) + jnp.sum(span_w, axis=1, keepdims=True)
    summed = jnp.dot(
        cache_w.astype(jnp.bfloat16), cv_ref[0], preferred_element_type=jnp.float32
    ) + jnp.dot(span_w.astype(jnp.bfloat16), nv_ref[0], preferred_element_type=jnp.float32)
    o_ref[0, 0] = summed
    m_ref[0, 0] = highest
    l_ref[0, 0] = totals


def local_attention(q_whole, cache_keys, cache_values, k_rot, v_new, cache_len, window_len, seq_index):
    req_local, span_total, local_cols = q_whole.shape
    heads_local = local_cols // HEAD_DIM
    slot_local = cache_keys.shape[1]
    span_local = k_rot.shape[1]
    kernel = functools.partial(attention_kernel, scaling=HEAD_DIM ** (-0.5))
    grid_spec = pltpu.PrefetchScalarGridSpec(
        num_scalar_prefetch=3,
        grid=(req_local, heads_local),
        in_specs=[
            pl.BlockSpec((1, span_total, HEAD_DIM), lambda r, h, *_: (r, 0, h)),
            pl.BlockSpec((1, slot_local, HEAD_DIM), lambda r, h, *_: (r, 0, h)),
            pl.BlockSpec((1, slot_local, HEAD_DIM), lambda r, h, *_: (r, 0, h)),
            pl.BlockSpec((1, span_local, HEAD_DIM), lambda r, h, *_: (r, 0, h)),
            pl.BlockSpec((1, span_local, HEAD_DIM), lambda r, h, *_: (r, 0, h)),
        ],
        out_specs=[
            pl.BlockSpec((1, 1, span_total, HEAD_DIM), lambda r, h, *_: (r, h, 0, 0)),
            pl.BlockSpec((1, 1, span_total, 1), lambda r, h, *_: (r, h, 0, 0)),
            pl.BlockSpec((1, 1, span_total, 1), lambda r, h, *_: (r, h, 0, 0)),
        ],
    )
    return pl.pallas_call(
        kernel,
        grid_spec=grid_spec,
        out_shape=[
            jax.ShapeDtypeStruct((req_local, heads_local, span_total, HEAD_DIM), jnp.float32),
            jax.ShapeDtypeStruct((req_local, heads_local, span_total, 1), jnp.float32),
            jax.ShapeDtypeStruct((req_local, heads_local, span_total, 1), jnp.float32),
        ],
    )(
        cache_len,
        window_len,
        jnp.reshape(seq_index, (1,)).astype(jnp.int32),
        q_whole,
        cache_keys,
        cache_values,
        k_rot,
        v_new,
    )


def on_device(
    tokens,
    w_query,
    w_key,
    w_value,
    q_gain,
    k_gain,
    cache_keys,
    cache_values,
    sink_keys,
    sink_values,
    sink_pos,
    cache_len,
    span_len,
    window_len,
):
    req_local, span_local, model_width = tokens.shape
    local_cols = w_query.shape[1]
    heads_local = local_cols // HEAD_DIM
    seq_count = lax.axis_size("seq")
    seq_index = lax.axis_index("seq")
    span_total = span_local * seq_count
    scaling = HEAD_DIM ** (-0.5)
    token_rows = tokens.reshape(req_local * span_local, model_width)
    w_all = lax.all_gather(
        jnp.concatenate([w_query, w_key, w_value], axis=1), ("req", "seq"), axis=0, tiled=True
    )
    proj = jnp.dot(token_rows, w_all, preferred_element_type=jnp.float32)
    q_proj = proj[:, :local_cols]
    k_proj = proj[:, local_cols : 2 * local_cols]
    v_proj = proj[:, 2 * local_cols :]
    q_squares, k_squares = lax.psum(
        (jnp.sum(q_proj * q_proj, axis=1), jnp.sum(k_proj * k_proj, axis=1)), "tp"
    )
    offsets = seq_index * span_local + jnp.arange(span_local, dtype=jnp.int32)
    positions = (cache_len[:, None] + offsets[None, :]).reshape(-1)
    q_local = normalize_rotate(q_proj, q_squares, q_gain, positions, D, HEAD_DIM).reshape(
        req_local, span_local, local_cols
    )
    k_rot = normalize_rotate(k_proj, k_squares, k_gain, positions, D, HEAD_DIM).reshape(
        req_local, span_local, local_cols
    )
    v_new = v_proj.astype(jnp.bfloat16).reshape(req_local, span_local, local_cols)
    q_whole = lax.all_gather(q_local, "seq", axis=1, tiled=True)
    part_sum, part_high, part_total = local_attention(
        q_whole, cache_keys, cache_values, k_rot, v_new, cache_len, window_len, seq_index
    )
    stats = jnp.concatenate([part_high, part_total], axis=3)
    got_sum = lax.all_to_all(
        part_sum.reshape(req_local, heads_local, seq_count, span_local, HEAD_DIM),
        "seq",
        split_axis=2,
        concat_axis=2,
        tiled=True,
    )
    got_stats = lax.all_to_all(
        stats.reshape(req_local, heads_local, seq_count, span_local, 2),
        "seq",
        split_axis=2,
        concat_axis=2,
        tiled=True,
    )
    got_high = got_stats[..., 0]
    got_total = got_stats[..., 1]
    own_heads = q_local.reshape(req_local, span_local, heads_local, HEAD_DIM)
    sink_heads = sink_keys.reshape(req_local, SINKS, heads_local, HEAD_DIM)
    sink_vheads = sink_values.reshape(req_local, SINKS, heads_local, HEAD_DIM)
    sink_scores = (
        jnp.einsum("rqhd,rshd->rhqs", own_heads, sink_heads, preferred_element_type=jnp.float32)
        * scaling
    )
    sink_edge = cache_len[:, None] + offsets[None, :] - window_len[:, None]
    sink_allowed = sink_pos[:, None, None, :] <= sink_edge[:, None, :, None]
    sink_high = jnp.max(jnp.where(sink_allowed, sink_scores, lowest), axis=3)
    sink_weights = jnp.where(sink_allowed, jnp.exp(sink_scores - sink_high[..., None]), 0.0)
    sink_total = jnp.sum(sink_weights, axis=3)
    sink_sum = jnp.einsum(
        "rhqs,rshd->rhqd",
        sink_weights.astype(jnp.bfloat16),
        sink_vheads,
        preferred_element_type=jnp.float32,
    )
    all_high = jnp.concatenate([got_high, sink_high[:, :, None]], axis=2)
    all_total = jnp.concatenate([got_total, sink_total[:, :, None]], axis=2)
    all_parts = jnp.concatenate([got_sum, sink_sum[:, :, None]], axis=2)
    peak_value = jnp.max(all_high, axis=2, keepdims=True)
    factor = jnp.exp(all_high - peak_value)
    denominator = jnp.sum(all_total * factor, axis=2)
    numerator = jnp.sum(all_parts * factor[..., None], axis=2)
    live_rows = (offsets[None, :] < span_len[:, None])[:, None, :]
    safe_total = jnp.where(live_rows, denominator, 1.0)
    mixed = jnp.where(live_rows[..., None], numerator / safe_total[..., None], 0.0)
    return (
        mixed.transpose(0, 2, 1, 3).reshape(req_local, span_local, local_cols).astype(jnp.bfloat16)
    )


def solution(mesh):
    placed = (
        P("req", "seq", None),
        P(("req", "seq"), "tp"),
        P(("req", "seq"), "tp"),
        P(("req", "seq"), "tp"),
        P("tp"),
        P("tp"),
        P("req", "seq", "tp"),
        P("req", "seq", "tp"),
        P("req", None, "tp"),
        P("req", None, "tp"),
        P("req", None),
        P("req"),
        P("req"),
        P("req"),
    )
    return jax.shard_map(
        on_device, mesh=mesh, in_specs=placed, out_specs=P("req", "seq", "tp"), check_vma=False
    )
```

time: 293 us -> 187 us (0.64)
  local copies, waits for them, and re-layouts: 78.6 us -> 9.75 us
  matrix products: 39.6 us -> 5.23 us
  other arithmetic: 31 us -> 4.62 us
  Pallas kernels: 0 us -> 16.6 us
  waiting for transfers between devices: 102 us -> 115 us
  starting transfers between devices: 10.1 us -> 6.85 us
    dynamic_update_slice x24 -> x0, local copies, waits for them, and re-layouts: 37.3 us -> none  [run_heads(): lax.map(lambda operands: partial_head(operands[0], operands[1], operands[...]
    dot_general x19 -> x1, matrix products: 39 us -> 4.67 us  [on_device(): proj = jnp.dot(token_rows, w_all, preferred_element_type=jnp.float32)]
    pallas_call x0 -> x1, Pallas kernels: none -> 16.6 us  [local_attention(): pl.pallas_call(kernel, grid_spec=grid_spec, out_shape=[jax.ShapeDtypeStru...]
    unnamed x46 -> x27, local copies, waits for them, and re-layouts: 16.3 us -> 0.84 us
    all_gather x3 -> x1, waiting for transfers between devices: 87 us -> 102 us  [on_device(): lax.all_gather(jnp.concatenate([w_query, w_key, w_value], axis=1), ('req'...]
    slice x8 -> x5, local copies, waits for them, and re-layouts: 12.2 us -> 1.64 us  [the longest x2 1.55 us: on_device(): v_proj = proj[:, 2 * local_cols:]]
    transpose x4 -> x0, other arithmetic: 9.77 us -> none  [the longest x2 6.6 us: on_device(): key_heads = keys_here.reshape(-1, heads_local, HEAD_DIM).transpose(1, 0, 2)]
    reduce_sum x10 -> x3, other arithmetic: 5.85 us -> 0.62 us  [the longest x1 0.47 us: on_device(): numerator = jnp.sum(all_parts * factor[..., None], axis=2)]
  transfers between devices with their start and end apart: 6 -> 3, of which waited for: 6 -> 3; matrix products, arithmetic and copies ran while one was open for 19% -> 1% of each run, Pallas kernels for 0% -> 0%
where the time goes in v1:
time: 187 us
  waiting for transfers between devices  115 us (61%)
  Pallas kernels  16.6 us (9%)
  blocking collectives  14.5 us (8%)
  between operations  13.7 us (7%)
  local copies, waits for them, and re-layouts  9.75 us (5%)
  starting transfers between devices  6.85 us (4%)
  matrix products  5.23 us (3%)
  other arithmetic  4.62 us (2%)
    all_gather x1, waiting for transfers between devices, on_device(): lax.all_gather(jnp.concatenate([w_query, w_key, w_value], axis=1), ('req'...  102 us
    pallas_call x1, Pallas kernels, local_attention(): pl.pallas_call(kernel, grid_spec=grid_spec, out_shape=[jax.ShapeDtypeStru...  16.6 us
    all_to_all x1, waiting for transfers between devices, on_device(): lax.all_to_all(part_sum.reshape(req_local, heads_local, seq_count, span_l...  11.3 us
    all_gather x1, blocking collectives, on_device(): q_whole = lax.all_gather(q_local, 'seq', axis=1, tiled=True)  8.46 us
    psum x1, blocking collectives, on_device(): lax.psum((jnp.sum(q_proj * q_proj, axis=1), jnp.sum(k_proj * k_proj, axis...  6.03 us
    dot_general x1, matrix products, on_device(): proj = jnp.dot(token_rows, w_all, preferred_element_type=jnp.float32)  4.67 us
  transfers between devices with their start and end apart: 3, of which 3 were waited for; matrix products, arithmetic and copies ran while one was open for 1% of the time, Pallas kernels for 0%

profile of v1, /device:TPU:0, one launch (start us, length us, event | category | flops | bytes accessed | tf_op | source)
XLA Modules:
  0.0 186.5 jit_solution(1089393803007799035)
XLA Ops:
  6.5 0.0 copy-start
  6.5 0.0 all-gather.2.cloned.1.call-start
  6.6 2.1 %pad_maximum_fusion = bf16[256,1536]{1,0:T(8,128)(2,1)} fusion(bf16[256,512]{1,0:T(8,128)(2,1)} %param.17, bf16[256,512]{1,0:T(8,128)(2,1)} %param.16, bf16[256,512]{1,0:T(8,128)(2,1)} %param.15), kind=kLoop, calls=%fused_computation.5 | loop fusion | flops 2359296 | bytes 1572864 | tf_op jit(solution)/shard_map/concatenate | solution.py:148
  8.7 0.0 all-gather.2.cloned.1.call-update
  8.8 0.0 copy-done.10
  8.8 0.1 broadcast_compare_fusion.1
  8.9 0.1 add_subtract_fusion
  9.0 0.1 broadcast_compare_fusion
  9.0 0.5 multiply_cosine_fusion
  9.6 101.8 %all-gather.2.cloned.1.call-done = bf16[2048,1536]{1,0:T(8,128)(2,1)} async-done(((bf16[256,1536]{1,0:T(8,128)(2,1)}), bf16[2048,1536]{1,0:T(8,128)(2,1)}) %all-gather.2.cloned.1.call-update) | async-done | bytes 6291472 | tf_op jit(solution)/shard_map/all_gather | solution.py:147
  111.3 4.7 %convolution_bitcast_fusion = f32[256,1536]{0,1:T(8,128)S(1)} fusion(bf16[2048,1536]{1,0:T(8,128)(2,1)} %all-gather.2.cloned.1.call-done, bf16[256,2048]{1,0:T(8,128)(2,1)S(1)} %bitcast.42), kind=kOutput, calls=%fused_computation | convolution fusion | flops 1610612736 | bytes 8912896 | tf_op jit(solution)/shard_map/dot_general | solution.py:150
  116.0 0.0 copy-start.4
  116.0 0.0 copy-start.5
  116.0 0.1 multiply_reduce_fusion
  116.1 0.7 slice.52
  116.9 6.0 %all-reduce = (f32[256]{0:T(256)S(1)}, f32[256]{0:T(256)S(1)}) all-reduce(f32[256]{0:T(256)S(1)} %get-tuple-element.12, f32[256]{0:T(256)S(1)} %get-tuple-element.11), channel_id=1, replica_groups=mesh['req'=4,'seq'=2,'tp'=4] {'tp'}, use_global_device_ids=true, to_apply=%region_1.0 | all-reduce | flops 512 | bytes 4096 | tf_op jit(solution)/shard_map/psum | solution.py:154
  122.9 0.2 multiply_multiply_fusion
  123.2 0.2 copy.79
  123.4 0.2 copy.80
  123.6 0.1 subtract_convert_fusion
  123.7 0.1 pad_maximum_fusion.1
  123.9 0.2 copy.58
  124.1 0.8 convert_element_type.41.nk_ref
  124.9 0.2 copy.77
  125.1 0.2 copy.78
  125.4 0.1 multiply_subtract_fusion
  125.5 0.1 maximum_convert_fusion
  125.7 0.2 copy.55
  125.9 0.1 convert_element_type.40
  126.0 8.5 %all_gather.7.q_ref = bf16[2,256,512]{2,1,0:T(8,128)(2,1)} all-gather(bf16[2,128,512]{2,1,0:T(8,128)(2,1)S(1)} %convert_element_type.40), channel_id=1, replica_groups=mesh['req'=4,'seq'=2,'tp'=4] {'seq'}, dimensions={1}, use_global_device_ids=true | all-gather | bytes 786432 | tf_op jit(solution)/shard_map/all_gather | solution.py:166
  134.5 0.8 copy.59
  135.3 16.6 %shard_map.136 = (f32[2,4,256,128]{3,2,1,0:T(8,128)}, f32[2,4,256,1]{3,2,1,0:T(8,128)}, f32[2,4,256,1]{3,2,1,0:T(8,128)}) custom-call(s32[2]{0:T(128)} %len_ref.1, s32[2]{0:T(128)} %win_ref.1, s32[1]{0:T(128)} %bitcast.seq_ref, bf16[2,256,512]{2,1,0:T(8,128)(2,1)} %all_gather.7.q_ref, bf16[2,2048,512]{2,1,0:T(8,128)(2,1)} %ck_ref.1, ...), custom_call_target="tpu_custom_call" | custom-call | tf_op jit(solution)/shard_map/pallas_call | solution.py:103
  151.9 0.0 copy-start.3
  152.0 1.6 copy.64
  153.6 1.6 copy.65
  155.2 0.6 copy.67
  155.8 3.2 %all-to-all-start.1 = ((f32[2,4,2,128,2]{3,1,0,4,2:T(4,128)}), f32[2,4,2,128,2]{3,1,0,4,2:T(4,128)S(1)}, u32[]{:S(2)}, u32[]{:S(2)}) async-start(f32[2,4,2,128,2]{3,1,0,4,2:T(4,128)} %copy.67), calls=%async_computation.1 | async-start | bytes 32768 | tf_op jit(solution)/shard_map/all_to_all | solution.py:178
  159.1 0.0 copy-done.9
  159.1 0.3 select_reduce_fusion
  159.4 0.3 convolution_bitcast_fusion.1
  159.7 1.1 copy.60
  160.8 2.1 %all-to-all-done.1 = f32[2,4,2,128,2]{3,1,0,4,2:T(4,128)S(1)} async-done(((f32[2,4,2,128,2]{3,1,0,4,2:T(4,128)}), f32[2,4,2,128,2]{3,1,0,4,2:T(4,128)S(1)}, u32[]{:S(2)}, u32[]{:S(2)}) %all-to-all-start.1) | async-done | bytes 16416 | tf_op jit(solution)/shard_map/all_to_all | solution.py:178
  162.9 3.6 %all-to-all-start = ((f32[2,4,2,128,128]{4,3,1,0,2:T(8,128)}), f32[2,4,2,128,128]{4,3,1,0,2:T(8,128)S(1)}, u32[]{:S(2)}, u32[]{:S(2)}) async-start(f32[2,4,2,128,128]{4,3,1,0,2:T(8,128)} %copy.60), calls=%async_computation | async-start | bytes 2097152 | tf_op jit(solution)/shard_map/all_to_all | solution.py:171
  166.6 11.3 %all-to-all-done = f32[2,4,2,128,128]{4,3,1,0,2:T(8,128)S(1)} async-done(((f32[2,4,2,128,128]{4,3,1,0,2:T(8,128)}), f32[2,4,2,128,128]{4,3,1,0,2:T(8,128)S(1)}, u32[]{:S(2)}, u32[]{:S(2)}) %all-to-all-start) | async-done | bytes 1048608 | tf_op jit(solution)/shard_map/all_to_all | solution.py:171
  177.9 0.5 fusion
  178.4 0.2 fusion.2
  178.6 0.2 copy.72
  178.8 0.9 copy.73
  (31 shorter events, 0.3 us)
Async XLA Ops:
  6.5 104.8 %copy-start = (bf16[2,128,2048]{2,1,0:T(8,128)(2,1)S(1)}, bf16[2,128,2048]{2,1,0:T(8,128)(2,1)}, u32[]{:S(2)}) copy-start(bf16[2,128,2048]{2,1,0:T(8,128)(2,1)} %param.14) | copy-start | bytes 3145732
  6.5 2.3 %copy-start.10 = (s32[2]{0:T(128)S(1)}, s32[2]{0:T(128)}, u32[]{:S(2)}) copy-start(s32[2]{0:T(128)} %param.26) | copy-start | bytes 28
  6.5 2.3 %copy-start.7 = (s32[2]{0:T(128)S(1)}, s32[2]{0:T(128)}, u32[]{:S(2)}) copy-start(s32[2]{0:T(128)} %len_ref.1) | copy-start | bytes 28
  6.5 2.3 %copy-start.6 = (s32[2]{0:T(128)S(1)}, s32[2]{0:T(128)}, u32[]{:S(2)}) copy-start(s32[2]{0:T(128)} %win_ref.1) | copy-start | bytes 28
  6.5 2.4 %copy-start.8 = (s32[2,4]{1,0:T(2,128)S(1)}, s32[2,4]{1,0:T(2,128)}, u32[]{:S(2)}) copy-start(s32[2,4]{1,0:T(2,128)} %param.24) | copy-start | bytes 100
  6.5 104.8 %all-gather.2.cloned.1.call-start = ((), (), s32[]{:S(2)}) async-start(), calls=%async_computation.2 | async-start | bytes 7077888 | tf_op jit(solution)/shard_map/all_gather | solution.py:147
  116.0 6.9 %copy-start.4 = (f32[512]{0:T(512)S(1)}, f32[512]{0:T(512)}, u32[]{:S(2)}) copy-start(f32[512]{0:T(512)} %param.19) | copy-start | bytes 6148
  116.0 6.9 %copy-start.5 = (f32[512]{0:T(512)S(1)}, f32[512]{0:T(512)}, u32[]{:S(2)}) copy-start(f32[512]{0:T(512)} %param.18) | copy-start | bytes 6148
  125.5 9.0 %copy-start.2 = (bf16[256,512]{0,1:T(8,128)(2,1)S(1)}, bf16[256,512]{0,1:T(8,128)(2,1)}, u32[]{:S(2)}) copy-start(bf16[256,512]{0,1:T(8,128)(2,1)} %slice.52) | copy-start | bytes 786436
  151.9 7.1 %copy-start.9 = (bf16[2,4,512]{2,1,0:T(4,128)(2,1)S(1)}, bf16[2,4,512]{2,1,0:T(4,128)(2,1)}, u32[]{:S(2)}) copy-start(bf16[2,4,512]{2,1,0:T(4,128)(2,1)} %param.22) | copy-start | bytes 24580
  151.9 7.4 %copy-start.3 = (bf16[2,4,512]{2,1,0:T(4,128)(2,1)S(1)}, bf16[2,4,512]{2,1,0:T(4,128)(2,1)}, u32[]{:S(2)}) copy-start(bf16[2,4,512]{2,1,0:T(4,128)(2,1)} %param.23) | copy-start | bytes 24580
  151.9 7.7 %copy-start.1 = (f32[2,4,256,128]{3,2,1,0:T(8,128)S(1)}, f32[2,4,256,128]{3,2,1,0:T(8,128)}, u32[]{:S(2)}) copy-start(f32[2,4,256,128]{3,2,1,0:T(8,128)} %get-tuple-element.8) | copy-start | bytes 3145732
  155.8 7.1 %all-to-all-start.1 = ((f32[2,4,2,128,2]{3,1,0,4,2:T(4,128)}), f32[2,4,2,128,2]{3,1,0,4,2:T(4,128)S(1)}, u32[]{:S(2)}, u32[]{:S(2)}) async-start(f32[2,4,2,128,2]{3,1,0,4,2:T(4,128)} %copy.67), calls=%async_computation.1 | async-start | bytes 32768 | tf_op jit(solution)/shard_map/all_to_all | solution.py:178
  162.9 15.0 %all-to-all-start = ((f32[2,4,2,128,128]{4,3,1,0,2:T(8,128)}), f32[2,4,2,128,128]{4,3,1,0,2:T(8,128)S(1)}, u32[]{:S(2)}, u32[]{:S(2)}) async-start(f32[2,4,2,128,128]{4,3,1,0,2:T(8,128)} %copy.60), calls=%async_computation | async-start | bytes 2097152 | tf_op jit(solution)/shard_map/all_to_all | solution.py:171
Sparse Core Ops, SparseCore 0:
  9.6 101.7 all-gather.1

commit v2 on v1

v2 whole, which is shorter than its diff:
```python
import functools

import jax
import jax.numpy as jnp
from jax import lax
from jax.experimental import pallas as pl
from jax.experimental.pallas import tpu as pltpu
from jax.sharding import PartitionSpec as P

D = 2048
HEAD_DIM = 128
WINDOW = 4096
SINKS = 4


rope_base = 500000.0
epsilon = 1e-06
lowest = -1e30


def rotate_heads(vectors, positions):
    half_dim = vectors.shape[-1] // 2
    powers = jnp.arange(half_dim, dtype=jnp.float32) * (2.0 / vectors.shape[-1])
    inverse = rope_base ** (-powers)
    angles = positions.astype(jnp.float32)[:, None] * inverse[None, :]
    cosine = jnp.cos(angles)[:, None, :]
    sine_part = jnp.sin(angles)[:, None, :]
    leading = vectors[..., :half_dim]
    trailing = vectors[..., half_dim:]
    return jnp.concatenate(
        [leading * cosine - trailing * sine_part, trailing * cosine + leading * sine_part], axis=-1
    )


def normalize_rotate(projected, squares, feature_gain, positions, model_width, head_size):
    factor = lax.rsqrt(squares / model_width + epsilon)
    normed = projected * factor[:, None] * feature_gain[None, :]
    shaped = normed.reshape(projected.shape[0], projected.shape[1] // head_size, head_size)
    return rotate_heads(shaped, positions).reshape(projected.shape).astype(jnp.bfloat16)


def cache_kernel(len_ref, win_ref, seq_ref, q_ref, ck_ref, cv_ref, o_ref, m_ref, l_ref, *, scaling):
    r = pl.program_id(0)
    length_now = len_ref[r]
    window_now = win_ref[r]
    seq_index = seq_ref[0]
    seq_count, _, span_local, _ = q_ref.shape
    slots = ck_ref.shape[1]
    keys = ck_ref[0]
    values = cv_ref[0]
    dims = (((1,), (1,)), ((), ()))
    row = lax.broadcasted_iota(jnp.int32, (span_local, slots), 0)
    slot = lax.broadcasted_iota(jnp.int32, (span_local, slots), 1) + seq_index * slots
    slot_pos = length_now - 1 - ((length_now - 1 - slot) & (WINDOW - 1))
    for shift in range(seq_count):
        owner = (seq_index - shift + seq_count) % seq_count
        scores = (
            lax.dot_general(q_ref[shift, 0], keys, dims, preferred_element_type=jnp.float32)
            * scaling
        )
        edge = length_now + owner * span_local + row - window_now
        allowed = (slot_pos >= 0) & (slot_pos > edge)
        highest = jnp.max(jnp.where(allowed, scores, lowest), axis=1, keepdims=True)
        weights = jnp.where(allowed, jnp.exp(scores - highest), 0.0)
        o_ref[shift, 0, 0] = jnp.dot(
            weights.astype(jnp.bfloat16), values, preferred_element_type=jnp.float32
        )
        m_ref[shift, 0, 0] = highest
        l_ref[shift, 0, 0] = jnp.sum(weights, axis=1, keepdims=True)


def cache_attention(q_parts, cache_keys, cache_values, cache_len, window_len, seq_index):
    seq_count, req_local, span_local, local_cols = q_parts.shape
    heads_local = local_cols // HEAD_DIM
    slot_local = cache_keys.shape[1]
    kernel = functools.partial(cache_kernel, scaling=HEAD_DIM ** (-0.5))
    part = (seq_count, 1, 1, span_local)
    grid_spec = pltpu.PrefetchScalarGridSpec(
        num_scalar_prefetch=3,
        grid=(req_local, heads_local),
        in_specs=[
            pl.BlockSpec((seq_count, 1, span_local, HEAD_DIM), lambda r, h, *_: (0, r, 0, h)),
            pl.BlockSpec((1, slot_local, HEAD_DIM), lambda r, h, *_: (r, 0, h)),
            pl.BlockSpec((1, slot_local, HEAD_DIM), lambda r, h, *_: (r, 0, h)),
        ],
        out_specs=[
            pl.BlockSpec(part + (HEAD_DIM,), lambda r, h, *_: (0, r, h, 0, 0)),
            pl.BlockSpec(part + (1,), lambda r, h, *_: (0, r, h, 0, 0)),
            pl.BlockSpec(part + (1,), lambda r, h, *_: (0, r, h, 0, 0)),
        ],
    )
    shape = (seq_count, req_local, heads_local, span_local)
    return pl.pallas_call(
        kernel,
        grid_spec=grid_spec,
        out_shape=[
            jax.ShapeDtypeStruct(shape + (HEAD_DIM,), jnp.float32),
            jax.ShapeDtypeStruct(shape + (1,), jnp.float32),
            jax.ShapeDtypeStruct(shape + (1,), jnp.float32),
        ],
    )(
        cache_len,
        window_len,
        jnp.reshape(seq_index, (1,)).astype(jnp.int32),
        q_parts,
        cache_keys,
        cache_values,
    )


def span_kernel(
    len_ref,
    win_ref,
    seq_ref,
    live_ref,
    sink_pos_ref,
    q_ref,
    nk_ref,
    nv_ref,
    sk_ref,
    sv_ref,
    ps_ref,
    pst_ref,
    out_ref,
    *,
    scaling,
):
    r = pl.program_id(0)
    length_now = len_ref[r]
    window_now = win_ref[r]
    seq_index = seq_ref[0]
    live_count = live_ref[r]
    seq_count, _, span_local, _ = nk_ref.shape
    queries = q_ref[0]
    dims = (((1,), (1,)), ((), ()))
    row = lax.broadcasted_iota(jnp.int32, (span_local, span_local), 0) + seq_index * span_local
    col = lax.broadcasted_iota(jnp.int32, (span_local, span_local), 1)
    span_scores, span_ok = [], []
    for shift in range(seq_count):
        owner = (seq_index - shift + seq_count) % seq_count
        span_scores.append(
            lax.dot_general(queries, nk_ref[shift, 0], dims, preferred_element_type=jnp.float32)
            * scaling
        )
        span_ok.append(owner * span_local + col <= row)
    query_f = queries.astype(jnp.float32)
    row_1 = lax.broadcasted_iota(jnp.int32, (span_local, 1), 0) + seq_index * span_local
    edge = length_now + row_1 - window_now
    sink_scores, sink_ok = [], []
    for sink in range(SINKS):
        key_f = sk_ref[0, sink : sink + 1, :].astype(jnp.float32)
        sink_scores.append(jnp.sum(query_f * key_f, axis=1, keepdims=True) * scaling)
        sink_ok.append(sink_pos_ref[r * SINKS + sink] <= edge)
    part_high = pst_ref[:, 0, 0, :, 0:1]
    part_total = pst_ref[:, 0, 0, :, 1:2]
    peak = jnp.max(part_high, axis=0)
    for scores, ok in zip(span_scores + sink_scores, span_ok + sink_ok):
        peak = jnp.maximum(peak, jnp.max(jnp.where(ok, scores, lowest), axis=1, keepdims=True))
    factor = jnp.exp(part_high - peak[None])
    denominator = jnp.sum(part_total * factor, axis=0)
    numerator = jnp.sum(ps_ref[:, 0, 0] * factor, axis=0)
    for shift in range(seq_count):
        weights = jnp.where(span_ok[shift], jnp.exp(span_scores[shift] - peak), 0.0)
        denominator = denominator + jnp.sum(weights, axis=1, keepdims=True)
        numerator = numerator + jnp.dot(
            weights.astype(jnp.bfloat16), nv_ref[shift, 0], preferred_element_type=jnp.float32
        )
    for sink in range(SINKS):
        weights = jnp.where(sink_ok[sink], jnp.exp(sink_scores[sink] - peak), 0.0)
        denominator = denominator + weights
        value_f = sv_ref[0, sink : sink + 1, :].astype(jnp.float32)
        numerator = numerator + weights.astype(jnp.bfloat16).astype(jnp.float32) * value_f
    live = row_1 < live_count
    safe = jnp.where(live, denominator, 1.0)
    out_ref[0] = jnp.where(live, numerator / safe, 0.0).astype(out_ref.dtype)


def span_attention(
    q_local, kv_parts, sink_keys, sink_values, parts_sum, parts_stats, scalars
):
    req_local, span_local, local_cols = q_local.shape
    seq_count = kv_parts.shape[0]
    heads_local = local_cols // HEAD_DIM
    kernel = functools.partial(span_kernel, scaling=HEAD_DIM ** (-0.5))
    part = (seq_count, 1, 1, span_local)
    grid_spec = pltpu.PrefetchScalarGridSpec(
        num_scalar_prefetch=5,
        grid=(req_local, heads_local),
        in_specs=[
            pl.BlockSpec((1, span_local, HEAD_DIM), lambda r, h, *_: (r, 0, h)),
            pl.BlockSpec((seq_count, 1, span_local, HEAD_DIM), lambda r, h, *_: (0, r, 0, h)),
            pl.BlockSpec(
                (seq_count, 1, span_local, HEAD_DIM),
                lambda r, h, *_: (0, r, 0, h + heads_local),
            ),
            pl.BlockSpec((1, SINKS, HEAD_DIM), lambda r, h, *_: (r, 0, h)),
            pl.BlockSpec((1, SINKS, HEAD_DIM), lambda r, h, *_: (r, 0, h)),
            pl.BlockSpec(part + (HEAD_DIM,), lambda r, h, *_: (0, r, h, 0, 0)),
            pl.BlockSpec(part + (2,), lambda r, h, *_: (0, r, h, 0, 0)),
        ],
        out_specs=pl.BlockSpec((1, span_local, HEAD_DIM), lambda r, h, *_: (r, 0, h)),
    )
    return pl.pallas_call(
        kernel,
        grid_spec=grid_spec,
        out_shape=jax.ShapeDtypeStruct((req_local, span_local, local_cols), jnp.bfloat16),
    )(*scalars, q_local, kv_parts, kv_parts, sink_keys, sink_values, parts_sum, parts_stats)


def shifted(x, axis_name, shift):
    count = lax.axis_size(axis_name)
    if shift % count == 0:
        return x
    return lax.ppermute(x, axis_name, [(a, (a + shift) % count) for a in range(count)])


def tp_sum(x):
    count = lax.axis_size("tp")
    assert count & (count - 1) == 0
    bit = 1
    while bit < count:
        x = x + lax.ppermute(x, "tp", [(a, a ^ bit) for a in range(count)])
        bit *= 2
    return x


def on_device(
    tokens,
    w_query,
    w_key,
    w_value,
    q_gain,
    k_gain,
    cache_keys,
    cache_values,
    sink_keys,
    sink_values,
    sink_pos,
    cache_len,
    span_len,
    window_len,
):
    req_local, span_local, model_width = tokens.shape
    local_cols = w_query.shape[1]
    seq_count = lax.axis_size("seq")
    seq_index = lax.axis_index("seq")
    token_rows = tokens.reshape(req_local * span_local, model_width)
    offsets = seq_index * span_local + jnp.arange(span_local, dtype=jnp.int32)
    positions = (cache_len[:, None] + offsets[None, :]).reshape(-1)
    wq_all = lax.all_gather(w_query, ("req", "seq"), axis=0, tiled=True)
    wkv_all = lax.all_gather(
        jnp.concatenate([w_key, w_value], axis=1), ("req", "seq"), axis=0, tiled=True
    )
    q_proj = jnp.dot(token_rows, wq_all, preferred_element_type=jnp.float32)
    q_squares = tp_sum(jnp.sum(q_proj * q_proj, axis=1))
    q_local = normalize_rotate(q_proj, q_squares, q_gain, positions, D, HEAD_DIM).reshape(
        req_local, span_local, local_cols
    )
    q_parts = jnp.stack([shifted(q_local, "seq", shift) for shift in range(seq_count)])
    c_sum, c_high, c_total = cache_attention(
        q_parts, cache_keys, cache_values, cache_len, window_len, seq_index
    )
    wkv_all, c_sum, c_high, c_total = lax.optimization_barrier((wkv_all, c_sum, c_high, c_total))
    c_stats = jnp.concatenate([c_high, c_total], axis=-1)
    parts_sum = jnp.stack([shifted(c_sum[s], "seq", -s) for s in range(seq_count)])
    parts_stats = jnp.stack([shifted(c_stats[s], "seq", -s) for s in range(seq_count)])
    kv_proj = jnp.dot(token_rows, wkv_all, preferred_element_type=jnp.float32)
    k_proj = kv_proj[:, :local_cols]
    k_squares = tp_sum(jnp.sum(k_proj * k_proj, axis=1))
    k_rot = normalize_rotate(k_proj, k_squares, k_gain, positions, D, HEAD_DIM)
    v_new = kv_proj[:, local_cols:].astype(jnp.bfloat16)
    kv_new = jnp.concatenate([k_rot, v_new], axis=1).reshape(req_local, span_local, 2 * local_cols)
    kv_parts = jnp.stack([shifted(kv_new, "seq", shift) for shift in range(seq_count)])
    scalars = (
        cache_len,
        window_len,
        jnp.reshape(seq_index, (1,)).astype(jnp.int32),
        span_len,
        sink_pos.reshape(-1),
    )
    return span_attention(
        q_local, kv_parts, sink_keys, sink_values, parts_sum, parts_stats, scalars
    )


def solution(mesh):
    placed = (
        P("req", "seq", None),
        P(("req", "seq"), "tp"),
        P(("req", "seq"), "tp"),
        P(("req", "seq"), "tp"),
        P("tp"),
        P("tp"),
        P("req", "seq", "tp"),
        P("req", "seq", "tp"),
        P("req", None, "tp"),
        P("req", None, "tp"),
        P("req", None),
        P("req"),
        P("req"),
        P("req"),
    )
    return jax.shard_map(
        on_device, mesh=mesh, in_specs=placed, out_specs=P("req", "seq", "tp"), check_vma=False
    )
```

time: 187 us -> 191 us (1.021)
  blocking collectives: 14.5 us -> 0 us
  Pallas kernels: 16.6 us -> 25.7 us
  waiting for transfers between devices: 115 us -> 122 us
  other arithmetic: 4.62 us -> 9.14 us
  local copies, waits for them, and re-layouts: 9.75 us -> 7.3 us
    ppermute x0 -> x8, waiting for transfers between devices: none -> 33.1 us  [the longest x4 28.8 us: shifted(): lax.ppermute(x, axis_name, [(a, (a + shift) % count) for a in range(count)])]
    all_to_all x2 -> x0, waiting for transfers between devices: 13.4 us -> none  [the longest x1 11.3 us: on_device(): lax.all_to_all(part_sum.reshape(req_local, heads_local, seq_count, span_l...]
    all_gather x1 -> x2, waiting for transfers between devices: 102 us -> 88.6 us  [the longest x1 51.6 us: on_device(): wq_all = lax.all_gather(w_query, ('req', 'seq'), axis=0, tiled=True)]
    pallas_call x1 -> x2, Pallas kernels: 16.6 us -> 25.7 us  [the longest x1 16.4 us: cache_attention(): pl.pallas_call(kernel, grid_spec=grid_spec, out_shape=[jax.ShapeDtypeStru...]
    all_gather x1 -> x0, blocking collectives: 8.46 us -> none  [on_device(): q_whole = lax.all_gather(q_local, 'seq', axis=1, tiled=True)]
    all_to_all x2 -> x0, starting transfers between devices: 6.82 us -> none  [the longest x1 3.58 us: on_device(): lax.all_to_all(part_sum.reshape(req_local, heads_local, seq_count, span_l...]
    ppermute x0 -> x8, starting transfers between devices: none -> 6.5 us  [the longest x4 3.41 us: shifted(): lax.ppermute(x, axis_name, [(a, (a + shift) % count) for a in range(count)])]
    psum x1 -> x0, blocking collectives: 6.03 us -> none  [on_device(): lax.psum((jnp.sum(q_proj * q_proj, axis=1), jnp.sum(k_proj * k_proj, axis...]
  transfers between devices with their start and end apart: 3 -> 10, of which waited for: 3 -> 8; matrix products, arithmetic and copies ran while one was open for 1% -> 9% of each run, Pallas kernels for 0% -> 9%
where the time goes in v2:
time: 191 us
  waiting for transfers between devices  122 us (64%)
  Pallas kernels  25.7 us (13%)
  between operations  13.6 us (7%)
  other arithmetic  9.14 us (5%)
  local copies, waits for them, and re-layouts  7.3 us (4%)
  starting transfers between devices  6.55 us (3%)
  matrix products  5.96 us (3%)
    all_gather x1, waiting for transfers between devices, on_device(): wq_all = lax.all_gather(w_query, ('req', 'seq'), axis=0, tiled=True)  51.6 us
    all_gather x1, waiting for transfers between devices, on_device(): lax.all_gather(jnp.concatenate([w_key, w_value], axis=1), ('req', 'seq'),...  37 us
    ppermute x4, waiting for transfers between devices, shifted(): lax.ppermute(x, axis_name, [(a, (a + shift) % count) for a in range(count)])  28.8 us
    pallas_call x1, Pallas kernels, cache_attention(): pl.pallas_call(kernel, grid_spec=grid_spec, out_shape=[jax.ShapeDtypeStru...  16.4 us
    pallas_call x1, Pallas kernels, span_attention(): pl.pallas_call(kernel, grid_spec=grid_spec, out_shape=jax.ShapeDtypeStruc...  9.28 us
    ppermute x4, waiting for transfers between devices, tp_sum(): x = x + lax.ppermute(x, 'tp', [(a, a ^ bit) for a in range(count)])  4.34 us
  transfers between devices with their start and end apart: 10, of which 8 were waited for; matrix products, arithmetic and copies ran while one was open for 9% of the time, Pallas kernels for 9%

profile of v2, /device:TPU:0, one launch (start us, length us, event | category | flops | bytes accessed | tf_op | source)
XLA Modules:
  0.0 190.7 jit_solution(14840624263677204597)
XLA Ops:
  6.5 0.7 all-gather.3.cloned.1.call-update
  7.3 0.0 all-gather.5.cloned.1.call-start
  7.3 1.9 pad_maximum_fusion.2
  9.2 0.0 all-gather.5.cloned.1.call-update
  9.2 0.7 convert_bitcast_fusion
  10.0 51.6 %all-gather.3.cloned.1.call-done = bf16[2048,512]{1,0:T(8,128)(2,1)} async-done(((bf16[256,512]{1,0:T(8,128)(2,1)}), bf16[2048,512]{1,0:T(8,128)(2,1)}) %all-gather.3.cloned.1.call-update) | async-done | bytes 2097168 | tf_op jit(solution)/shard_map/all_gather | solution.py:250
  61.5 2.4 %multiply_reduce_fusion.1 = (f32[256]{0:T(256)S(1)}, f32[256,512]{1,0:T(8,128)S(1)}) fusion(bf16[256,2048]{1,0:T(8,128)(2,1)S(1)} %bitcast.22, bf16[2048,512]{1,0:T(8,128)(2,1)} %all-gather.3.cloned.1.call-done), kind=kOutput, calls=%fused_computation.16 | convolution fusion | flops 537132800 | bytes 3671040 | tf_op jit(solution)/shard_map/dot_general | solution.py:254
  63.9 0.1 collective-permute-start
  64.0 1.1 collective-permute-done
  65.1 1.5 collective-permute-start.1
  66.6 0.5 multiply_cosine_fusion
  67.1 1.6 collective-permute-done.1
  68.7 0.1 multiply_multiply_fusion.1
  68.8 0.2 reshape.116
  69.0 0.5 multiply_subtract_fusion
  69.5 0.4 maximum_convert_fusion
  69.9 0.1 convert_element_type.36.q_ref
  70.0 0.6 collective-permute-start.2
  70.6 0.1 convert_element_type.37
  70.7 12.2 %collective-permute-done.2 = bf16[2,128,512]{2,1,0:T(8,128)(2,1)S(1)} collective-permute-done((bf16[2,128,512]{2,1,0:T(8,128)(2,1)S(1)}, bf16[2,128,512]{2,1,0:T(8,128)(2,1)S(1)}, u32[]{:S(2)}, u32[]{:S(2)}) %collective-permute-start.2) | collective-permute-done | bytes 262176 | tf_op jit(solution)/shard_map/ppermute | solution.py:214
  82.9 0.9 pad_maximum_fusion.3.q_ref
  83.8 16.4 %shard_map.136 = (f32[2,2,4,128,128]{4,3,2,1,0:T(8,128)}, f32[2,2,4,128,1]{4,3,2,1,0:T(8,128)}, f32[2,2,4,128,1]{4,3,2,1,0:T(8,128)}) custom-call(s32[2]{0:T(128)} %len_ref.3, s32[2]{0:T(128)} %win_ref.3, s32[1]{0:T(128)} %bitcast.seq_ref, bf16[2,2,128,512]{3,2,1,0:T(8,128)(2,1)} %pad_maximum_fusion.3.q_ref, bf16[2,2048,512]{2,1,0:T(8,128)(2,1)} %ck_ref.1, ...), custom_call_target="tpu_custom_call" | custom-call | tf_op jit(solution)/shard_map/pallas_call | solution.py:93
  100.3 37.0 %all-gather.5.cloned.1.call-done = bf16[2048,1024]{1,0:T(8,128)(2,1)} async-done(((bf16[256,1024]{1,0:T(8,128)(2,1)}), bf16[2048,1024]{1,0:T(8,128)(2,1)}) %all-gather.5.cloned.1.call-update) | async-done | bytes 4194320 | tf_op jit(solution)/shard_map/all_gather | solution.py:251
  137.3 3.6 %convolution_bitcast_fusion = f32[256,1024]{0,1:T(8,128)S(1)} fusion(bf16[2048,1024]{1,0:T(8,128)(2,1)} %all-gather.5.cloned.1.call-done, bf16[256,2048]{1,0:T(8,128)(2,1)S(1)} %bitcast.23), kind=kOutput, calls=%fused_computation | convolution fusion | flops 1073741824 | bytes 6291456 | tf_op jit(solution)/shard_map/dot_general | solution.py:267
  140.9 0.1 multiply_reduce_fusion
  140.9 0.1 collective-permute-start.3
  141.0 1.1 collective-permute-done.3
  142.1 1.5 collective-permute-start.4
  143.6 0.9 fusion.2
  144.5 0.6 collective-permute-start.6
  145.2 0.5 collective-permute-done.4
  145.7 0.1 multiply_multiply_fusion
  145.9 0.2 copy.28
  146.2 0.2 copy.29
  146.4 0.3 subtract_convert_fusion
  146.7 0.4 pad_maximum_fusion.5
  147.1 0.2 copy.22
  147.3 0.2 copy.23
  147.5 1.0 collective-permute-start.5
  148.5 1.6 copy.25
  150.0 1.6 copy.26
  151.6 1.2 collective-permute-start.7
  152.8 0.6 reshape.114.sink_pos_ref
  153.4 16.6 %collective-permute-done.7 = f32[2,4,128,2]{2,1,3,0:T(4,128)S(1)} collective-permute-done((f32[2,4,128,2]{2,1,3,0:T(4,128)S(1)}, f32[2,4,128,2]{2,1,3,0:T(4,128)S(1)}, u32[]{:S(2)}, u32[]{:S(2)}) %collective-permute-start.7) | collective-permute-done | bytes 8224 | tf_op jit(solution)/shard_map/ppermute | solution.py:214
  170.0 1.4 copy.27.pst_ref
  171.4 2.1 %pad_maximum_fusion.1.ps_ref = f32[2,2,4,128,128]{4,3,2,1,0:T(8,128)} fusion(f32[1,2,4,128,128]{4,3,2,1,0:T(8,128)} %bitcast.11, f32[1,2,4,128,128]{4,3,2,1,0:T(8,128)S(1)} %get-tuple-element.21), kind=kLoop, calls=%fused_computation.2 | loop fusion | flops 262144 | bytes 2097152 | tf_op jit(solution)/shard_map/stack | solution.py:265
  173.5 1.1 pad_maximum_fusion.nk_ref.nv_ref
  174.5 9.3 %shard_map.137 = bf16[2,128,512]{2,1,0:T(8,128)(2,1)} custom-call(s32[2]{0:T(128)} %len_ref.3, s32[2]{0:T(128)} %win_ref.3, s32[1]{0:T(128)} %bitcast.seq_ref, s32[2]{0:T(128)} %live_ref.1, s32[8]{0:T(128)} %reshape.114.sink_pos_ref, bf16[2,128,512]{2,1,0:T(8,128)(2,1)} %copy-done.1, bf16[2,2,128,1024]{3,2,1,0:T(8,128)(2,1)} %pad_maximum_fusion.nk_ref.nv_ref, ...), custom_call_target="tpu_custom_call" | custom-call | tf_op jit(solution)/shard_map/pallas_call | solution.py:203
  (26 shorter events, 0.2 us)
Async XLA Ops:
  6.5 55.0 %copy-start = (bf16[2,128,2048]{2,1,0:T(8,128)(2,1)S(1)}, bf16[2,128,2048]{2,1,0:T(8,128)(2,1)}, u32[]{:S(2)}) copy-start(bf16[2,128,2048]{2,1,0:T(8,128)(2,1)} %param.14) | copy-start | bytes 3145732
  6.5 62.1 %copy-start.3 = (f32[512]{0:T(512)S(1)}, f32[512]{0:T(512)}, u32[]{:S(2)}) copy-start(f32[512]{0:T(512)} %param.18) | copy-start | bytes 6148
  6.5 55.0 %all-gather.3.cloned.1.call-start = ((), (), s32[]{:S(2)}) async-start(), calls=%async_computation | async-start | bytes 2359296 | tf_op jit(solution)/shard_map/all_gather | solution.py:250
  7.3 130.0 %all-gather.5.cloned.1.call-start = ((), (), s32[]{:S(2)}) async-start(), calls=%async_computation.1 | async-start | bytes 4718592 | tf_op jit(solution)/shard_map/all_gather | solution.py:251
  63.9 1.2 collective-permute-start
  65.1 3.6 %collective-permute-start.1 = (f32[256]{0:T(256)S(1)}, f32[256]{0:T(256)S(1)}, u32[]{:S(2)}, u32[]{:S(2)}) collective-permute-start(f32[256]{0:T(256)S(1)} %add.53), channel_id=1, source_target_pairs={{0,2},{1,3},{2,0},{3,1},{4,6},{5,7},{6,4},{7,5},{8,10},{9,11},{10,... | collective-permute-start | bytes 3080 | tf_op jit(solution)/shard_map/ppermute | solution.py:222
  70.0 30.3 %copy-start.1 = (bf16[2,128,512]{2,1,0:T(8,128)(2,1)}, bf16[2,128,512]{2,1,0:T(8,128)(2,1)S(1)}, u32[]{:S(2)}) copy-start(bf16[2,128,512]{2,1,0:T(8,128)(2,1)S(1)} %convert_element_type.36.q_ref) | copy-start | bytes 786436
  70.0 12.9 %collective-permute-start.2 = (bf16[2,128,512]{2,1,0:T(8,128)(2,1)S(1)}, bf16[2,128,512]{2,1,0:T(8,128)(2,1)S(1)}, u32[]{:S(2)}, u32[]{:S(2)}) collective-permute-start(bf16[2,128,512]{2,1,0:T(8,128)(2,1)S(1)} %convert_element_type.36.q_ref), channel_id=1, source_target_pairs={{0,4},{4,0},{1,5},{5,1},{2,6},{6,2},{3,7},{7,3},{8,12},{12,8},{9,1... | collective-permute-start | bytes 786440 | tf_op jit(solution)/shard_map/ppermute | solution.py:214
  137.3 6.4 %copy-start.2 = (f32[2,2,4,128,128]{4,3,2,1,0:T(8,128)S(1)}, f32[2,2,4,128,128]{4,3,2,1,0:T(8,128)}, u32[]{:S(2)}) copy-start(f32[2,2,4,128,128]{4,3,2,1,0:T(8,128)} %get-tuple-element.16) | copy-start | bytes 3145732
  137.3 8.5 %copy-start.4 = (f32[512]{0:T(512)S(1)}, f32[512]{0:T(512)}, u32[]{:S(2)}) copy-start(f32[512]{0:T(512)} %param.19) | copy-start | bytes 6148
  140.9 1.2 collective-permute-start.3
  142.1 3.6 %collective-permute-start.4 = (f32[256]{0:T(256)S(1)}, f32[256]{0:T(256)S(1)}, u32[]{:S(2)}, u32[]{:S(2)}) collective-permute-start(f32[256]{0:T(256)S(1)} %add.62), channel_id=1, source_target_pairs={{0,2},{1,3},{2,0},{3,1},{4,6},{5,7},{6,4},{7,5},{8,10},{9,11},{10,... | collective-permute-start | bytes 3080 | tf_op jit(solution)/shard_map/ppermute | solution.py:222
  144.5 26.8 %collective-permute-start.6 = (f32[2,4,128,128]{3,2,1,0:T(8,128)}, f32[2,4,128,128]{3,2,1,0:T(8,128)}, u32[]{:S(2)}, u32[]{:S(2)}) collective-permute-start(f32[2,4,128,128]{3,2,1,0:T(8,128)} %get-tuple-element.22), channel_id=1, source_target_pairs={{0,4},{4,0},{1,5},{5,1},{2,6},{6,2},{3,7},{7,3},{8,12},{12,8},{9,1... | collective-permute-start | bytes 1572872 | tf_op jit(solution)/shard_map/ppermute | solution.py:214
  146.1 6.6 %copy-start.5 = (s32[2,4]{1,0:T(2,128)S(1)}, s32[2,4]{1,0:T(2,128)}, u32[]{:S(2)}) copy-start(s32[2,4]{1,0:T(2,128)} %param.24) | copy-start | bytes 100
  147.5 26.0 %collective-permute-start.5 = (bf16[2,128,1024]{2,1,0:T(8,128)(2,1)S(1)}, bf16[2,128,1024]{2,1,0:T(8,128)(2,1)S(1)}, u32[]{:S(2)}, u32[]{:S(2)}) collective-permute-start(bf16[2,128,1024]{2,1,0:T(8,128)(2,1)S(1)} %bitcast.25), channel_id=1, source_target_pairs={{0,4},{4,0},{1,5},{5,1},{2,6},{6,2},{3,7},{7,3},{8,12},{12,8},{9,1... | collective-permute-start | bytes 1572872 | tf_op jit(solution)/shard_map/ppermute | solution.py:214
  151.6 18.4 %collective-permute-start.7 = (f32[2,4,128,2]{2,1,3,0:T(4,128)S(1)}, f32[2,4,128,2]{2,1,3,0:T(4,128)S(1)}, u32[]{:S(2)}, u32[]{:S(2)}) collective-permute-start(f32[2,4,128,2]{2,1,3,0:T(4,128)S(1)} %get-tuple-element.28), channel_id=1, source_target_pairs={{0,4},{4,0},{1,5},{5,1},{2,6},{6,2},{3,7},{7,3},{8,12},{12,8},{9,1... | collective-permute-start | bytes 24584 | tf_op jit(solution)/shard_map/ppermute | solution.py:214
Sparse Core Ops, SparseCore 0:
  9.5 51.9 all-gather.2
  63.6 73.5 all-gather.4

commit v3 on v2

--- a/solution.py
+++ b/solution.py
@@ -260,10 +260,10 @@
     c_sum, c_high, c_total = cache_attention(
         q_parts, cache_keys, cache_values, cache_len, window_len, seq_index
     )
-    wkv_all, c_sum, c_high, c_total = lax.optimization_barrier((wkv_all, c_sum, c_high, c_total))
     c_stats = jnp.concatenate([c_high, c_total], axis=-1)
     parts_sum = jnp.stack([shifted(c_sum[s], "seq", -s) for s in range(seq_count)])
     parts_stats = jnp.stack([shifted(c_stats[s], "seq", -s) for s in range(seq_count)])
+    wkv_all, parts_sum, parts_stats = lax.optimization_barrier((wkv_all, parts_sum, parts_stats))
     kv_proj = jnp.dot(token_rows, wkv_all, preferred_element_type=jnp.float32)
     k_proj = kv_proj[:, :local_cols]
     k_squares = tp_sum(jnp.sum(k_proj * k_proj, axis=1))

time: 191 us -> 188 us (0.984)
  waiting for transfers between devices: 122 us -> 120 us
    all_gather x1, waiting for transfers between devices: 37 us -> 20.4 us  [on_device(): lax.all_gather(jnp.concatenate([w_key, w_value], axis=1), ('req', 'seq'),...]
    ppermute x4, waiting for transfers between devices: 28.8 us -> 42 us  [shifted(): lax.ppermute(x, axis_name, [(a, (a + shift) % count) for a in range(count)])]
    pallas_call x0 -> x2, local copies, waits for them, and re-layouts: none -> 3.12 us  [cache_attention(): pl.pallas_call(kernel, grid_spec=grid_spec, out_shape=[jax.ShapeDtypeStru...]
  transfers between devices with their start and end apart: 10 -> 10, of which waited for: 8 -> 9; matrix products, arithmetic and copies ran while one was open for 9% -> 8% of each run, Pallas kernels for 9% -> 9%
where the time goes in v3:
time: 188 us
  waiting for transfers between devices  120 us (64%)
  Pallas kernels  25.7 us (14%)
  between operations  13.6 us (7%)
  other arithmetic  8.08 us (4%)
  local copies, waits for them, and re-layouts  7.72 us (4%)
  starting transfers between devices  6.52 us (3%)
  matrix products  5.87 us (3%)
    all_gather x1, waiting for transfers between devices, on_device(): wq_all = lax.all_gather(w_query, ('req', 'seq'), axis=0, tiled=True)  51.5 us
    ppermute x4, waiting for transfers between devices, shifted(): lax.ppermute(x, axis_name, [(a, (a + shift) % count) for a in range(count)])  42 us
    all_gather x1, waiting for transfers between devices, on_device(): lax.all_gather(jnp.concatenate([w_key, w_value], axis=1), ('req', 'seq'),...  20.4 us
    pallas_call x1, Pallas kernels, cache_attention(): pl.pallas_call(kernel, grid_spec=grid_spec, out_shape=[jax.ShapeDtypeStru...  16.4 us
    pallas_call x1, Pallas kernels, span_attention(): pl.pallas_call(kernel, grid_spec=grid_spec, out_shape=jax.ShapeDtypeStruc...  9.28 us
    ppermute x4, waiting for transfers between devices, tp_sum(): x = x + lax.ppermute(x, 'tp', [(a, a ^ bit) for a in range(count)])  5.86 us
  transfers between devices with their start and end apart: 10, of which 9 were waited for; matrix products, arithmetic and copies ran while one was open for 8% of the time, Pallas kernels for 9%

profile of v3, /device:TPU:0, one launch (start us, length us, event | category | flops | bytes accessed | tf_op | source)
XLA Modules:
  0.0 187.9 jit_solution(887752689632083268)
XLA Ops:
  6.5 0.7 all-gather.3.cloned.1.call-update
  7.3 0.0 all-gather.5.cloned.1.call-start
  7.3 1.9 %pad_maximum_fusion.2 = bf16[256,1024]{1,0:T(8,128)(2,1)} fusion(bf16[256,512]{1,0:T(8,128)(2,1)} %param.17, bf16[256,512]{1,0:T(8,128)(2,1)} %param.16), kind=kLoop, calls=%fused_computation.5 | loop fusion | flops 1048576 | bytes 1048576 | tf_op jit(solution)/shard_map/concatenate | solution.py:252
  9.2 0.7 convert_bitcast_fusion
  10.0 51.5 %all-gather.3.cloned.1.call-done = bf16[2048,512]{1,0:T(8,128)(2,1)} async-done(((bf16[256,512]{1,0:T(8,128)(2,1)}), bf16[2048,512]{1,0:T(8,128)(2,1)}) %all-gather.3.cloned.1.call-update) | async-done | bytes 2097168 | tf_op jit(solution)/shard_map/all_gather | solution.py:250
  61.5 2.4 %multiply_reduce_fusion.1 = (f32[256]{0:T(256)S(1)}, f32[256,512]{1,0:T(8,128)S(1)}) fusion(bf16[256,2048]{1,0:T(8,128)(2,1)S(1)} %bitcast.22, bf16[2048,512]{1,0:T(8,128)(2,1)} %all-gather.3.cloned.1.call-done), kind=kOutput, calls=%fused_computation.16 | convolution fusion | flops 537132800 | bytes 3671040 | tf_op jit(solution)/shard_map/dot_general | solution.py:254
  63.9 0.1 collective-permute-start
  64.0 1.1 collective-permute-done
  65.1 1.5 collective-permute-start.1
  66.6 0.5 multiply_cosine_fusion
  67.1 1.6 collective-permute-done.1
  68.7 0.1 multiply_multiply_fusion.1
  68.8 0.2 reshape.116
  69.0 0.5 multiply_subtract_fusion
  69.5 0.4 maximum_convert_fusion
  69.8 0.1 convert_element_type.36.q_ref
  70.0 0.6 collective-permute-start.2
  70.6 0.1 convert_element_type.37
  70.7 12.2 %collective-permute-done.2 = bf16[2,128,512]{2,1,0:T(8,128)(2,1)S(1)} collective-permute-done((bf16[2,128,512]{2,1,0:T(8,128)(2,1)S(1)}, bf16[2,128,512]{2,1,0:T(8,128)(2,1)S(1)}, u32[]{:S(2)}, u32[]{:S(2)}) %collective-permute-start.2) | collective-permute-done | bytes 262176 | tf_op jit(solution)/shard_map/ppermute | solution.py:214
  82.9 0.9 pad_maximum_fusion.3.q_ref
  83.8 16.4 %shard_map.136 = (f32[2,2,4,128,128]{4,3,2,1,0:T(8,128)}, f32[2,2,4,128,1]{4,3,2,1,0:T(8,128)}, f32[2,2,4,128,1]{4,3,2,1,0:T(8,128)}) custom-call(s32[2]{0:T(128)} %len_ref.3, s32[2]{0:T(128)} %win_ref.3, s32[1]{0:T(128)} %bitcast.seq_ref, bf16[2,2,128,512]{3,2,1,0:T(8,128)(2,1)} %pad_maximum_fusion.3.q_ref, bf16[2,2048,512]{2,1,0:T(8,128)(2,1)} %ck_ref.1, ...), custom_call_target="tpu_custom_call" | custom-call | tf_op jit(solution)/shard_map/pallas_call | solution.py:93
  100.2 1.3 fusion.2
  101.5 0.6 collective-permute-start.3
  102.1 1.6 copy.20
  103.7 1.6 copy.21
  105.2 1.5 collective-permute-start.4
  106.8 19.4 %collective-permute-done.4 = f32[2,4,128,2]{2,1,3,0:T(4,128)S(1)} collective-permute-done((f32[2,4,128,2]{2,1,3,0:T(4,128)S(1)}, f32[2,4,128,2]{2,1,3,0:T(4,128)S(1)}, u32[]{:S(2)}, u32[]{:S(2)}) %collective-permute-start.4) | collective-permute-done | bytes 8224 | tf_op jit(solution)/shard_map/ppermute | solution.py:214
  126.2 1.1 pad_maximum_fusion.ps_ref
  127.3 20.4 %all-gather.5.cloned.1.call-done = bf16[2048,1024]{1,0:T(8,128)(2,1)} async-done(((bf16[256,1024]{1,0:T(8,128)(2,1)}), bf16[2048,1024]{1,0:T(8,128)(2,1)}) %all-gather.5.cloned.1.call-update) | async-done | bytes 4194320 | tf_op jit(solution)/shard_map/all_gather | solution.py:251
  147.7 3.5 %convolution_bitcast_fusion = f32[256,1024]{0,1:T(8,128)S(1)} fusion(bf16[2048,1024]{1,0:T(8,128)(2,1)} %all-gather.5.cloned.1.call-done, bf16[256,2048]{1,0:T(8,128)(2,1)S(1)} %bitcast.23), kind=kOutput, calls=%fused_computation | convolution fusion | flops 1073741824 | bytes 6291456 | tf_op jit(solution)/shard_map/dot_general | solution.py:267
  151.2 0.1 multiply_reduce_fusion
  151.3 0.1 collective-permute-start.5
  151.3 1.1 collective-permute-done.5
  152.5 1.5 collective-permute-start.6
  154.0 2.1 %collective-permute-done.6 = f32[256]{0:T(256)S(1)} collective-permute-done((f32[256]{0:T(256)S(1)}, f32[256]{0:T(256)S(1)}, u32[]{:S(2)}, u32[]{:S(2)}) %collective-permute-start.6) | collective-permute-done | bytes 1056 | tf_op jit(solution)/shard_map/ppermute | solution.py:222
  156.1 0.1 multiply_multiply_fusion
  156.3 0.2 copy.28
  156.5 0.2 copy.29
  156.7 0.3 subtract_convert_fusion
  157.0 0.4 pad_maximum_fusion.5
  157.4 0.2 copy.24
  157.6 0.2 copy.25
  157.8 0.6 collective-permute-start.7
  158.4 0.7 reshape.114.sink_pos_ref
  159.1 1.4 copy.27.pst_ref
  160.4 10.3 %collective-permute-done.7 = bf16[2,128,1024]{2,1,0:T(8,128)(2,1)S(1)} collective-permute-done((bf16[2,128,1024]{2,1,0:T(8,128)(2,1)S(1)}, bf16[2,128,1024]{2,1,0:T(8,128)(2,1)S(1)}, u32[]{:S(2)}, u32[]{:S(2)}) %collective-permute-start.7) | collective-permute-done | bytes 524320 | tf_op jit(solution)/shard_map/ppermute | solution.py:214
  170.8 1.1 pad_maximum_fusion.1.nk_ref.nv_ref
  171.8 9.3 %shard_map.137 = bf16[2,128,512]{2,1,0:T(8,128)(2,1)} custom-call(s32[2]{0:T(128)} %len_ref.3, s32[2]{0:T(128)} %win_ref.3, s32[1]{0:T(128)} %bitcast.seq_ref, s32[2]{0:T(128)} %live_ref.1, s32[8]{0:T(128)} %reshape.114.sink_pos_ref, bf16[2,128,512]{2,1,0:T(8,128)(2,1)} %copy-done.1, bf16[2,2,128,1024]{3,2,1,0:T(8,128)(2,1)} %pad_maximum_fusion.1.nk_ref.nv_ref, ...), custom_call_target="tpu_custom_call" | custom-call | tf_op jit(solution)/shard_map/pallas_call | solution.py:203
  (24 shorter events, 0.2 us)
Async XLA Ops:
  6.5 55.0 %copy-start = (bf16[2,128,2048]{2,1,0:T(8,128)(2,1)S(1)}, bf16[2,128,2048]{2,1,0:T(8,128)(2,1)}, u32[]{:S(2)}) copy-start(bf16[2,128,2048]{2,1,0:T(8,128)(2,1)} %param.14) | copy-start | bytes 3145732
  6.5 62.1 %copy-start.2 = (f32[512]{0:T(512)S(1)}, f32[512]{0:T(512)}, u32[]{:S(2)}) copy-start(f32[512]{0:T(512)} %param.18) | copy-start | bytes 6148
  6.5 55.0 %all-gather.3.cloned.1.call-start = ((), (), s32[]{:S(2)}) async-start(), calls=%async_computation | async-start | bytes 2359296 | tf_op jit(solution)/shard_map/all_gather | solution.py:250
  7.3 140.4 %all-gather.5.cloned.1.call-start = ((), (), s32[]{:S(2)}) async-start(), calls=%async_computation.1 | async-start | bytes 4718592 | tf_op jit(solution)/shard_map/all_gather | solution.py:251
  63.9 1.2 collective-permute-start
  65.1 3.6 %collective-permute-start.1 = (f32[256]{0:T(256)S(1)}, f32[256]{0:T(256)S(1)}, u32[]{:S(2)}, u32[]{:S(2)}) collective-permute-start(f32[256]{0:T(256)S(1)} %add.53), channel_id=1, source_target_pairs={{0,2},{1,3},{2,0},{3,1},{4,6},{5,7},{6,4},{7,5},{8,10},{9,11},{10,... | collective-permute-start | bytes 3080 | tf_op jit(solution)/shard_map/ppermute | solution.py:222
  69.9 30.2 %copy-start.1 = (bf16[2,128,512]{2,1,0:T(8,128)(2,1)}, bf16[2,128,512]{2,1,0:T(8,128)(2,1)S(1)}, u32[]{:S(2)}) copy-start(bf16[2,128,512]{2,1,0:T(8,128)(2,1)S(1)} %convert_element_type.36.q_ref) | copy-start | bytes 786436
  70.0 12.9 %collective-permute-start.2 = (bf16[2,128,512]{2,1,0:T(8,128)(2,1)S(1)}, bf16[2,128,512]{2,1,0:T(8,128)(2,1)S(1)}, u32[]{:S(2)}, u32[]{:S(2)}) collective-permute-start(bf16[2,128,512]{2,1,0:T(8,128)(2,1)S(1)} %convert_element_type.36.q_ref), channel_id=1, source_target_pairs={{0,4},{4,0},{1,5},{5,1},{2,6},{6,2},{3,7},{7,3},{8,12},{12,8},{9,1... | collective-permute-start | bytes 786440 | tf_op jit(solution)/shard_map/ppermute | solution.py:214
  101.5 24.7 %collective-permute-start.3 = (f32[2,4,128,128]{3,2,1,0:T(8,128)S(1)}, f32[2,4,128,128]{3,2,1,0:T(8,128)S(1)}, u32[]{:S(2)}, u32[]{:S(2)}) collective-permute-start(f32[2,4,128,128]{3,2,1,0:T(8,128)S(1)} %get-tuple-element.20), channel_id=1, source_target_pairs={{0,4},{4,0},{1,5},{5,1},{2,6},{6,2},{3,7},{7,3},{8,12},{12,8},{9,1... | collective-permute-start | bytes 1572872 | tf_op jit(solution)/shard_map/ppermute | solution.py:214
  105.2 21.0 %collective-permute-start.4 = (f32[2,4,128,2]{2,1,3,0:T(4,128)S(1)}, f32[2,4,128,2]{2,1,3,0:T(4,128)S(1)}, u32[]{:S(2)}, u32[]{:S(2)}) collective-permute-start(f32[2,4,128,2]{2,1,3,0:T(4,128)S(1)} %get-tuple-element.26), channel_id=1, source_target_pairs={{0,4},{4,0},{1,5},{5,1},{2,6},{6,2},{3,7},{7,3},{8,12},{12,8},{9,1... | collective-permute-start | bytes 24584 | tf_op jit(solution)/shard_map/ppermute | solution.py:214
  127.3 28.8 %copy-start.3 = (f32[512]{0:T(512)S(1)}, f32[512]{0:T(512)}, u32[]{:S(2)}) copy-start(f32[512]{0:T(512)} %param.19) | copy-start | bytes 6148
  151.3 1.2 collective-permute-start.5
  152.5 3.6 %collective-permute-start.6 = (f32[256]{0:T(256)S(1)}, f32[256]{0:T(256)S(1)}, u32[]{:S(2)}, u32[]{:S(2)}) collective-permute-start(f32[256]{0:T(256)S(1)} %add.62), channel_id=1, source_target_pairs={{0,2},{1,3},{2,0},{3,1},{4,6},{5,7},{6,4},{7,5},{8,10},{9,11},{10,... | collective-permute-start | bytes 3080 | tf_op jit(solution)/shard_map/ppermute | solution.py:222
  156.2 2.2 %copy-start.4 = (s32[2,4]{1,0:T(2,128)S(1)}, s32[2,4]{1,0:T(2,128)}, u32[]{:S(2)}) copy-start(s32[2,4]{1,0:T(2,128)} %param.24) | copy-start | bytes 100
  157.8 12.9 %collective-permute-start.7 = (bf16[2,128,1024]{2,1,0:T(8,128)(2,1)S(1)}, bf16[2,128,1024]{2,1,0:T(8,128)(2,1)S(1)}, u32[]{:S(2)}, u32[]{:S(2)}) collective-permute-start(bf16[2,128,1024]{2,1,0:T(8,128)(2,1)S(1)} %bitcast.25), channel_id=1, source_target_pairs={{0,4},{4,0},{1,5},{5,1},{2,6},{6,2},{3,7},{7,3},{8,12},{12,8},{9,1... | collective-permute-start | bytes 1572872 | tf_op jit(solution)/shard_map/ppermute | solution.py:214
Sparse Core Ops, SparseCore 0:
  9.5 51.9 all-gather.2
  63.6 84.0 all-gather.4

commit v4 on v3

--- a/solution.py
+++ b/solution.py
@@ -283,6 +283,230 @@
     )
 
 
+def pair_cache_kernel(len_ref, win_ref, seq_ref, q_ref, ck_ref, cv_ref, o_ref, m_ref, l_ref, *, scaling):
+    r = pl.program_id(0)
+    length_now = len_ref[r]
+    window_now = win_ref[r]
+    seq_index = seq_ref[0]
+    queries = q_ref[0]
+    rows, slots = queries.shape[0], ck_ref.shape[1]
+    dims = (((1,), (1,)), ((), ()))
+    scores = (
+        lax.dot_general(queries, ck_ref[0], dims, preferred_element_type=jnp.float32) * scaling
+    )
+    row = lax.broadcasted_iota(jnp.int32, (rows, slots), 0)
+    slot = lax.broadcasted_iota(jnp.int32, (rows, slots), 1) + seq_index * slots
+    edge = length_now + row - window_now
+    slot_pos = length_now - 1 - ((length_now - 1 - slot) & (WINDOW - 1))
+    allowed = (slot_pos >= 0) & (slot_pos > edge)
+    highest = jnp.max(jnp.where(allowed, scores, lowest), axis=1, keepdims=True)
+    weights = jnp.where(allowed, jnp.exp(scores - highest), 0.0)
+    o_ref[0, 0] = jnp.dot(weights.astype(jnp.bfloat16), cv_ref[0], preferred_element_type=jnp.float32)
+    m_ref[0, 0] = highest
+    l_ref[0, 0] = jnp.sum(weights, axis=1, keepdims=True)
+
+
+def pair_span_kernel(
+    len_ref, win_ref, sink_pos_ref, seq_ref, q_ref, nk_ref, nv_ref, sk_ref, sv_ref, o_ref, m_ref, l_ref, *, scaling
+):
+    r = pl.program_id(0)
+    length_now = len_ref[r]
+    window_now = win_ref[r]
+    queries = q_ref[0]
+    rows = queries.shape[0]
+    dims = (((1,), (1,)), ((), ()))
+    scores = (
+        lax.dot_general(queries, nk_ref[0], dims, preferred_element_type=jnp.float32) * scaling
+    )
+    row = lax.broadcasted_iota(jnp.int32, scores.shape, 0)
+    key = lax.broadcasted_iota(jnp.int32, scores.shape, 1)
+    allowed = key <= row
+    query_f = queries.astype(jnp.float32)
+    row_1 = lax.broadcasted_iota(jnp.int32, (rows, 1), 0)
+    edge = length_now + row_1 - window_now
+    sink_scores, sink_ok = [], []
+    for sink in range(SINKS):
+        key_f = sk_ref[0, sink : sink + 1, :].astype(jnp.float32)
+        sink_scores.append(jnp.sum(query_f * key_f, axis=1, keepdims=True) * scaling)
+        sink_ok.append(sink_pos_ref[r * SINKS + sink] <= edge)
+    highest = jnp.max(jnp.where(allowed, scores, lowest), axis=1, keepdims=True)
+    for part, ok in zip(sink_scores, sink_ok):
+        highest = jnp.maximum(highest, jnp.where(ok, part, lowest))
+    weights = jnp.where(allowed, jnp.exp(scores - highest), 0.0)
+    totals = jnp.sum(weights, axis=1, keepdims=True)
+    summed = jnp.dot(weights.astype(jnp.bfloat16), nv_ref[0], preferred_element_type=jnp.float32)
+    for sink in range(SINKS):
+        sink_w = jnp.where(sink_ok[sink], jnp.exp(sink_scores[sink] - highest), 0.0)
+        totals = totals + sink_w
+        value_f = sv_ref[0, sink : sink + 1, :].astype(jnp.float32)
+        summed = summed + sink_w.astype(jnp.bfloat16).astype(jnp.float32) * value_f
+    o_ref[0, 0] = summed
+    m_ref[0, 0] = highest
+    l_ref[0, 0] = totals
+
+
+def pair_partials(kernel, scalars, q_spec_index, operands, in_specs, req_local, heads, rows):
+    grid_spec = pltpu.PrefetchScalarGridSpec(
+        num_scalar_prefetch=len(scalars),
+        grid=(req_local, heads),
+        in_specs=in_specs,
+        out_specs=[
+            pl.BlockSpec((1, 1, rows, HEAD_DIM), lambda r, h, *_: (r, h, 0, 0)),
+            pl.BlockSpec((1, 1, rows, 1), lambda r, h, *_: (r, h, 0, 0)),
+            pl.BlockSpec((1, 1, rows, 1), lambda r, h, *_: (r, h, 0, 0)),
+        ],
+    )
+    shape = (req_local, heads, rows)
+    return pl.pallas_call(
+        functools.partial(kernel, scaling=HEAD_DIM ** (-0.5)),
+        grid_spec=grid_spec,
+        out_shape=[
+            jax.ShapeDtypeStruct(shape + (HEAD_DIM,), jnp.float32),
+            jax.ShapeDtypeStruct(shape + (1,), jnp.float32),
+            jax.ShapeDtypeStruct(shape + (1,), jnp.float32),
+        ],
+    )(*scalars, *operands)
+
+
+def merge_parts(first, second):
+    s1, m1, l1 = first
+    s2, m2, l2 = second
+    peak = jnp.maximum(m1, m2)
+    f1 = jnp.exp(m1 - peak)
+    f2 = jnp.exp(m2 - peak)
+    return (s1 * f1 + s2 * f2, peak, l1 * f1 + l2 * f2)
+
+
+def swap_seq(x):
+    return lax.ppermute(x, "seq", [(0, 1), (1, 0)])
+
+
+def on_device_pair(
+    tokens,
+    w_query,
+    w_key,
+    w_value,
+    q_gain,
+    k_gain,
+    cache_keys,
+    cache_values,
+    sink_keys,
+    sink_values,
+    sink_pos,
+    cache_len,
+    span_len,
+    window_len,
+):
+    req_local, span_local, model_width = tokens.shape
+    local_cols = w_query.shape[1]
+    half = local_cols // 2
+    heads_local = local_cols // HEAD_DIM
+    heads_half = heads_local // 2
+    seq_index = lax.axis_index("seq")
+    first = seq_index == 0
+    span_total = 2 * span_local
+    slot_local = cache_keys.shape[1]
+    weights = (w_query, w_key, w_value)
+    mine = jnp.concatenate(
+        [lax.dynamic_slice_in_dim(w, seq_index * half, half, axis=1) for w in weights], axis=1
+    )
+    other = jnp.concatenate(
+        [lax.dynamic_slice_in_dim(w, (1 - seq_index) * half, half, axis=1) for w in weights], axis=1
+    )
+    got = swap_seq(other)
+    pair_rows = jnp.where(first, jnp.concatenate([mine, got], 0), jnp.concatenate([got, mine], 0))
+    w_all = lax.all_gather(pair_rows, "req", axis=0, tiled=True)
+    tokens_other = swap_seq(tokens)
+    tokens_all = jnp.where(
+        first,
+        jnp.concatenate([tokens, tokens_other], axis=1),
+        jnp.concatenate([tokens_other, tokens], axis=1),
+    )
+    token_rows = tokens_all.reshape(req_local * span_total, model_width)
+    proj = jnp.dot(token_rows, w_all, preferred_element_type=jnp.float32)
+    q_proj = proj[:, :half]
+    k_proj = proj[:, half : 2 * half]
+    v_proj = proj[:, 2 * half :]
+    squares = jnp.stack([jnp.sum(q_proj * q_proj, axis=1), jnp.sum(k_proj * k_proj, axis=1)])
+    squares = tp_sum(squares)
+    squares = squares + swap_seq(squares)
+    offsets = jnp.arange(span_total, dtype=jnp.int32)
+    positions = (cache_len[:, None] + offsets[None, :]).reshape(-1)
+    q_gain_half = lax.dynamic_slice_in_dim(q_gain, seq_index * half, half)
+    k_gain_half = lax.dynamic_slice_in_dim(k_gain, seq_index * half, half)
+    q_half = normalize_rotate(q_proj, squares[0], q_gain_half, positions, D, HEAD_DIM).reshape(
+        req_local, span_total, half
+    )
+    k_half = normalize_rotate(k_proj, squares[1], k_gain_half, positions, D, HEAD_DIM).reshape(
+        req_local, span_total, half
+    )
+    v_half = v_proj.astype(jnp.bfloat16).reshape(req_local, span_total, half)
+    q_other = swap_seq(q_half)
+    q_full = jnp.where(
+        first, jnp.concatenate([q_half, q_other], -1), jnp.concatenate([q_other, q_half], -1)
+    )
+    seq_arr = jnp.reshape(seq_index, (1,)).astype(jnp.int32)
+    head_block = lambda r, h, *_: (r, 0, h)
+    cache_part = pair_partials(
+        pair_cache_kernel,
+        (cache_len, window_len, seq_arr),
+        None,
+        (q_full, cache_keys, cache_values),
+        [
+            pl.BlockSpec((1, span_total, HEAD_DIM), head_block),
+            pl.BlockSpec((1, slot_local, HEAD_DIM), head_block),
+            pl.BlockSpec((1, slot_local, HEAD_DIM), head_block),
+        ],
+        req_local,
+        heads_local,
+        span_total,
+    )
+    sink_block = lambda r, h, len_ref, win_ref, pos_ref, seq_ref: (r, 0, h + seq_ref[0] * heads_half)
+    span_part = pair_partials(
+        pair_span_kernel,
+        (cache_len, window_len, sink_pos.reshape(-1), seq_arr),
+        None,
+        (q_half, k_half, v_half, sink_keys, sink_values),
+        [
+            pl.BlockSpec((1, span_total, HEAD_DIM), head_block),
+            pl.BlockSpec((1, span_total, HEAD_DIM), head_block),
+            pl.BlockSpec((1, span_total, HEAD_DIM), head_block),
+            pl.BlockSpec((1, SINKS, HEAD_DIM), sink_block),
+            pl.BlockSpec((1, SINKS, HEAD_DIM), sink_block),
+        ],
+        req_local,
+        heads_half,
+        span_total,
+    )
+    empty = (
+        jnp.zeros_like(cache_part[0]),
+        jnp.full_like(cache_part[1], lowest),
+        jnp.zeros_like(cache_part[2]),
+    )
+    span_wide = tuple(
+        lax.dynamic_update_slice_in_dim(e, p, seq_index * heads_half, axis=1)
+        for e, p in zip(empty, span_part)
+    )
+    merged = merge_parts(cache_part, span_wide)
+    own_rows = tuple(
+        lax.dynamic_slice_in_dim(x, seq_index * span_local, span_local, axis=2) for x in merged
+    )
+    far_rows = tuple(
+        lax.dynamic_slice_in_dim(x, (1 - seq_index) * span_local, span_local, axis=2)
+        for x in merged
+    )
+    got_sum = swap_seq(far_rows[0])
+    got_stats = swap_seq(jnp.concatenate([far_rows[1], far_rows[2]], axis=-1))
+    total_sum, _, total = merge_parts(own_rows, (got_sum, got_stats[..., 0:1], got_stats[..., 1:2]))
+    own_offsets = seq_index * span_local + jnp.arange(span_local, dtype=jnp.int32)
+    live_rows = (own_offsets[None, :] < span_len[:, None])[:, None, :, None]
+    safe_total = jnp.where(live_rows, total, 1.0)
+    mixed = jnp.where(live_rows, total_sum / safe_total, 0.0)
+    return (
+        mixed.transpose(0, 2, 1, 3).reshape(req_local, span_local, local_cols).astype(jnp.bfloat16)
+    )
+
+
 def solution(mesh):
     placed = (
         P("req", "seq", None),
@@ -300,6 +524,7 @@
         P("req"),
         P("req"),
     )
+    body = on_device_pair if mesh.shape["seq"] == 2 else on_device
     return jax.shard_map(
-        on_device, mesh=mesh, in_specs=placed, out_specs=P("req", "seq", "tp"), check_vma=False
-    )
+        body, mesh=mesh, in_specs=placed, out_specs=P("req", "seq", "tp"), check_vma=False
+    )

time: 188 us -> 170 us (0.904)
  waiting for transfers between devices: 120 us -> 93.4 us
  other arithmetic: 8.08 us -> 15.9 us
  Pallas kernels: 25.7 us -> 20.4 us
  starting transfers between devices: 6.52 us -> 11.5 us
  local copies, waits for them, and re-layouts: 7.72 us -> 10.6 us
    all_gather x2 -> x1, waiting for transfers between devices: 71.9 us -> 38.4 us  [on_device_pair(): w_all = lax.all_gather(pair_rows, 'req', axis=0, tiled=True)]
    ppermute x4 -> x6, waiting for transfers between devices: 42 us -> 52.7 us  [swap_seq(): return lax.ppermute(x, 'seq', [(0, 1), (1, 0)])]
    ppermute x4 -> x6, starting transfers between devices: 3.4 us -> 9.91 us  [swap_seq(): return lax.ppermute(x, 'seq', [(0, 1), (1, 0)])]
    pallas_call x2, Pallas kernels: 25.7 us -> 20.4 us  [pair_partials(): pl.pallas_call(functools.partial(kernel, scaling=HEAD_DIM ** (-0.5)), gri...]
    select_n x0 -> x3, other arithmetic: none -> 4.5 us  [the longest x1 2.34 us: on_device_pair(): jnp.where(first, jnp.concatenate([tokens, tokens_other], axis=1), jnp.con...]
    exp x0 -> x2, other arithmetic: none -> 3.79 us  [merge_parts(): f1 = jnp.exp(m1 - peak)]
    ppermute x4 -> x2, waiting for transfers between devices: 5.86 us -> 2.27 us  [tp_sum(): x = x + lax.ppermute(x, 'tp', [(a, a ^ bit) for a in range(count)])]
    dynamic_slice x0 -> x7, local copies, waits for them, and re-layouts: none -> 3.3 us  [the longest x2 2.21 us: on_device_pair(): lax.dynamic_slice_in_dim(w, seq_index * half, half, axis=1)]
  transfers between devices with their start and end apart: 10 -> 9, of which waited for: 9 -> 7; matrix products, arithmetic and copies ran while one was open for 8% -> 5% of each run, Pallas kernels for 9% -> 3%
where the time goes in v4:
time: 170 us
  waiting for transfers between devices  93.4 us (55%)
  Pallas kernels  20.4 us (12%)
  other arithmetic  15.9 us (9%)
  between operations  13.8 us (8%)
  starting transfers between devices  11.5 us (7%)
  local copies, waits for them, and re-layouts  10.6 us (6%)
  matrix products  4.34 us (3%)
    ppermute x6, waiting for transfers between devices, swap_seq(): return lax.ppermute(x, 'seq', [(0, 1), (1, 0)])  52.7 us
    all_gather x1, waiting for transfers between devices, on_device_pair(): w_all = lax.all_gather(pair_rows, 'req', axis=0, tiled=True)  38.4 us
    pallas_call x2, Pallas kernels, pair_partials(): pl.pallas_call(functools.partial(kernel, scaling=HEAD_DIM ** (-0.5)), gri...  20.4 us
    ppermute x6, starting transfers between devices, swap_seq(): return lax.ppermute(x, 'seq', [(0, 1), (1, 0)])  9.91 us
    dot_general x1, matrix products, on_device_pair(): proj = jnp.dot(token_rows, w_all, preferred_element_type=jnp.float32)  4.34 us
    exp x2, other arithmetic, merge_parts(): f1 = jnp.exp(m1 - peak)  3.79 us
  transfers between devices with their start and end apart: 9, of which 7 were waited for; matrix products, arithmetic and copies ran while one was open for 5% of the time, Pallas kernels for 3%

profile of v4, /device:TPU:0, one launch (start us, length us, event | category | flops | bytes accessed | tf_op | source)
XLA Modules:
  0.0 169.9 jit_solution(11455723946617024264)
XLA Ops:
  6.5 1.0 constant_dynamic-slice_fusion.8
  7.5 1.2 constant_dynamic-slice_fusion.6
  8.8 3.0 %collective-permute-start.1 = (bf16[256,768]{1,0:T(8,128)(2,1)S(1)}, bf16[256,768]{1,0:T(8,128)(2,1)S(1)}, u32[]{:S(2)}, u32[]{:S(2)}) collective-permute-start(bf16[256,768]{1,0:T(8,128)(2,1)S(1)} %pad_maximum_fusion.1), channel_id=1, source_target_pairs={{0,4},{4,0},{1,5},{5,1},{2,6},{6,2},{3,7},{7,3},{8,12},{12,8},{9,1... | collective-permute-start | bytes 1179656 | tf_op jit(solution)/shard_map/ppermute | solution.py:381
  11.8 9.1 %collective-permute-done.1 = bf16[256,768]{1,0:T(8,128)(2,1)S(1)} collective-permute-done((bf16[256,768]{1,0:T(8,128)(2,1)S(1)}, bf16[256,768]{1,0:T(8,128)(2,1)S(1)}, u32[]{:S(2)}, u32[]{:S(2)}) %collective-permute-start.1) | collective-permute-done | bytes 393248 | tf_op jit(solution)/shard_map/ppermute | solution.py:381
  20.9 1.2 maximum_select_fusion.1
  22.2 1.8 %collective-permute-start = (bf16[2,128,2048]{2,1,0:T(8,128)(2,1)S(1)}, bf16[2,128,2048]{2,1,0:T(8,128)(2,1)S(1)}, u32[]{:S(2)}, u32[]{:S(2)}) collective-permute-start(bf16[2,128,2048]{2,1,0:T(8,128)(2,1)S(1)} %copy-done.6), channel_id=1, source_target_pairs={{0,4},{4,0},{1,5},{5,1},{2,6},{6,2},{3,7},{7,3},{8,12},{12,8},{9,1... | collective-permute-start | bytes 3145736 | tf_op jit(solution)/shard_map/ppermute | solution.py:381
  24.1 22.5 %collective-permute-done = bf16[2,128,2048]{2,1,0:T(8,128)(2,1)S(1)} collective-permute-done((bf16[2,128,2048]{2,1,0:T(8,128)(2,1)S(1)}, bf16[2,128,2048]{2,1,0:T(8,128)(2,1)S(1)}, u32[]{:S(2)}, u32[]{:S(2)}) %collective-permute-start) | collective-permute-done | bytes 1048608 | tf_op jit(solution)/shard_map/ppermute | solution.py:381
  46.6 2.3 %maximum_select_fusion = bf16[2,256,2048]{2,1,0:T(8,128)(2,1)} fusion(bf16[2,128,2048]{2,1,0:T(8,128)(2,1)S(1)} %collective-permute-done, bf16[2,128,2048]{2,1,0:T(8,128)(2,1)S(1)} %copy-done.6, pred[]{:T(512)S(6)} %eq.3), kind=kLoop, calls=%fused_computation | loop fusion | flops 9437184 | bytes 4194305 | tf_op jit(solution)/shard_map/jit(_where)/select_n | solution.py:420
  49.0 38.4 %all-gather.2.cloned.1.call-done = bf16[2048,768]{1,0:T(8,128)(2,1)} async-done(((bf16[512,768]{1,0:T(8,128)(2,1)}), bf16[2048,768]{1,0:T(8,128)(2,1)}) %all-gather.2.cloned.1.call-update) | async-done | bytes 3145744 | tf_op jit(solution)/shard_map/all_gather | solution.py:418
  87.4 4.3 %fusion.15 = f32[512,768]{1,0:T(8,128)S(1)} fusion(bf16[512,2048]{1,0:T(8,128)(2,1)} %bitcast.15, bf16[2048,768]{1,0:T(8,128)(2,1)} %all-gather.2.cloned.1.call-done), kind=kOutput, calls=%fused_computation.60 | convolution fusion | flops 1610612736 | bytes 6815744 | tf_op jit(solution)/shard_map/dot_general | solution.py:426
  91.7 0.2 multiply_reduce_fusion.1
  92.1 1.1 collective-permute-done.2
  93.2 1.5 collective-permute-start.3
  94.7 1.0 multiply_cosine_fusion
  95.7 1.1 collective-permute-done.3
  96.9 1.5 collective-permute-start.4
  98.4 0.7 reshape.147.sink_pos_ref
  99.2 0.7 slice.96
  100.0 0.6 collective-permute-done.4
  100.6 0.2 multiply_multiply_fusion
  100.8 0.3 reshape.148
  101.1 0.3 reshape.146
  101.3 1.8 %subtract_convert_fusion = (bf16[512,2,64]{2,1,0:T(2,128)(2,1)S(1)}, bf16[512,2,64]{2,1,0:T(2,128)(2,1)S(1)}, bf16[512,2,64]{2,1,0:T(2,128)(2,1)S(1)}, bf16[512,2,64]{2,1,0:T(2,128)(2,1)S(1)}) fusion(f32[512,2,128]{2,1,0:T(2,128)S(1)} %reshape.148, f32[512,64]{1,0:T(8,128)S(1)} %get-tuple-element.42, f32[512,64]{1,0:T(8,128)S(1)} %get-tuple-element.41, ...), kind=kLoop, calls=%fused_computation.19 | loop fusion | flops 1048576 | bytes 1835008 | tf_op jit(solution)/shard_map/convert.1
  103.1 0.7 pad_maximum_fusion.2
  103.8 0.2 convert_element_type.33.q_ref
  104.0 0.7 pad_maximum_fusion.3
  104.8 0.9 convert_element_type.34.nk_ref
  105.6 1.5 collective-permute-start.5
  107.1 4.9 %shard_map.137 = (f32[2,2,256,128]{3,2,1,0:T(8,128)}, f32[2,2,256,1]{3,2,1,0:T(8,128)}, f32[2,2,256,1]{3,2,1,0:T(8,128)}) custom-call(s32[2]{0:T(128)} %len_ref.3, s32[2]{0:T(128)} %win_ref.3, s32[8]{0:T(128)} %reshape.147.sink_pos_ref, s32[1]{0:T(128)} %bitcast.seq_ref, bf16[2,256,256]{2,1,0:T(8,128)(2,1)} %copy-done.4, ...), custom_call_target="tpu_custom_call" | custom-call | tf_op jit(solution)/shard_map/pallas_call | solution.py:360
  112.1 1.2 constant_dynamic-update-slice_fusion
  113.6 0.7 copy-done.1
  114.3 0.2 copy-done.5
  114.5 0.9 maximum_select_fusion.2.q_ref
  115.4 15.5 %shard_map.136 = (f32[2,4,256,128]{3,2,1,0:T(8,128)}, f32[2,4,256,1]{3,2,1,0:T(8,128)}, f32[2,4,256,1]{3,2,1,0:T(8,128)}) custom-call(s32[2]{0:T(128)} %len_ref.3, s32[2]{0:T(128)} %win_ref.3, s32[1]{0:T(128)} %bitcast.seq_ref, bf16[2,256,512]{2,1,0:T(8,128)(2,1)} %maximum_select_fusion.2.q_ref, bf16[2,2048,512]{2,1,0:T(8,128)(2,1)} %ck_ref.1, ...), custom_call_target="tpu_custom_call" | custom-call | tf_op jit(solution)/shard_map/pallas_call | solution.py:360
  130.9 2.0 %fusion.5 = (f32[2,4,256]{2,1,0:T(4,128)S(1)}, f32[2,4,256]{2,1,0:T(4,128)S(1)}, f32[2,4,256,1]{3,2,1,0:T(8,128)S(1)}) fusion(f32[2,4,256,1]{3,2,1,0:T(8,128)} %get-tuple-element.12, f32[2,4,256,1]{3,2,1,0:T(8,128)S(1)} %constant_dynamic-update-slice_fusion.2), kind=kLoop, calls=%fused_computation.26 | loop fusion | flops 6144 | bytes 40960 | tf_op jit(solution)/shard_map/exp | solution.py:375
  133.0 0.1 copy-done.8
  133.0 0.4 multiply_add_fusion
  133.5 0.8 copy-done.7
  134.3 0.6 multiply_add_fusion.1
  134.9 0.9 constant_dynamic-slice_fusion
  135.8 0.6 collective-permute-start.7
  136.3 0.2 pad_maximum_fusion
  136.5 1.5 collective-permute-start.6
  138.1 20.5 %collective-permute-done.6 = f32[2,4,128,2]{3,2,1,0:T(8,128)S(1)} collective-permute-done((f32[2,4,128,2]{3,2,1,0:T(8,128)S(1)}, f32[2,4,128,2]{3,2,1,0:T(8,128)S(1)}, u32[]{:S(2)}, u32[]{:S(2)}) %collective-permute-start.6) | collective-permute-done | bytes 8224 | tf_op jit(solution)/shard_map/ppermute | solution.py:381
  158.6 1.8 %fusion.9 = (f32[2,4,128]{2,1,0:T(4,128)S(1)}, f32[2,4,128]{2,1,0:T(4,128)S(1)}, f32[2,4,128]{2,1,0:T(4,128)S(1)}) fusion(f32[2,4,128,2]{3,2,1,0:T(8,128)S(1)} %collective-permute-done.6, f32[2,4,256,1]{3,2,1,0:T(8,128)S(1)} %get-tuple-element.24, s32[]{:T(128)S(6)} %select_n.73, f32[2,4,256,1]{3,2,1,0:T(8,128)} %copy-done.3, ...), kind=kLoop, calls=%fused_computation.35 | loop fusion | flops 7168 | bytes 28932 | tf_op jit(solution)/shard_map/exp | solution.py:375
  160.4 1.6 fusion.7
  162.0 0.2 copy.22
  162.2 0.9 copy.23
  (53 shorter events, 0.9 us)
Async XLA Ops:
  6.5 80.8 %all-gather.2.cloned.1.call-start = ((), (), s32[]{:S(2)}) async-start(), calls=%async_computation | async-start | bytes 3932160 | tf_op jit(solution)/shard_map/all_gather | solution.py:418
  7.5 14.7 %copy-start.6 = (bf16[2,128,2048]{2,1,0:T(8,128)(2,1)S(1)}, bf16[2,128,2048]{2,1,0:T(8,128)(2,1)}, u32[]{:S(2)}) copy-start(bf16[2,128,2048]{2,1,0:T(8,128)(2,1)} %param.14) | copy-start | bytes 3145732
  7.5 16.5 %copy-start.11 = (s32[2]{0:T(128)S(1)}, s32[2]{0:T(128)}, u32[]{:S(2)}) copy-start(s32[2]{0:T(128)} %len_ref.3) | copy-start | bytes 28
  8.8 12.1 %collective-permute-start.1 = (bf16[256,768]{1,0:T(8,128)(2,1)S(1)}, bf16[256,768]{1,0:T(8,128)(2,1)S(1)}, u32[]{:S(2)}, u32[]{:S(2)}) collective-permute-start(bf16[256,768]{1,0:T(8,128)(2,1)S(1)} %pad_maximum_fusion.1), channel_id=1, source_target_pairs={{0,4},{4,0},{1,5},{5,1},{2,6},{6,2},{3,7},{7,3},{8,12},{12,8},{9,1... | collective-permute-start | bytes 1179656 | tf_op jit(solution)/shard_map/ppermute | solution.py:381
  22.2 24.4 %collective-permute-start = (bf16[2,128,2048]{2,1,0:T(8,128)(2,1)S(1)}, bf16[2,128,2048]{2,1,0:T(8,128)(2,1)S(1)}, u32[]{:S(2)}, u32[]{:S(2)}) collective-permute-start(bf16[2,128,2048]{2,1,0:T(8,128)(2,1)S(1)} %copy-done.6), channel_id=1, source_target_pairs={{0,4},{4,0},{1,5},{5,1},{2,6},{6,2},{3,7},{7,3},{8,12},{12,8},{9,1... | collective-permute-start | bytes 3145736 | tf_op jit(solution)/shard_map/ppermute | solution.py:381
  87.4 11.1 %copy-start.14 = (s32[2,4]{1,0:T(2,128)S(1)}, s32[2,4]{1,0:T(2,128)}, u32[]{:S(2)}) copy-start(s32[2,4]{1,0:T(2,128)} %param.24) | copy-start | bytes 100
  87.4 11.7 %copy-start.12 = (f32[512]{0:T(512)S(1)}, f32[512]{0:T(512)}, u32[]{:S(2)}) copy-start(f32[512]{0:T(512)} %param.19) | copy-start | bytes 6148
  87.4 11.8 %copy-start.13 = (f32[512]{0:T(512)S(1)}, f32[512]{0:T(512)}, u32[]{:S(2)}) copy-start(f32[512]{0:T(512)} %param.18) | copy-start | bytes 6148
  91.9 1.2 collective-permute-start.2
  93.2 3.7 %collective-permute-start.3 = (f32[2,512]{1,0:T(2,128)S(1)}, f32[2,512]{1,0:T(2,128)S(1)}, u32[]{:S(2)}, u32[]{:S(2)}) collective-permute-start(f32[2,512]{1,0:T(2,128)S(1)} %fusion.14), channel_id=1, source_target_pairs={{0,2},{1,3},{2,0},{3,1},{4,6},{5,7},{6,4},{7,5},{8,10},{9,11},{10,... | collective-permute-start | bytes 12296 | tf_op jit(solution)/shard_map/ppermute | solution.py:222
  96.9 3.7 %collective-permute-start.4 = (f32[2,512]{1,0:T(2,128)S(1)}, f32[2,512]{1,0:T(2,128)S(1)}, u32[]{:S(2)}, u32[]{:S(2)}) collective-permute-start(f32[2,512]{1,0:T(2,128)S(1)} %fusion.18), channel_id=1, source_target_pairs={{0,4},{4,0},{1,5},{5,1},{2,6},{6,2},{3,7},{7,3},{8,12},{12,8},{9,1... | collective-permute-start | bytes 12296 | tf_op jit(solution)/shard_map/ppermute | solution.py:381
  104.0 3.1 %copy-start.4 = (bf16[2,256,256]{2,1,0:T(8,128)(2,1)}, bf16[2,256,256]{2,1,0:T(8,128)(2,1)S(1)}, u32[]{:S(2)}) copy-start(bf16[2,256,256]{2,1,0:T(8,128)(2,1)S(1)} %convert_element_type.33.q_ref) | copy-start | bytes 786436
  105.6 8.7 %collective-permute-start.5 = (bf16[2,256,256]{2,1,0:T(8,128)(2,1)S(1)}, bf16[2,256,256]{2,1,0:T(8,128)(2,1)S(1)}, u32[]{:S(2)}, u32[]{:S(2)}) collective-permute-start(bf16[2,256,256]{2,1,0:T(8,128)(2,1)S(1)} %convert_element_type.33.q_ref), channel_id=1, source_target_pairs={{0,4},{4,0},{1,5},{5,1},{2,6},{6,2},{3,7},{7,3},{8,12},{12,8},{9,1... | collective-permute-start | bytes 786440 | tf_op jit(solution)/shard_map/ppermute | solution.py:381
  112.0 1.4 copy-start.10
  112.1 1.4 copy-start.9
  113.3 1.0 copy-start.1
  113.3 1.2 copy-start.5
  130.9 2.1 %copy-start = (f32[2,4,256,1]{3,2,1,0:T(8,128)S(1)}, f32[2,4,256,1]{3,2,1,0:T(8,128)}, u32[]{:S(2)}) copy-start(f32[2,4,256,1]{3,2,1,0:T(8,128)} %get-tuple-element.12) | copy-start | bytes 24580
  130.9 2.1 %copy-start.2 = (f32[2,4,256,1]{3,2,1,0:T(8,128)S(1)}, f32[2,4,256,1]{3,2,1,0:T(8,128)}, u32[]{:S(2)}) copy-start(f32[2,4,256,1]{3,2,1,0:T(8,128)} %copy-done.1) | copy-start | bytes 24580
  130.9 2.2 %copy-start.8 = (f32[2,4,256,1]{3,2,1,0:T(8,128)S(1)}, f32[2,4,256,1]{3,2,1,0:T(8,128)}, u32[]{:S(2)}) copy-start(f32[2,4,256,1]{3,2,1,0:T(8,128)} %get-tuple-element.15) | copy-start | bytes 24580
  133.0 1.2 copy-start.7
  133.4 1.5 copy-start.3
  134.9 3.2 %copy-start.15 = (s32[2]{0:T(128)S(1)}, s32[2]{0:T(128)}, u32[]{:S(2)}) copy-start(s32[2]{0:T(128)} %param.26) | copy-start | bytes 28
  135.8 24.6 %collective-permute-start.7 = (f32[2,4,128,128]{3,2,1,0:T(8,128)}, f32[2,4,128,128]{3,2,1,0:T(8,128)}, u32[]{:S(2)}, u32[]{:S(2)}) collective-permute-start(f32[2,4,128,128]{3,2,1,0:T(8,128)} %constant_dynamic-slice_fusion), channel_id=1, source_target_pairs={{0,4},{4,0},{1,5},{5,1},{2,6},{6,2},{3,7},{7,3},{8,12},{12,8},{9,1... | collective-permute-start | bytes 1572872 | tf_op jit(solution)/shard_map/ppermute | solution.py:381
  136.5 22.1 %collective-permute-start.6 = (f32[2,4,128,2]{3,2,1,0:T(8,128)S(1)}, f32[2,4,128,2]{3,2,1,0:T(8,128)S(1)}, u32[]{:S(2)}, u32[]{:S(2)}) collective-permute-start(f32[2,4,128,2]{3,2,1,0:T(8,128)S(1)} %pad_maximum_fusion), channel_id=1, source_target_pairs={{0,4},{4,0},{1,5},{5,1},{2,6},{6,2},{3,7},{7,3},{8,12},{12,8},{9,1... | collective-permute-start | bytes 24584 | tf_op jit(solution)/shard_map/ppermute | solution.py:381
Sparse Core Ops, SparseCore 0:
  22.3 64.9 all-gather.1

commit v5 on v4

--- a/solution.py
+++ b/solution.py
@@ -283,27 +283,39 @@
     )
 
 
-def pair_cache_kernel(len_ref, win_ref, seq_ref, q_ref, ck_ref, cv_ref, o_ref, m_ref, l_ref, *, scaling):
+def pair_cache_kernel(
+    len_ref, win_ref, seq_ref, first_ref, q_ref, ck_ref, cv_ref, o_ref, m_ref, l_ref, *, scaling
+):
     r = pl.program_id(0)
-    length_now = len_ref[r]
+    length_now = len_ref[r] + first_ref[0]
     window_now = win_ref[r]
     seq_index = seq_ref[0]
-    queries = q_ref[0]
-    rows, slots = queries.shape[0], ck_ref.shape[1]
+    rows, slots = q_ref.shape[1], ck_ref.shape[1]
+    heads = q_ref.shape[2] // HEAD_DIM
     dims = (((1,), (1,)), ((), ()))
-    scores = (
-        lax.dot_general(queries, ck_ref[0], dims, preferred_element_type=jnp.float32) * scaling
-    )
     row = lax.broadcasted_iota(jnp.int32, (rows, slots), 0)
     slot = lax.broadcasted_iota(jnp.int32, (rows, slots), 1) + seq_index * slots
     edge = length_now + row - window_now
     slot_pos = length_now - 1 - ((length_now - 1 - slot) & (WINDOW - 1))
     allowed = (slot_pos >= 0) & (slot_pos > edge)
-    highest = jnp.max(jnp.where(allowed, scores, lowest), axis=1, keepdims=True)
-    weights = jnp.where(allowed, jnp.exp(scores - highest), 0.0)
-    o_ref[0, 0] = jnp.dot(weights.astype(jnp.bfloat16), cv_ref[0], preferred_element_type=jnp.float32)
-    m_ref[0, 0] = highest
-    l_ref[0, 0] = jnp.sum(weights, axis=1, keepdims=True)
+    bias = jnp.where(allowed, 0.0, lowest)
+    for h in range(heads):
+        cols = slice(h * HEAD_DIM, (h + 1) * HEAD_DIM)
+        scores = (
+            lax.dot_general(q_ref[0, :, cols], ck_ref[0, :, cols], dims, preferred_element_type=jnp.float32)
+            * scaling
+            + bias
+        )
+        highest = jnp.max(scores, axis=1, keepdims=True)
+        weights = jnp.exp(scores - highest)
+        some = highest > lowest
+        o_ref[0, h] = jnp.where(
+            some,
+            jnp.dot(weights.astype(jnp.bfloat16), cv_ref[0, :, cols], preferred_element_type=jnp.float32),
+            0.0,
+        )
+        m_ref[0, h] = highest
+        l_ref[0, h] = jnp.where(some, jnp.sum(weights, axis=1, keepdims=True), 0.0)
 
 
 def pair_span_kernel(
@@ -312,48 +324,107 @@
     r = pl.program_id(0)
     length_now = len_ref[r]
     window_now = win_ref[r]
-    queries = q_ref[0]
-    rows = queries.shape[0]
+    rows = q_ref.shape[1]
+    heads = q_ref.shape[2] // HEAD_DIM
     dims = (((1,), (1,)), ((), ()))
-    scores = (
-        lax.dot_general(queries, nk_ref[0], dims, preferred_element_type=jnp.float32) * scaling
-    )
-    row = lax.broadcasted_iota(jnp.int32, scores.shape, 0)
-    key = lax.broadcasted_iota(jnp.int32, scores.shape, 1)
+    row = lax.broadcasted_iota(jnp.int32, (rows, rows), 0)
+    key = lax.broadcasted_iota(jnp.int32, (rows, rows), 1)
     allowed = key <= row
-    query_f = queries.astype(jnp.float32)
     row_1 = lax.broadcasted_iota(jnp.int32, (rows, 1), 0)
     edge = length_now + row_1 - window_now
-    sink_scores, sink_ok = [], []
-    for sink in range(SINKS):
-        key_f = sk_ref[0, sink : sink + 1, :].astype(jnp.float32)
-        sink_scores.append(jnp.sum(query_f * key_f, axis=1, keepdims=True) * scaling)
-        sink_ok.append(sink_pos_ref[r * SINKS + sink] <= edge)
-    highest = jnp.max(jnp.where(allowed, scores, lowest), axis=1, keepdims=True)
-    for part, ok in zip(sink_scores, sink_ok):
-        highest = jnp.maximum(highest, jnp.where(ok, part, lowest))
-    weights = jnp.where(allowed, jnp.exp(scores - highest), 0.0)
-    totals = jnp.sum(weights, axis=1, keepdims=True)
-    summed = jnp.dot(weights.astype(jnp.bfloat16), nv_ref[0], preferred_element_type=jnp.float32)
-    for sink in range(SINKS):
-        sink_w = jnp.where(sink_ok[sink], jnp.exp(sink_scores[sink] - highest), 0.0)
-        totals = totals + sink_w
-        value_f = sv_ref[0, sink : sink + 1, :].astype(jnp.float32)
-        summed = summed + sink_w.astype(jnp.bfloat16).astype(jnp.float32) * value_f
-    o_ref[0, 0] = summed
-    m_ref[0, 0] = highest
-    l_ref[0, 0] = totals
+    sink_ok = [sink_pos_ref[r * SINKS + sink] <= edge for sink in range(SINKS)]
+    for h in range(heads):
+        cols = slice(h * HEAD_DIM, (h + 1) * HEAD_DIM)
+        queries = q_ref[0, :, cols]
+        scores = (
+            lax.dot_general(queries, nk_ref[0, :, cols], dims, preferred_element_type=jnp.float32)
+            * scaling
+        )
+        query_f = queries.astype(jnp.float32)
+        sink_scores = []
+        for sink in range(SINKS):
+            key_f = sk_ref[0, sink : sink + 1, cols].astype(jnp.float32)
+            sink_scores.append(jnp.sum(query_f * key_f, axis=1, keepdims=True) * scaling)
+        highest = jnp.max(jnp.where(allowed, scores, lowest), axis=1, keepdims=True)
+        for part, ok in zip(sink_scores, sink_ok):
+            highest = jnp.maximum(highest, jnp.where(ok, part, lowest))
+        weights = jnp.where(allowed, jnp.exp(scores - highest), 0.0)
+        totals = jnp.sum(weights, axis=1, keepdims=True)
+        summed = jnp.dot(
+            weights.astype(jnp.bfloat16), nv_ref[0, :, cols], preferred_element_type=jnp.float32
+        )
+        for sink in range(SINKS):
+            sink_w = jnp.where(sink_ok[sink], jnp.exp(sink_scores[sink] - highest), 0.0)
+            totals = totals + sink_w
+            value_f = sv_ref[0, sink : sink + 1, cols].astype(jnp.float32)
+            summed = summed + sink_w.astype(jnp.bfloat16).astype(jnp.float32) * value_f
+        o_ref[0, h] = summed
+        m_ref[0, h] = highest
+        l_ref[0, h] = totals
+
+
+def merged_cache_kernel(
+    len_ref, win_ref, seq_ref, first_ref, owner_ref, qa_ref, qb_ref, ck_ref, cv_ref, ss_ref, sm_ref,
+    sl_ref, o_ref, st_ref, *, scaling, normalize
+):
+    r = pl.program_id(0)
+    length_now = len_ref[r] + first_ref[0]
+    window_now = win_ref[r]
+    seq_index = seq_ref[0]
+    rows, slots = qa_ref.shape[1], ck_ref.shape[1]
+    heads_half = ss_ref.shape[1]
+    heads = 2 * heads_half
+    dims = (((1,), (1,)), ((), ()))
+    row = lax.broadcasted_iota(jnp.int32, (rows, slots), 0)
+    slot = lax.broadcasted_iota(jnp.int32, (rows, slots), 1) + seq_index * slots
+    edge = length_now + row - window_now
+    cached = len_ref[r]
+    slot_pos = cached - 1 - ((cached - 1 - slot) & (WINDOW - 1))
+    allowed = (slot_pos >= 0) & (slot_pos > edge)
+    bias = jnp.where(allowed, 0.0, lowest)
+    for h in range(heads):
+        cols = slice(h * HEAD_DIM, (h + 1) * HEAD_DIM)
+        j = h % heads_half
+        local = slice(j * HEAD_DIM, (j + 1) * HEAD_DIM)
+        here = (h // heads_half) == seq_index
+        queries = jnp.where(here, qa_ref[0, :, local], qb_ref[0, :, local])
+        scores = (
+            lax.dot_general(queries, ck_ref[0, :, cols], dims, preferred_element_type=jnp.float32)
+            * scaling
+            + bias
+        )
+        highest = jnp.max(scores, axis=1, keepdims=True)
+        weights = jnp.exp(scores - highest)
+        some = highest > lowest
+        summed = jnp.where(
+            some,
+            jnp.dot(weights.astype(jnp.bfloat16), cv_ref[0, :, cols], preferred_element_type=jnp.float32),
+            0.0,
+        )
+        totals = jnp.where(some, jnp.sum(weights, axis=1, keepdims=True), 0.0)
+        span_high = sm_ref[0, j]
+        peak = jnp.maximum(highest, span_high)
+        f_cache = jnp.exp(highest - peak)
+        f_span = jnp.exp(span_high - peak)
+        summed = jnp.where(here, summed * f_cache + ss_ref[0, j] * f_span, summed)
+        totals = jnp.where(here, totals * f_cache + sl_ref[0, j] * f_span, totals)
+        highest = jnp.where(here, peak, highest)
+        if normalize:
+            summed = summed / jnp.where(totals > 0, totals, 1.0)
+        o_ref[0, h] = summed.astype(o_ref.dtype)
+        st_ref[0, h, :, 0:1] = highest
+        st_ref[0, h, :, 1:2] = totals
 
 
 def pair_partials(kernel, scalars, q_spec_index, operands, in_specs, req_local, heads, rows):
     grid_spec = pltpu.PrefetchScalarGridSpec(
         num_scalar_prefetch=len(scalars),
-        grid=(req_local, heads),
+        grid=(req_local,),
         in_specs=in_specs,
         out_specs=[
-            pl.BlockSpec((1, 1, rows, HEAD_DIM), lambda r, h, *_: (r, h, 0, 0)),
-            pl.BlockSpec((1, 1, rows, 1), lambda r, h, *_: (r, h, 0, 0)),
-            pl.BlockSpec((1, 1, rows, 1), lambda r, h, *_: (r, h, 0, 0)),
+            pl.BlockSpec((1, heads, rows, HEAD_DIM), lambda r, *_: (r, 0, 0, 0)),
+            pl.BlockSpec((1, heads, rows, 1), lambda r, *_: (r, 0, 0, 0)),
+            pl.BlockSpec((1, heads, rows, 1), lambda r, *_: (r, 0, 0, 0)),
         ],
     )
     shape = (req_local, heads, rows)
@@ -407,21 +478,23 @@
     span_total = 2 * span_local
     slot_local = cache_keys.shape[1]
     weights = (w_query, w_key, w_value)
+    other = jnp.concatenate(
+        [jnp.where(first, w[:, half:], w[:, :half]) for w in weights], axis=1
+    )
+    got = swap_seq(other)
     mine = jnp.concatenate(
-        [lax.dynamic_slice_in_dim(w, seq_index * half, half, axis=1) for w in weights], axis=1
-    )
-    other = jnp.concatenate(
-        [lax.dynamic_slice_in_dim(w, (1 - seq_index) * half, half, axis=1) for w in weights], axis=1
-    )
-    got = swap_seq(other)
-    pair_rows = jnp.where(first, jnp.concatenate([mine, got], 0), jnp.concatenate([got, mine], 0))
-    w_all = lax.all_gather(pair_rows, "req", axis=0, tiled=True)
+        [jnp.where(first, w[:, :half], w[:, half:]) for w in weights], axis=1
+    )
+    w_all = lax.all_gather(jnp.concatenate([mine, got], 0), "req", axis=0, tiled=True)
     tokens_other = swap_seq(tokens)
     tokens_all = jnp.where(
         first,
         jnp.concatenate([tokens, tokens_other], axis=1),
         jnp.concatenate([tokens_other, tokens], axis=1),
     )
+    row_block = w_query.shape[0]
+    blocks = tokens_all.reshape(req_local, span_total, model_width // (2 * row_block), 2, row_block)
+    tokens_all = jnp.where(first, blocks, blocks[:, :, :, ::-1, :]).reshape(tokens_all.shape)
     token_rows = tokens_all.reshape(req_local * span_total, model_width)
     proj = jnp.dot(token_rows, w_all, preferred_element_type=jnp.float32)
     q_proj = proj[:, :half]
@@ -446,58 +519,87 @@
         first, jnp.concatenate([q_half, q_other], -1), jnp.concatenate([q_other, q_half], -1)
     )
     seq_arr = jnp.reshape(seq_index, (1,)).astype(jnp.int32)
-    head_block = lambda r, h, *_: (r, 0, h)
-    cache_part = pair_partials(
-        pair_cache_kernel,
-        (cache_len, window_len, seq_arr),
-        None,
-        (q_full, cache_keys, cache_values),
-        [
-            pl.BlockSpec((1, span_total, HEAD_DIM), head_block),
-            pl.BlockSpec((1, slot_local, HEAD_DIM), head_block),
-            pl.BlockSpec((1, slot_local, HEAD_DIM), head_block),
-        ],
-        req_local,
-        heads_local,
-        span_total,
-    )
-    sink_block = lambda r, h, len_ref, win_ref, pos_ref, seq_ref: (r, 0, h + seq_ref[0] * heads_half)
+    head_block = lambda r, *_: (r, 0, 0)
+    sink_block = lambda r, len_ref, win_ref, pos_ref, seq_ref: (r, 0, seq_ref[0])
     span_part = pair_partials(
         pair_span_kernel,
         (cache_len, window_len, sink_pos.reshape(-1), seq_arr),
         None,
         (q_half, k_half, v_half, sink_keys, sink_values),
         [
-            pl.BlockSpec((1, span_total, HEAD_DIM), head_block),
-            pl.BlockSpec((1, span_total, HEAD_DIM), head_block),
-            pl.BlockSpec((1, span_total, HEAD_DIM), head_block),
-            pl.BlockSpec((1, SINKS, HEAD_DIM), sink_block),
-            pl.BlockSpec((1, SINKS, HEAD_DIM), sink_block),
+            pl.BlockSpec((1, span_total, half), head_block),
+            pl.BlockSpec((1, span_total, half), head_block),
+            pl.BlockSpec((1, span_total, half), head_block),
+            pl.BlockSpec((1, SINKS, half), sink_block),
+            pl.BlockSpec((1, SINKS, half), sink_block),
         ],
         req_local,
         heads_half,
         span_total,
     )
-    empty = (
-        jnp.zeros_like(cache_part[0]),
-        jnp.full_like(cache_part[1], lowest),
-        jnp.zeros_like(cache_part[2]),
-    )
-    span_wide = tuple(
-        lax.dynamic_update_slice_in_dim(e, p, seq_index * heads_half, axis=1)
-        for e, p in zip(empty, span_part)
-    )
-    merged = merge_parts(cache_part, span_wide)
-    own_rows = tuple(
-        lax.dynamic_slice_in_dim(x, seq_index * span_local, span_local, axis=2) for x in merged
-    )
-    far_rows = tuple(
-        lax.dynamic_slice_in_dim(x, (1 - seq_index) * span_local, span_local, axis=2)
-        for x in merged
-    )
-    got_sum = swap_seq(far_rows[0])
-    got_stats = swap_seq(jnp.concatenate([far_rows[1], far_rows[2]], axis=-1))
-    total_sum, _, total = merge_parts(own_rows, (got_sum, got_stats[..., 0:1], got_stats[..., 1:2]))
+
+    def rows_of(x, owner):
+        return lax.dynamic_slice_in_dim(x, owner * span_local, span_local, axis=2)
+
+    def cache_rows(owner, normalize):
+        first_row = jnp.reshape(owner * span_local, (1,)).astype(jnp.int32)
+        q_block = lambda r, len_ref, win_ref, seq_ref, first_ref, owner_ref: (r, owner_ref[0], 0)
+        span_block = lambda r, len_ref, win_ref, seq_ref, first_ref, owner_ref: (
+            r,
+            0,
+            owner_ref[0],
+            0,
+        )
+        grid_spec = pltpu.PrefetchScalarGridSpec(
+            num_scalar_prefetch=5,
+            grid=(req_local,),
+            in_specs=[
+                pl.BlockSpec((1, span_local, half), q_block),
+                pl.BlockSpec((1, span_local, half), q_block),
+                pl.BlockSpec((1, slot_local, local_cols), head_block),
+                pl.BlockSpec((1, slot_local, local_cols), head_block),
+                pl.BlockSpec((1, heads_half, span_local, HEAD_DIM), span_block),
+                pl.BlockSpec((1, heads_half, span_local, 1), span_block),
+                pl.BlockSpec((1, heads_half, span_local, 1), span_block),
+            ],
+            out_specs=[
+                pl.BlockSpec((1, heads_local, span_local, HEAD_DIM), lambda r, *_: (r, 0, 0, 0)),
+                pl.BlockSpec((1, heads_local, span_local, 2), lambda r, *_: (r, 0, 0, 0)),
+            ],
+        )
+        shape = (req_local, heads_local, span_local)
+        return pl.pallas_call(
+            functools.partial(
+                merged_cache_kernel, scaling=HEAD_DIM ** (-0.5), normalize=normalize
+            ),
+            grid_spec=grid_spec,
+            out_shape=[
+                jax.ShapeDtypeStruct(
+                    shape + (HEAD_DIM,), jnp.bfloat16 if normalize else jnp.float32
+                ),
+                jax.ShapeDtypeStruct(shape + (2,), jnp.float32),
+            ],
+        )(
+            cache_len,
+            window_len,
+            seq_arr,
+            first_row,
+            jnp.reshape(owner, (1,)).astype(jnp.int32),
+            q_half,
+            q_other,
+            cache_keys,
+            cache_values,
+            *span_part,
+        )
+
+    far_norm, far_stats = cache_rows(1 - seq_index, True)
+    got_norm = swap_seq(far_norm)
+    got_stats = swap_seq(far_stats)
+    own_sum, own_stats = cache_rows(seq_index, False)
+    own_rows = (own_sum, own_stats[..., 0:1], own_stats[..., 1:2])
+    got_total = got_stats[..., 1:2]
+    got_sum = got_norm.astype(jnp.float32) * got_total
+    total_sum, _, total = merge_parts(own_rows, (got_sum, got_stats[..., 0:1], got_total))
     own_offsets = seq_index * span_local + jnp.arange(span_local, dtype=jnp.int32)
     live_rows = (own_offsets[None, :] < span_len[:, None])[:, None, :, None]
     safe_total = jnp.where(live_rows, total, 1.0)

time: 170 us -> 149 us (0.88)
  waiting for transfers between devices: 93.4 us -> 50.7 us
  local copies, waits for them, and re-layouts: 10.6 us -> 27 us
  other arithmetic: 15.9 us -> 19.6 us
    all_gather x1, waiting for transfers between devices: 38.4 us -> 12 us  [on_device_pair(): lax.all_gather(jnp.concatenate([mine, got], 0), 'req', axis=0, tiled=True)]
    pallas_call x0 -> x2, Pallas kernels: none -> 17.7 us  [cache_rows(): pl.pallas_call(functools.partial(merged_cache_kernel, scaling=HEAD_DIM **...]
    ppermute x6, waiting for transfers between devices: 52.7 us -> 35.4 us  [swap_seq(): return lax.ppermute(x, 'seq', [(0, 1), (1, 0)])]
    pallas_call x2 -> x1, Pallas kernels: 20.4 us -> 4.32 us  [pair_partials(): pl.pallas_call(functools.partial(kernel, scaling=HEAD_DIM ** (-0.5)), gri...]
    rev x0 -> x1, local copies, waits for them, and re-layouts: none -> 15.3 us  [on_device_pair(): blocks[:, :, :, ::-1, :]]
    another operation x0 -> x1, local copies, waits for them, and re-layouts: none -> 4.49 us  [on_device_pair(): token_rows = tokens_all.reshape(req_local * span_total, model_width)]
    select_n x1, other arithmetic: 2.34 us -> 5.75 us  [on_device_pair(): jnp.where(first, jnp.concatenate([tokens, tokens_other], axis=1), jnp.con...]
    dynamic_slice x5 -> x0, local copies, waits for them, and re-layouts: 3.15 us -> none  [the longest x2 2.21 us: on_device_pair(): lax.dynamic_slice_in_dim(w, seq_index * half, half, axis=1)]
  transfers between devices with their start and end apart: 9 -> 9, of which waited for: 7 -> 8; matrix products, arithmetic and copies ran while one was open for 5% -> 25% of each run, Pallas kernels for 3% -> 9%
where the time goes in v5:
time: 149 us
  waiting for transfers between devices  50.7 us (34%)
  local copies, waits for them, and re-layouts  27 us (18%)
  Pallas kernels  22 us (15%)
  other arithmetic  19.6 us (13%)
  between operations  13.6 us (9%)
  starting transfers between devices  11.5 us (8%)
  matrix products  4.3 us (3%)
    ppermute x6, waiting for transfers between devices, swap_seq(): return lax.ppermute(x, 'seq', [(0, 1), (1, 0)])  35.4 us
    pallas_call x2, Pallas kernels, cache_rows(): pl.pallas_call(functools.partial(merged_cache_kernel, scaling=HEAD_DIM **...  17.7 us
    rev x1, local copies, waits for them, and re-layouts, on_device_pair(): blocks[:, :, :, ::-1, :]  15.3 us
    all_gather x1, waiting for transfers between devices, on_device_pair(): lax.all_gather(jnp.concatenate([mine, got], 0), 'req', axis=0, tiled=True)  12 us
    ppermute x6, starting transfers between devices, swap_seq(): return lax.ppermute(x, 'seq', [(0, 1), (1, 0)])  9.9 us
    select_n x1, other arithmetic, on_device_pair(): jnp.where(first, jnp.concatenate([tokens, tokens_other], axis=1), jnp.con...  5.75 us
    another operation x1, local copies, waits for them, and re-layouts, on_device_pair(): token_rows = tokens_all.reshape(req_local * span_total, model_width)  4.49 us
    pallas_call x1, Pallas kernels, pair_partials(): pl.pallas_call(functools.partial(kernel, scaling=HEAD_DIM ** (-0.5)), gri...  4.32 us
  transfers between devices with their start and end apart: 9, of which 8 were waited for; matrix products, arithmetic and copies ran while one was open for 25% of the time, Pallas kernels for 9%

profile of v5, /device:TPU:0, one launch (start us, length us, event | category | flops | bytes accessed | tf_op | source)
XLA Modules:
  0.0 148.7 jit_solution(10250039149282869918)
XLA Ops:
  6.5 1.0 broadcast_select_fusion.7
  7.5 1.2 broadcast_select_fusion.5
  8.8 3.0 %collective-permute-start.1 = (bf16[256,768]{1,0:T(8,128)(2,1)S(1)}, bf16[256,768]{1,0:T(8,128)(2,1)S(1)}, u32[]{:S(2)}, u32[]{:S(2)}) collective-permute-start(bf16[256,768]{1,0:T(8,128)(2,1)S(1)} %pad_maximum_fusion.1), channel_id=1, source_target_pairs={{0,4},{4,0},{1,5},{5,1},{2,6},{6,2},{3,7},{7,3},{8,12},{12,8},{9,1... | collective-permute-start | bytes 1179656 | tf_op jit(solution)/shard_map/ppermute | solution.py:452
  11.8 9.1 %collective-permute-done.1 = bf16[256,768]{1,0:T(8,128)(2,1)S(1)} collective-permute-done((bf16[256,768]{1,0:T(8,128)(2,1)S(1)}, bf16[256,768]{1,0:T(8,128)(2,1)S(1)}, u32[]{:S(2)}, u32[]{:S(2)}) %collective-permute-start.1) | collective-permute-done | bytes 393248 | tf_op jit(solution)/shard_map/ppermute | solution.py:452
  20.9 0.9 pad_maximum_fusion
  21.9 1.8 %collective-permute-start = (bf16[2,128,2048]{2,1,0:T(8,128)(2,1)S(1)}, bf16[2,128,2048]{2,1,0:T(8,128)(2,1)S(1)}, u32[]{:S(2)}, u32[]{:S(2)}) collective-permute-start(bf16[2,128,2048]{2,1,0:T(8,128)(2,1)S(1)} %copy-done.2), channel_id=1, source_target_pairs={{0,4},{4,0},{1,5},{5,1},{2,6},{6,2},{3,7},{7,3},{8,12},{12,8},{9,1... | collective-permute-start | bytes 3145736 | tf_op jit(solution)/shard_map/ppermute | solution.py:452
  23.7 0.8 concatenate.29
  24.5 21.8 %collective-permute-done = bf16[2,128,2048]{2,1,0:T(8,128)(2,1)S(1)} collective-permute-done((bf16[2,128,2048]{2,1,0:T(8,128)(2,1)S(1)}, bf16[2,128,2048]{2,1,0:T(8,128)(2,1)S(1)}, u32[]{:S(2)}, u32[]{:S(2)}) %collective-permute-start) | collective-permute-done | bytes 1048608 | tf_op jit(solution)/shard_map/ppermute | solution.py:452
  46.3 1.6 %concatenate.30 = bf16[2,128,4,2,256]{4,3,2,1,0:T(2,128)(2,1)} reshape(bf16[2,128,2048]{2,1,0:T(8,128)(2,1)S(1)} %collective-permute-done) | data formatting | bytes 2097152 | tf_op jit(solution)/shard_map/concatenate | solution.py:492
  47.9 5.7 %broadcast_select_fusion.1 = bf16[2,256,4,2,256]{4,3,2,1,0:T(2,128)(2,1)S(1)} fusion(pred[]{:T(512)S(6)} %eq.3, bf16[2,128,4,2,256]{4,3,2,1,0:T(2,128)(2,1)} %concatenate.30, bf16[2,128,4,2,256]{4,3,2,1,0:T(2,128)(2,1)S(1)} %concatenate.29), kind=kLoop, calls=%fused_computation.1 | loop fusion | flops 3145728 | bytes 4194305 | tf_op jit(solution)/shard_map/jit(_where)/select_n | solution.py:490
  53.6 15.3 %rev.3 = bf16[2,256,4,2,256]{4,3,2,1,0:T(2,128)(2,1)} reverse(bf16[2,256,4,2,256]{4,3,2,1,0:T(2,128)(2,1)S(1)} %broadcast_select_fusion.1), dimensions={3} | reverse | bytes 4194304 | tf_op jit(solution)/shard_map/rev | solution.py:497
  68.9 1.6 %broadcast_select_fusion = bf16[2,256,1,8,256]{4,3,2,1,0:T(8,128)(2,1)} fusion(bf16[2,256,1,8,256]{4,3,2,1,0:T(8,128)(2,1)S(1)} %bitcast.20, bf16[2,256,1,8,256]{4,3,2,1,0:T(8,128)(2,1)} %bitcast.22, pred[]{:T(512)S(6)} %eq.3), kind=kLoop, calls=%fused_computation | loop fusion | flops 1048576 | bytes 6291457 | tf_op jit(solution)/shard_map/jit(_where)/select_n | solution.py:497
  70.5 4.5 %reshape_reshape.3 = bf16[512,2048]{1,0:T(8,128)(2,1)} reshape(bf16[2,256,4,2,256]{4,3,2,1,0:T(2,128)(2,1)} %bitcast.21) | data formatting | bytes 4194304 | tf_op jit(solution)/shard_map/reshape;reshape | solution.py:498
  75.0 12.0 %all-gather.2.cloned.1.call-done = bf16[2048,768]{1,0:T(8,128)(2,1)} async-done(((bf16[512,768]{1,0:T(8,128)(2,1)}), bf16[2048,768]{1,0:T(8,128)(2,1)}) %all-gather.2.cloned.1.call-update) | async-done | bytes 3145744 | tf_op jit(solution)/shard_map/all_gather | solution.py:488
  87.0 4.3 %fusion.10 = f32[512,768]{1,0:T(8,128)S(1)} fusion(bf16[512,2048]{1,0:T(8,128)(2,1)} %reshape_reshape.3, bf16[2048,768]{1,0:T(8,128)(2,1)} %all-gather.2.cloned.1.call-done), kind=kOutput, calls=%fused_computation.45 | convolution fusion | flops 1610612736 | bytes 6815744 | tf_op jit(solution)/shard_map/dot_general | solution.py:499
  91.4 0.2 multiply_reduce_fusion.1
  91.8 1.1 collective-permute-done.2
  92.8 1.5 %collective-permute-start.3 = (f32[2,512]{1,0:T(2,128)S(1)}, f32[2,512]{1,0:T(2,128)S(1)}, u32[]{:S(2)}, u32[]{:S(2)}) collective-permute-start(f32[2,512]{1,0:T(2,128)S(1)} %fusion.9), channel_id=1, source_target_pairs={{0,2},{1,3},{2,0},{3,1},{4,6},{5,7},{6,4},{7,5},{8,10},{9,11},{10,... | collective-permute-start | bytes 12296 | tf_op jit(solution)/shard_map/ppermute | solution.py:222
  94.4 2.1 %collective-permute-done.3 = f32[2,512]{1,0:T(2,128)S(1)} collective-permute-done((f32[2,512]{1,0:T(2,128)S(1)}, f32[2,512]{1,0:T(2,128)S(1)}, u32[]{:S(2)}, u32[]{:S(2)}) %collective-permute-start.3) | collective-permute-done | bytes 4128 | tf_op jit(solution)/shard_map/ppermute | solution.py:222
  96.5 1.5 %collective-permute-start.4 = (f32[2,512]{1,0:T(2,128)S(1)}, f32[2,512]{1,0:T(2,128)S(1)}, u32[]{:S(2)}, u32[]{:S(2)}) collective-permute-start(f32[2,512]{1,0:T(2,128)S(1)} %fusion.13), channel_id=1, source_target_pairs={{0,4},{4,0},{1,5},{5,1},{2,6},{6,2},{3,7},{7,3},{8,12},{12,8},{9,1... | collective-permute-start | bytes 12296 | tf_op jit(solution)/shard_map/ppermute | solution.py:452
  98.1 1.7 %multiply_cosine_fusion = (f32[512,64]{1,0:T(8,128)S(1)}, f32[512,64]{1,0:T(8,128)}) fusion(f32[64]{0:T(128)S(1)} %negate_power_fusion, f32[512]{0:T(512)S(1)} %bitcast.31), kind=kLoop, calls=%fused_computation.21 | loop fusion | flops 32768 | bytes 264448 | tf_op jit(solution)/shard_map/cos | solution.py:26
  99.8 0.1 dynamic_slice.7
  99.9 0.1 dynamic_slice.6
  100.0 0.2 collective-permute-done.4
  100.2 0.2 multiply_multiply_fusion
  100.4 0.3 reshape.159
  100.7 0.3 reshape.157
  101.0 2.5 %subtract_convert_fusion = (bf16[512,2,64]{2,1,0:T(2,128)(2,1)S(1)}, bf16[512,2,64]{2,1,0:T(2,128)(2,1)S(1)}, bf16[512,2,64]{2,1,0:T(2,128)(2,1)S(1)}, bf16[512,2,64]{2,1,0:T(2,128)(2,1)S(1)}) fusion(f32[512,2,128]{2,1,0:T(2,128)S(1)} %reshape.159, f32[512,64]{1,0:T(8,128)} %get-tuple-element.42, f32[512,64]{1,0:T(8,128)S(1)} %get-tuple-element.41, ...), kind=kLoop, calls=%fused_computation.11 | loop fusion | flops 1048576 | bytes 1835008 | tf_op jit(solution)/shard_map/convert.1
  103.5 0.7 pad_maximum_fusion.2
  104.2 0.2 convert_element_type.36.q_ref.qa_ref
  104.4 1.5 %collective-permute-start.5 = (bf16[2,256,256]{2,1,0:T(8,128)(2,1)S(1)}, bf16[2,256,256]{2,1,0:T(8,128)(2,1)S(1)}, u32[]{:S(2)}, u32[]{:S(2)}) collective-permute-start(bf16[2,256,256]{2,1,0:T(8,128)(2,1)S(1)} %convert_element_type.36.q_ref.qa_ref), channel_id=1, source_target_pairs={{0,4},{4,0},{1,5},{5,1},{2,6},{6,2},{3,7},{7,3},{8,12},{12,8},{9,1... | collective-permute-start | bytes 786440 | tf_op jit(solution)/shard_map/ppermute | solution.py:452
  105.9 0.6 reshape.158.sink_pos_ref
  106.5 0.8 slice.152
  107.3 0.7 pad_maximum_fusion.3
  108.0 0.9 convert_element_type.37.nk_ref
  108.9 4.3 %shard_map.136 = (f32[2,2,256,128]{3,2,1,0:T(8,128)}, f32[2,2,256,1]{3,2,1,0:T(8,128)}, f32[2,2,256,1]{3,2,1,0:T(8,128)}) custom-call(s32[2]{0:T(128)} %len_ref.5, s32[2]{0:T(128)} %win_ref.5, s32[8]{0:T(128)} %reshape.158.sink_pos_ref, s32[1]{0:T(128)} %bitcast.seq_ref.owner_ref, bf16[2,256,256]{2,1,0:T(8,128)(2,1)} %copy-done, ...), custom_call_target="tpu_custom_call" | custom-call | tf_op jit(solution)/shard_map/pallas_call | solution.py:431
  113.2 0.7 copy-done.1
  113.9 9.0 %shard_map.138 = (bf16[2,4,128,128]{3,2,1,0:T(8,128)(2,1)}, f32[2,4,128,2]{3,2,1,0:T(8,128)}) custom-call(s32[2]{0:T(128)} %len_ref.5, s32[2]{0:T(128)} %win_ref.5, s32[1]{0:T(128)} %bitcast.seq_ref.owner_ref, s32[1]{0:T(128)} %bitcast.7.first_ref, s32[1]{0:T(128)} %bitcast.8.owner_ref, bf16[2,256,256]{2,1,0:T(8,128)(2,1)} %copy-done, ...), custom_call_target="tpu_custom_call" | custom-call | tf_op jit(solution)/shard_map/pallas_call | solution.py:571
  122.9 0.6 collective-permute-start.6
  123.4 1.5 collective-permute-start.7
  124.9 0.1 broadcast_compare_fusion
  125.0 8.7 %shard_map.137 = (f32[2,4,128,128]{3,2,1,0:T(8,128)}, f32[2,4,128,2]{3,2,1,0:T(8,128)}) custom-call(s32[2]{0:T(128)} %len_ref.5, s32[2]{0:T(128)} %win_ref.5, s32[1]{0:T(128)} %bitcast.seq_ref.owner_ref, s32[1]{0:T(128)} %bitcast.1.first_ref, s32[1]{0:T(128)} %bitcast.seq_ref.owner_ref, bf16[2,256,256]{2,1,0:T(8,128)(2,1)} %copy-done, ...), custom_call_target="tpu_custom_call" | custom-call | tf_op jit(solution)/shard_map/pallas_call | solution.py:571
  133.7 3.6 %collective-permute-done.6 = f32[2,4,128,2]{3,2,1,0:T(8,128)S(1)} collective-permute-done((f32[2,4,128,2]{3,2,1,0:T(8,128)}, f32[2,4,128,2]{3,2,1,0:T(8,128)S(1)}, u32[]{:S(2)}, u32[]{:S(2)}) %collective-permute-start.6) | collective-permute-done | bytes 8224 | tf_op jit(solution)/shard_map/ppermute | solution.py:452
  137.3 2.1 %fusion.4 = (f32[2,4,128]{2,1,0:T(4,128)S(1)}, f32[2,4,128]{2,1,0:T(4,128)S(1)}, f32[2,4,128]{2,1,0:T(4,128)S(1)}, f32[2,4,128]{2,1,0:T(4,128)S(1)}) fusion(f32[2,4,128,2]{3,2,1,0:T(8,128)S(1)} %collective-permute-done.6, f32[2,4,128,2]{3,2,1,0:T(8,128)} %get-tuple-element.16, pred[2,128]{1,0:T(4,128)(4,1)S(1)} %broadcast_compare_fusion), kind=kLoop, calls=%fused_computation.32 | loop fusion | flops 7168 | bytes 33024 | tf_op jit(solution)/shard_map/exp | solution.py:446
  139.4 0.7 collective-permute-done.7
  140.1 0.7 fusion.2
  140.8 0.2 copy.15
  141.0 0.9 copy.16
  (31 shorter events, 0.3 us)
Async XLA Ops:
  6.5 80.5 %all-gather.2.cloned.1.call-start = ((), (), s32[]{:S(2)}) async-start(), calls=%async_computation | async-start | bytes 3932160 | tf_op jit(solution)/shard_map/all_gather | solution.py:488
  7.5 14.4 %copy-start.2 = (bf16[2,128,2048]{2,1,0:T(8,128)(2,1)S(1)}, bf16[2,128,2048]{2,1,0:T(8,128)(2,1)}, u32[]{:S(2)}) copy-start(bf16[2,128,2048]{2,1,0:T(8,128)(2,1)} %param.14) | copy-start | bytes 3145732
  8.8 12.1 %collective-permute-start.1 = (bf16[256,768]{1,0:T(8,128)(2,1)S(1)}, bf16[256,768]{1,0:T(8,128)(2,1)S(1)}, u32[]{:S(2)}, u32[]{:S(2)}) collective-permute-start(bf16[256,768]{1,0:T(8,128)(2,1)S(1)} %pad_maximum_fusion.1), channel_id=1, source_target_pairs={{0,4},{4,0},{1,5},{5,1},{2,6},{6,2},{3,7},{7,3},{8,12},{12,8},{9,1... | collective-permute-start | bytes 1179656 | tf_op jit(solution)/shard_map/ppermute | solution.py:452
  21.9 24.4 %collective-permute-start = (bf16[2,128,2048]{2,1,0:T(8,128)(2,1)S(1)}, bf16[2,128,2048]{2,1,0:T(8,128)(2,1)S(1)}, u32[]{:S(2)}, u32[]{:S(2)}) collective-permute-start(bf16[2,128,2048]{2,1,0:T(8,128)(2,1)S(1)} %copy-done.2), channel_id=1, source_target_pairs={{0,4},{4,0},{1,5},{5,1},{2,6},{6,2},{3,7},{7,3},{8,12},{12,8},{9,1... | collective-permute-start | bytes 3145736 | tf_op jit(solution)/shard_map/ppermute | solution.py:452
  75.0 16.7 %copy-start.4 = (s32[2]{0:T(128)S(1)}, s32[2]{0:T(128)}, u32[]{:S(2)}) copy-start(s32[2]{0:T(128)} %len_ref.5) | copy-start | bytes 28
  75.0 24.8 %copy-start.5 = (f32[512]{0:T(512)S(1)}, f32[512]{0:T(512)}, u32[]{:S(2)}) copy-start(f32[512]{0:T(512)} %param.19) | copy-start | bytes 6148
  75.0 24.9 %copy-start.6 = (f32[512]{0:T(512)S(1)}, f32[512]{0:T(512)}, u32[]{:S(2)}) copy-start(f32[512]{0:T(512)} %param.18) | copy-start | bytes 6148
  91.6 1.2 collective-permute-start.2
  92.8 3.7 %collective-permute-start.3 = (f32[2,512]{1,0:T(2,128)S(1)}, f32[2,512]{1,0:T(2,128)S(1)}, u32[]{:S(2)}, u32[]{:S(2)}) collective-permute-start(f32[2,512]{1,0:T(2,128)S(1)} %fusion.9), channel_id=1, source_target_pairs={{0,2},{1,3},{2,0},{3,1},{4,6},{5,7},{6,4},{7,5},{8,10},{9,11},{10,... | collective-permute-start | bytes 12296 | tf_op jit(solution)/shard_map/ppermute | solution.py:222
  96.5 3.7 %collective-permute-start.4 = (f32[2,512]{1,0:T(2,128)S(1)}, f32[2,512]{1,0:T(2,128)S(1)}, u32[]{:S(2)}, u32[]{:S(2)}) collective-permute-start(f32[2,512]{1,0:T(2,128)S(1)} %fusion.13), channel_id=1, source_target_pairs={{0,4},{4,0},{1,5},{5,1},{2,6},{6,2},{3,7},{7,3},{8,12},{12,8},{9,1... | collective-permute-start | bytes 12296 | tf_op jit(solution)/shard_map/ppermute | solution.py:452
  101.0 4.9 %copy-start.7 = (s32[2,4]{1,0:T(2,128)S(1)}, s32[2,4]{1,0:T(2,128)}, u32[]{:S(2)}) copy-start(s32[2,4]{1,0:T(2,128)} %param.24) | copy-start | bytes 100
  104.4 4.5 %copy-start = (bf16[2,256,256]{2,1,0:T(8,128)(2,1)}, bf16[2,256,256]{2,1,0:T(8,128)(2,1)S(1)}, u32[]{:S(2)}) copy-start(bf16[2,256,256]{2,1,0:T(8,128)(2,1)S(1)} %convert_element_type.36.q_ref.qa_ref) | copy-start | bytes 786436
  104.4 8.8 %collective-permute-start.5 = (bf16[2,256,256]{2,1,0:T(8,128)(2,1)S(1)}, bf16[2,256,256]{2,1,0:T(8,128)(2,1)S(1)}, u32[]{:S(2)}, u32[]{:S(2)}) collective-permute-start(bf16[2,256,256]{2,1,0:T(8,128)(2,1)S(1)} %convert_element_type.36.q_ref.qa_ref), channel_id=1, source_target_pairs={{0,4},{4,0},{1,5},{5,1},{2,6},{6,2},{3,7},{7,3},{8,12},{12,8},{9,1... | collective-permute-start | bytes 786440 | tf_op jit(solution)/shard_map/ppermute | solution.py:452
  113.2 0.7 copy-start.1
  113.9 11.0 %copy-start.8 = (s32[2]{0:T(128)S(1)}, s32[2]{0:T(128)}, u32[]{:S(2)}) copy-start(s32[2]{0:T(128)} %param.26) | copy-start | bytes 28
  122.9 14.4 %collective-permute-start.6 = (f32[2,4,128,2]{3,2,1,0:T(8,128)}, f32[2,4,128,2]{3,2,1,0:T(8,128)S(1)}, u32[]{:S(2)}, u32[]{:S(2)}) collective-permute-start(f32[2,4,128,2]{3,2,1,0:T(8,128)} %get-tuple-element.17), channel_id=1, source_target_pairs={{0,4},{4,0},{1,5},{5,1},{2,6},{6,2},{3,7},{7,3},{8,12},{12,8},{9,1... | collective-permute-start | bytes 24584 | tf_op jit(solution)/shard_map/ppermute | solution.py:452
  123.4 16.7 %collective-permute-start.7 = (bf16[2,4,128,128]{3,2,1,0:T(8,128)(2,1)}, bf16[2,4,128,128]{3,2,1,0:T(8,128)(2,1)S(1)}, u32[]{:S(2)}, u32[]{:S(2)}) collective-permute-start(bf16[2,4,128,128]{3,2,1,0:T(8,128)(2,1)} %get-tuple-element.18), channel_id=1, source_target_pairs={{0,4},{4,0},{1,5},{5,1},{2,6},{6,2},{3,7},{7,3},{8,12},{12,8},{9,1... | collective-permute-start | bytes 786440 | tf_op jit(solution)/shard_map/ppermute | solution.py:452
  133.7 6.4 %copy-start.3 = (f32[2,4,128,128]{3,2,1,0:T(8,128)S(1)}, f32[2,4,128,128]{3,2,1,0:T(8,128)}, u32[]{:S(2)}) copy-start(f32[2,4,128,128]{3,2,1,0:T(8,128)} %get-tuple-element.15) | copy-start | bytes 1572868
Sparse Core Ops, SparseCore 0:
  22.0 64.9 all-gather.1

commit v6 on v5

--- a/solution.py
+++ b/solution.py
@@ -411,7 +411,7 @@
         highest = jnp.where(here, peak, highest)
         if normalize:
             summed = summed / jnp.where(totals > 0, totals, 1.0)
-        o_ref[0, h] = summed.astype(o_ref.dtype)
+        o_ref[0, :, cols] = summed.astype(o_ref.dtype)
         st_ref[0, h, :, 0:1] = highest
         st_ref[0, h, :, 1:2] = totals
 
@@ -563,7 +563,7 @@
                 pl.BlockSpec((1, heads_half, span_local, 1), span_block),
             ],
             out_specs=[
-                pl.BlockSpec((1, heads_local, span_local, HEAD_DIM), lambda r, *_: (r, 0, 0, 0)),
+                pl.BlockSpec((1, span_local, local_cols), lambda r, *_: (r, 0, 0)),
                 pl.BlockSpec((1, heads_local, span_local, 2), lambda r, *_: (r, 0, 0, 0)),
             ],
         )
@@ -575,7 +575,8 @@
             grid_spec=grid_spec,
             out_shape=[
                 jax.ShapeDtypeStruct(
-                    shape + (HEAD_DIM,), jnp.bfloat16 if normalize else jnp.float32
+                    (req_local, span_local, local_cols),
+                    jnp.bfloat16 if normalize else jnp.float32,
                 ),
                 jax.ShapeDtypeStruct(shape + (2,), jnp.float32),
             ],
@@ -596,17 +597,25 @@
     got_norm = swap_seq(far_norm)
     got_stats = swap_seq(far_stats)
     own_sum, own_stats = cache_rows(seq_index, False)
-    own_rows = (own_sum, own_stats[..., 0:1], own_stats[..., 1:2])
-    got_total = got_stats[..., 1:2]
-    got_sum = got_norm.astype(jnp.float32) * got_total
-    total_sum, _, total = merge_parts(own_rows, (got_sum, got_stats[..., 0:1], got_total))
+    own_high, own_total = own_stats[..., 0], own_stats[..., 1]
+    got_high, got_total = got_stats[..., 0], got_stats[..., 1]
+    peak = jnp.maximum(own_high, got_high)
+    own_factor = jnp.exp(own_high - peak)
+    got_factor = jnp.exp(got_high - peak) * got_total
+    total = own_total * own_factor + got_factor
+
+    def per_row(x):
+        return jnp.transpose(x, (0, 2, 1))[..., None]
+
+    heads_shape = (req_local, span_local, heads_local, HEAD_DIM)
+    total_sum = own_sum.reshape(heads_shape) * per_row(own_factor) + got_norm.reshape(
+        heads_shape
+    ).astype(jnp.float32) * per_row(got_factor)
     own_offsets = seq_index * span_local + jnp.arange(span_local, dtype=jnp.int32)
-    live_rows = (own_offsets[None, :] < span_len[:, None])[:, None, :, None]
-    safe_total = jnp.where(live_rows, total, 1.0)
+    live_rows = (own_offsets[None, :] < span_len[:, None])[:, :, None, None]
+    safe_total = jnp.where(live_rows, per_row(total), 1.0)
     mixed = jnp.where(live_rows, total_sum / safe_total, 0.0)
-    return (
-        mixed.transpose(0, 2, 1, 3).reshape(req_local, span_local, local_cols).astype(jnp.bfloat16)
-    )
+    return mixed.reshape(req_local, span_local, local_cols).astype(jnp.bfloat16)
 
 
 def solution(mesh):

time: 149 us -> 148 us (level)
  local copies, waits for them, and re-layouts: 27 us -> 30.2 us
  waiting for transfers between devices: 50.7 us -> 48.2 us
  other arithmetic: 19.6 us -> 17.6 us
    slice x0 -> x2, local copies, waits for them, and re-layouts: none -> 2.22 us  [the longest x1 1.7 us: on_device_pair(): own_high, own_total = (own_stats[..., 0], own_stats[..., 1])]
    exp x1 -> x0, other arithmetic: 2.15 us -> none  [merge_parts(): f1 = jnp.exp(m1 - peak)]
    ppermute x2, waiting for transfers between devices: 3.19 us -> 1.51 us  [tp_sum(): x = x + lax.ppermute(x, 'tp', [(a, a ^ bit) for a in range(count)])]
  transfers between devices with their start and end apart: 9 -> 9, of which waited for: 8 -> 7; matrix products, arithmetic and copies ran while one was open for 25% -> 26% of each run, Pallas kernels for 9% -> 9%
where the time goes in v6:
time: 148 us
  waiting for transfers between devices  48.2 us (33%)
  local copies, waits for them, and re-layouts  30.2 us (20%)
  Pallas kernels  22.1 us (15%)
  other arithmetic  17.6 us (12%)
  between operations  13.7 us (9%)
  starting transfers between devices  11.6 us (8%)
  matrix products  4.3 us (3%)
    ppermute x6, waiting for transfers between devices, swap_seq(): return lax.ppermute(x, 'seq', [(0, 1), (1, 0)])  34.6 us
    pallas_call x2, Pallas kernels, cache_rows(): pl.pallas_call(functools.partial(merged_cache_kernel, scaling=HEAD_DIM **...  17.7 us
    rev x1, local copies, waits for them, and re-layouts, on_device_pair(): blocks[:, :, :, ::-1, :]  15.3 us
    all_gather x1, waiting for transfers between devices, on_device_pair(): lax.all_gather(jnp.concatenate([mine, got], 0), 'req', axis=0, tiled=True)  12.1 us
    ppermute x6, starting transfers between devices, swap_seq(): return lax.ppermute(x, 'seq', [(0, 1), (1, 0)])  9.96 us
    select_n x1, other arithmetic, on_device_pair(): jnp.where(first, jnp.concatenate([tokens, tokens_other], axis=1), jnp.con...  5.75 us
    another operation x1, local copies, waits for them, and re-layouts, on_device_pair(): token_rows = tokens_all.reshape(req_local * span_total, model_width)  4.48 us
    pallas_call x1, Pallas kernels, pair_partials(): pl.pallas_call(functools.partial(kernel, scaling=HEAD_DIM ** (-0.5)), gri...  4.34 us
  transfers between devices with their start and end apart: 9, of which 7 were waited for; matrix products, arithmetic and copies ran while one was open for 26% of the time, Pallas kernels for 9%

profile of v6, /device:TPU:0, one launch (start us, length us, event | category | flops | bytes accessed | tf_op | source)
XLA Modules:
  0.0 147.7 jit_solution(12095742892533312778)
XLA Ops:
  6.5 1.0 broadcast_select_fusion.7
  7.5 1.2 broadcast_select_fusion.5
  8.8 3.0 %collective-permute-start.1 = (bf16[256,768]{1,0:T(8,128)(2,1)S(1)}, bf16[256,768]{1,0:T(8,128)(2,1)S(1)}, u32[]{:S(2)}, u32[]{:S(2)}) collective-permute-start(bf16[256,768]{1,0:T(8,128)(2,1)S(1)} %pad_maximum_fusion.1), channel_id=1, source_target_pairs={{0,4},{4,0},{1,5},{5,1},{2,6},{6,2},{3,7},{7,3},{8,12},{12,8},{9,1... | collective-permute-start | bytes 1179656 | tf_op jit(solution)/shard_map/ppermute | solution.py:452
  11.8 9.1 %collective-permute-done.1 = bf16[256,768]{1,0:T(8,128)(2,1)S(1)} collective-permute-done((bf16[256,768]{1,0:T(8,128)(2,1)S(1)}, bf16[256,768]{1,0:T(8,128)(2,1)S(1)}, u32[]{:S(2)}, u32[]{:S(2)}) %collective-permute-start.1) | collective-permute-done | bytes 393248 | tf_op jit(solution)/shard_map/ppermute | solution.py:452
  20.9 1.0 pad_maximum_fusion
  21.9 1.8 %collective-permute-start = (bf16[2,128,2048]{2,1,0:T(8,128)(2,1)S(1)}, bf16[2,128,2048]{2,1,0:T(8,128)(2,1)S(1)}, u32[]{:S(2)}, u32[]{:S(2)}) collective-permute-start(bf16[2,128,2048]{2,1,0:T(8,128)(2,1)S(1)} %copy-done.2), channel_id=1, source_target_pairs={{0,4},{4,0},{1,5},{5,1},{2,6},{6,2},{3,7},{7,3},{8,12},{12,8},{9,1... | collective-permute-start | bytes 3145736 | tf_op jit(solution)/shard_map/ppermute | solution.py:452
  23.7 0.8 concatenate.29
  24.6 21.7 %collective-permute-done = bf16[2,128,2048]{2,1,0:T(8,128)(2,1)S(1)} collective-permute-done((bf16[2,128,2048]{2,1,0:T(8,128)(2,1)S(1)}, bf16[2,128,2048]{2,1,0:T(8,128)(2,1)S(1)}, u32[]{:S(2)}, u32[]{:S(2)}) %collective-permute-start) | collective-permute-done | bytes 1048608 | tf_op jit(solution)/shard_map/ppermute | solution.py:452
  46.3 1.6 %concatenate.30 = bf16[2,128,4,2,256]{4,3,2,1,0:T(2,128)(2,1)} reshape(bf16[2,128,2048]{2,1,0:T(8,128)(2,1)S(1)} %collective-permute-done) | data formatting | bytes 2097152 | tf_op jit(solution)/shard_map/concatenate | solution.py:492
  47.9 5.7 %broadcast_select_fusion.1 = bf16[2,256,4,2,256]{4,3,2,1,0:T(2,128)(2,1)S(1)} fusion(pred[]{:T(512)S(6)} %eq.3, bf16[2,128,4,2,256]{4,3,2,1,0:T(2,128)(2,1)} %concatenate.30, bf16[2,128,4,2,256]{4,3,2,1,0:T(2,128)(2,1)S(1)} %concatenate.29), kind=kLoop, calls=%fused_computation.1 | loop fusion | flops 3145728 | bytes 4194305 | tf_op jit(solution)/shard_map/jit(_where)/select_n | solution.py:490
  53.7 15.3 %rev.3 = bf16[2,256,4,2,256]{4,3,2,1,0:T(2,128)(2,1)} reverse(bf16[2,256,4,2,256]{4,3,2,1,0:T(2,128)(2,1)S(1)} %broadcast_select_fusion.1), dimensions={3} | reverse | bytes 4194304 | tf_op jit(solution)/shard_map/rev | solution.py:497
  68.9 1.6 %broadcast_select_fusion = bf16[2,256,1,8,256]{4,3,2,1,0:T(8,128)(2,1)} fusion(bf16[2,256,1,8,256]{4,3,2,1,0:T(8,128)(2,1)S(1)} %bitcast.23, bf16[2,256,1,8,256]{4,3,2,1,0:T(8,128)(2,1)} %bitcast.25, pred[]{:T(512)S(6)} %eq.3), kind=kLoop, calls=%fused_computation | loop fusion | flops 1048576 | bytes 6291457 | tf_op jit(solution)/shard_map/jit(_where)/select_n | solution.py:497
  70.5 4.5 %reshape_reshape.3 = bf16[512,2048]{1,0:T(8,128)(2,1)} reshape(bf16[2,256,4,2,256]{4,3,2,1,0:T(2,128)(2,1)} %bitcast.24) | data formatting | bytes 4194304 | tf_op jit(solution)/shard_map/reshape;reshape | solution.py:498
  75.0 12.1 %all-gather.2.cloned.1.call-done = bf16[2048,768]{1,0:T(8,128)(2,1)} async-done(((bf16[512,768]{1,0:T(8,128)(2,1)}), bf16[2048,768]{1,0:T(8,128)(2,1)}) %all-gather.2.cloned.1.call-update) | async-done | bytes 3145744 | tf_op jit(solution)/shard_map/all_gather | solution.py:488
  87.1 4.3 %fusion.10 = f32[512,768]{1,0:T(8,128)S(1)} fusion(bf16[512,2048]{1,0:T(8,128)(2,1)} %reshape_reshape.3, bf16[2048,768]{1,0:T(8,128)(2,1)} %all-gather.2.cloned.1.call-done), kind=kOutput, calls=%fused_computation.48 | convolution fusion | flops 1610612736 | bytes 6815744 | tf_op jit(solution)/shard_map/dot_general | solution.py:499
  91.4 0.2 multiply_reduce_fusion.1
  91.7 1.1 collective-permute-done.2
  92.9 1.5 %collective-permute-start.3 = (f32[2,512]{1,0:T(2,128)S(1)}, f32[2,512]{1,0:T(2,128)S(1)}, u32[]{:S(2)}, u32[]{:S(2)}) collective-permute-start(f32[2,512]{1,0:T(2,128)S(1)} %fusion.9), channel_id=1, source_target_pairs={{0,2},{1,3},{2,0},{3,1},{4,6},{5,7},{6,4},{7,5},{8,10},{9,11},{10,... | collective-permute-start | bytes 12296 | tf_op jit(solution)/shard_map/ppermute | solution.py:222
  94.4 1.7 %multiply_cosine_fusion = (f32[512,64]{1,0:T(8,128)S(1)}, f32[512,64]{1,0:T(8,128)}) fusion(f32[64]{0:T(128)S(1)} %negate_power_fusion, f32[512]{0:T(512)S(1)} %bitcast.33), kind=kLoop, calls=%fused_computation.19 | loop fusion | flops 32768 | bytes 264448 | tf_op jit(solution)/shard_map/cos | solution.py:26
  96.1 0.4 collective-permute-done.3
  96.5 1.5 %collective-permute-start.4 = (f32[2,512]{1,0:T(2,128)S(1)}, f32[2,512]{1,0:T(2,128)S(1)}, u32[]{:S(2)}, u32[]{:S(2)}) collective-permute-start(f32[2,512]{1,0:T(2,128)S(1)} %fusion.13), channel_id=1, source_target_pairs={{0,4},{4,0},{1,5},{5,1},{2,6},{6,2},{3,7},{7,3},{8,12},{12,8},{9,1... | collective-permute-start | bytes 12296 | tf_op jit(solution)/shard_map/ppermute | solution.py:452
  98.2 0.6 reshape.167.sink_pos_ref
  98.8 1.4 collective-permute-done.4
  100.2 0.2 multiply_multiply_fusion
  100.4 0.3 reshape.168
  100.7 0.3 reshape.166
  101.0 2.5 %subtract_convert_fusion = (bf16[512,2,64]{2,1,0:T(2,128)(2,1)S(1)}, bf16[512,2,64]{2,1,0:T(2,128)(2,1)S(1)}, bf16[512,2,64]{2,1,0:T(2,128)(2,1)S(1)}, bf16[512,2,64]{2,1,0:T(2,128)(2,1)S(1)}) fusion(f32[512,2,128]{2,1,0:T(2,128)S(1)} %reshape.168, f32[512,64]{1,0:T(8,128)} %get-tuple-element.45, f32[512,64]{1,0:T(8,128)S(1)} %get-tuple-element.44, ...), kind=kLoop, calls=%fused_computation.10 | loop fusion | flops 1048576 | bytes 1835008 | tf_op jit(solution)/shard_map/convert.1
  103.5 0.7 pad_maximum_fusion.2
  104.4 1.5 %collective-permute-start.5 = (bf16[2,256,256]{2,1,0:T(8,128)(2,1)S(1)}, bf16[2,256,256]{2,1,0:T(8,128)(2,1)S(1)}, u32[]{:S(2)}, u32[]{:S(2)}) collective-permute-start(bf16[2,256,256]{2,1,0:T(8,128)(2,1)S(1)} %convert_element_type.31.q_ref.qa_ref), channel_id=1, source_target_pairs={{0,4},{4,0},{1,5},{5,1},{2,6},{6,2},{3,7},{7,3},{8,12},{12,8},{9,1... | collective-permute-start | bytes 786440 | tf_op jit(solution)/shard_map/ppermute | solution.py:452
  106.0 0.8 slice.133
  106.8 0.7 pad_maximum_fusion.3
  107.5 0.9 convert_element_type.32.nk_ref
  108.4 4.3 %shard_map.136 = (f32[2,2,256,128]{3,2,1,0:T(8,128)}, f32[2,2,256,1]{3,2,1,0:T(8,128)}, f32[2,2,256,1]{3,2,1,0:T(8,128)}) custom-call(s32[2]{0:T(128)} %len_ref.5, s32[2]{0:T(128)} %win_ref.5, s32[8]{0:T(128)} %reshape.167.sink_pos_ref, s32[1]{0:T(128)} %bitcast.seq_ref.owner_ref, bf16[2,256,256]{2,1,0:T(8,128)(2,1)} %copy-done, ...), custom_call_target="tpu_custom_call" | custom-call | tf_op jit(solution)/shard_map/pallas_call | solution.py:431
  112.7 0.7 copy-done.1
  113.4 8.8 %shard_map.138 = (bf16[2,128,512]{2,1,0:T(8,128)(2,1)}, f32[2,4,128,2]{3,2,1,0:T(8,128)}) custom-call(s32[2]{0:T(128)} %len_ref.5, s32[2]{0:T(128)} %win_ref.5, s32[1]{0:T(128)} %bitcast.seq_ref.owner_ref, s32[1]{0:T(128)} %bitcast.7.first_ref, s32[1]{0:T(128)} %bitcast.8.owner_ref, bf16[2,256,256]{2,1,0:T(8,128)(2,1)} %copy-done, ...), custom_call_target="tpu_custom_call" | custom-call | tf_op jit(solution)/shard_map/pallas_call | solution.py:571
  122.3 0.6 collective-permute-start.6
  122.8 8.9 %shard_map.137 = (f32[2,128,512]{2,1,0:T(8,128)}, f32[2,4,128,2]{3,2,1,0:T(8,128)}) custom-call(s32[2]{0:T(128)} %len_ref.5, s32[2]{0:T(128)} %win_ref.5, s32[1]{0:T(128)} %bitcast.seq_ref.owner_ref, s32[1]{0:T(128)} %bitcast.1.first_ref, s32[1]{0:T(128)} %bitcast.seq_ref.owner_ref, bf16[2,256,256]{2,1,0:T(8,128)(2,1)} %copy-done, ...), custom_call_target="tpu_custom_call" | custom-call | tf_op jit(solution)/shard_map/pallas_call | solution.py:571
  131.7 1.7 %slice_reduce_fusion.3 = (f32[2,4,128]{2,1,0:T(4,128)S(1)}, f32[2,4,128]{2,1,0:T(4,128)S(1)}) fusion(f32[2,4,128,2]{3,2,1,0:T(8,128)} %get-tuple-element.16), kind=kLoop, calls=%fused_computation.8 | loop fusion | bytes 16384 | tf_op jit(solution)/shard_map/slice | solution.py:600
  133.4 1.5 %collective-permute-start.7 = (bf16[2,128,512]{2,1,0:T(8,128)(2,1)S(1)}, bf16[2,128,512]{2,1,0:T(8,128)(2,1)S(1)}, u32[]{:S(2)}, u32[]{:S(2)}) collective-permute-start(bf16[2,128,512]{2,1,0:T(8,128)(2,1)S(1)} %copy-done.7), channel_id=1, source_target_pairs={{0,4},{4,0},{1,5},{5,1},{2,6},{6,2},{3,7},{7,3},{8,12},{12,8},{9,1... | collective-permute-start | bytes 786440 | tf_op jit(solution)/shard_map/ppermute | solution.py:452
  134.9 0.5 slice_reduce_fusion
  135.6 0.3 div.19
  136.0 0.2 div.20
  136.3 0.3 mul.195
  136.7 0.2 mul.196
  137.0 0.3 mul.191
  137.4 0.2 mul.192
  137.6 2.4 %collective-permute-done.7 = bf16[2,128,512]{2,1,0:T(8,128)(2,1)S(1)} collective-permute-done((bf16[2,128,512]{2,1,0:T(8,128)(2,1)S(1)}, bf16[2,128,512]{2,1,0:T(8,128)(2,1)S(1)}, u32[]{:S(2)}, u32[]{:S(2)}) %collective-permute-start.7) | collective-permute-done | bytes 262176 | tf_op jit(solution)/shard_map/ppermute | solution.py:452
  140.0 0.8 select_convert_fusion
  (42 shorter events, 1.1 us)
Async XLA Ops:
  6.5 80.5 %all-gather.2.cloned.1.call-start = ((), (), s32[]{:S(2)}) async-start(), calls=%async_computation | async-start | bytes 3932160 | tf_op jit(solution)/shard_map/all_gather | solution.py:488
  7.5 14.4 %copy-start.2 = (bf16[2,128,2048]{2,1,0:T(8,128)(2,1)S(1)}, bf16[2,128,2048]{2,1,0:T(8,128)(2,1)}, u32[]{:S(2)}) copy-start(bf16[2,128,2048]{2,1,0:T(8,128)(2,1)} %param.14) | copy-start | bytes 3145732
  8.8 12.1 %collective-permute-start.1 = (bf16[256,768]{1,0:T(8,128)(2,1)S(1)}, bf16[256,768]{1,0:T(8,128)(2,1)S(1)}, u32[]{:S(2)}, u32[]{:S(2)}) collective-permute-start(bf16[256,768]{1,0:T(8,128)(2,1)S(1)} %pad_maximum_fusion.1), channel_id=1, source_target_pairs={{0,4},{4,0},{1,5},{5,1},{2,6},{6,2},{3,7},{7,3},{8,12},{12,8},{9,1... | collective-permute-start | bytes 1179656 | tf_op jit(solution)/shard_map/ppermute | solution.py:452
  20.9 3.6 %copy-start.4 = (s32[2]{0:T(128)S(1)}, s32[2]{0:T(128)}, u32[]{:S(2)}) copy-start(s32[2]{0:T(128)} %len_ref.5) | copy-start | bytes 28
  21.9 24.4 %collective-permute-start = (bf16[2,128,2048]{2,1,0:T(8,128)(2,1)S(1)}, bf16[2,128,2048]{2,1,0:T(8,128)(2,1)S(1)}, u32[]{:S(2)}, u32[]{:S(2)}) collective-permute-start(bf16[2,128,2048]{2,1,0:T(8,128)(2,1)S(1)} %copy-done.2), channel_id=1, source_target_pairs={{0,4},{4,0},{1,5},{5,1},{2,6},{6,2},{3,7},{7,3},{8,12},{12,8},{9,1... | collective-permute-start | bytes 3145736 | tf_op jit(solution)/shard_map/ppermute | solution.py:452
  75.0 23.1 %copy-start.5 = (f32[512]{0:T(512)S(1)}, f32[512]{0:T(512)}, u32[]{:S(2)}) copy-start(f32[512]{0:T(512)} %param.19) | copy-start | bytes 6148
  75.0 23.2 %copy-start.6 = (f32[512]{0:T(512)S(1)}, f32[512]{0:T(512)}, u32[]{:S(2)}) copy-start(f32[512]{0:T(512)} %param.18) | copy-start | bytes 6148
  75.0 23.2 %copy-start.8 = (s32[2,4]{1,0:T(2,128)S(1)}, s32[2,4]{1,0:T(2,128)}, u32[]{:S(2)}) copy-start(s32[2,4]{1,0:T(2,128)} %param.24) | copy-start | bytes 100
  91.6 1.2 collective-permute-start.2
  92.9 3.7 %collective-permute-start.3 = (f32[2,512]{1,0:T(2,128)S(1)}, f32[2,512]{1,0:T(2,128)S(1)}, u32[]{:S(2)}, u32[]{:S(2)}) collective-permute-start(f32[2,512]{1,0:T(2,128)S(1)} %fusion.9), channel_id=1, source_target_pairs={{0,2},{1,3},{2,0},{3,1},{4,6},{5,7},{6,4},{7,5},{8,10},{9,11},{10,... | collective-permute-start | bytes 12296 | tf_op jit(solution)/shard_map/ppermute | solution.py:222
  96.5 3.7 %collective-permute-start.4 = (f32[2,512]{1,0:T(2,128)S(1)}, f32[2,512]{1,0:T(2,128)S(1)}, u32[]{:S(2)}, u32[]{:S(2)}) collective-permute-start(f32[2,512]{1,0:T(2,128)S(1)} %fusion.13), channel_id=1, source_target_pairs={{0,4},{4,0},{1,5},{5,1},{2,6},{6,2},{3,7},{7,3},{8,12},{12,8},{9,1... | collective-permute-start | bytes 12296 | tf_op jit(solution)/shard_map/ppermute | solution.py:452
  101.0 4.9 %copy-start.9 = (s32[2]{0:T(128)S(1)}, s32[2]{0:T(128)}, u32[]{:S(2)}) copy-start(s32[2]{0:T(128)} %param.26) | copy-start | bytes 28
  104.4 4.0 %copy-start = (bf16[2,256,256]{2,1,0:T(8,128)(2,1)}, bf16[2,256,256]{2,1,0:T(8,128)(2,1)S(1)}, u32[]{:S(2)}) copy-start(bf16[2,256,256]{2,1,0:T(8,128)(2,1)S(1)} %convert_element_type.31.q_ref.qa_ref) | copy-start | bytes 786436
  104.4 8.3 %collective-permute-start.5 = (bf16[2,256,256]{2,1,0:T(8,128)(2,1)S(1)}, bf16[2,256,256]{2,1,0:T(8,128)(2,1)S(1)}, u32[]{:S(2)}, u32[]{:S(2)}) collective-permute-start(bf16[2,256,256]{2,1,0:T(8,128)(2,1)S(1)} %convert_element_type.31.q_ref.qa_ref), channel_id=1, source_target_pairs={{0,4},{4,0},{1,5},{5,1},{2,6},{6,2},{3,7},{7,3},{8,12},{12,8},{9,1... | collective-permute-start | bytes 786440 | tf_op jit(solution)/shard_map/ppermute | solution.py:452
  112.7 0.7 copy-start.1
  122.3 12.7 %collective-permute-start.6 = (f32[2,4,128,2]{3,2,1,0:T(8,128)}, f32[2,4,128,2]{3,2,1,0:T(8,128)S(1)}, u32[]{:S(2)}, u32[]{:S(2)}) collective-permute-start(f32[2,4,128,2]{3,2,1,0:T(8,128)} %get-tuple-element.17), channel_id=1, source_target_pairs={{0,4},{4,0},{1,5},{5,1},{2,6},{6,2},{3,7},{7,3},{8,12},{12,8},{9,1... | collective-permute-start | bytes 24584 | tf_op jit(solution)/shard_map/ppermute | solution.py:452
  122.8 10.6 %copy-start.7 = (bf16[2,128,512]{2,1,0:T(8,128)(2,1)S(1)}, bf16[2,128,512]{2,1,0:T(8,128)(2,1)}, u32[]{:S(2)}) copy-start(bf16[2,128,512]{2,1,0:T(8,128)(2,1)} %get-tuple-element.18) | copy-start | bytes 786436
  133.4 6.6 %collective-permute-start.7 = (bf16[2,128,512]{2,1,0:T(8,128)(2,1)S(1)}, bf16[2,128,512]{2,1,0:T(8,128)(2,1)S(1)}, u32[]{:S(2)}, u32[]{:S(2)}) collective-permute-start(bf16[2,128,512]{2,1,0:T(8,128)(2,1)S(1)} %copy-done.7), channel_id=1, source_target_pairs={{0,4},{4,0},{1,5},{5,1},{2,6},{6,2},{3,7},{7,3},{8,12},{12,8},{9,1... | collective-permute-start | bytes 786440 | tf_op jit(solution)/shard_map/ppermute | solution.py:452
  136.2 3.8 %copy-start.3 = (f32[2,128,512]{2,1,0:T(8,128)S(1)}, f32[2,128,512]{2,1,0:T(8,128)}, u32[]{:S(2)}) copy-start(f32[2,128,512]{2,1,0:T(8,128)} %get-tuple-element.15) | copy-start | bytes 1572868
Sparse Core Ops, SparseCore 0:
  22.0 64.9 all-gather.1

commit v7 on v6

--- a/solution.py
+++ b/solution.py
@@ -332,7 +332,7 @@
     allowed = key <= row
     row_1 = lax.broadcasted_iota(jnp.int32, (rows, 1), 0)
     edge = length_now + row_1 - window_now
-    sink_ok = [sink_pos_ref[r * SINKS + sink] <= edge for sink in range(SINKS)]
+    sink_ok = [sink_pos_ref[r, sink] <= edge for sink in range(SINKS)]
     for h in range(heads):
         cols = slice(h * HEAD_DIM, (h + 1) * HEAD_DIM)
         queries = q_ref[0, :, cols]
@@ -523,7 +523,7 @@
     sink_block = lambda r, len_ref, win_ref, pos_ref, seq_ref: (r, 0, seq_ref[0])
     span_part = pair_partials(
         pair_span_kernel,
-        (cache_len, window_len, sink_pos.reshape(-1), seq_arr),
+        (cache_len, window_len, sink_pos, seq_arr),
         None,
         (q_half, k_half, v_half, sink_keys, sink_values),
         [

time: 148 us -> 148 us (level)
  no operation moved by 1% of the time
where the time goes in v7:
time: 148 us
  waiting for transfers between devices  48.8 us (33%)
  local copies, waits for them, and re-layouts  29.7 us (20%)
  Pallas kernels  22.1 us (15%)
  other arithmetic  17.6 us (12%)
  between operations  13.7 us (9%)
  starting transfers between devices  11.6 us (8%)
  matrix products  4.3 us (3%)
    ppermute x6, waiting for transfers between devices, swap_seq(): return lax.ppermute(x, 'seq', [(0, 1), (1, 0)])  35.2 us
    pallas_call x2, Pallas kernels, cache_rows(): pl.pallas_call(functools.partial(merged_cache_kernel, scaling=HEAD_DIM **...  17.7 us
    rev x1, local copies, waits for them, and re-layouts, on_device_pair(): blocks[:, :, :, ::-1, :]  15.3 us
    all_gather x1, waiting for transfers between devices, on_device_pair(): lax.all_gather(jnp.concatenate([mine, got], 0), 'req', axis=0, tiled=True)  12 us
    ppermute x6, starting transfers between devices, swap_seq(): return lax.ppermute(x, 'seq', [(0, 1), (1, 0)])  9.97 us
    select_n x1, other arithmetic, on_device_pair(): jnp.where(first, jnp.concatenate([tokens, tokens_other], axis=1), jnp.con...  5.75 us
    another operation x1, local copies, waits for them, and re-layouts, on_device_pair(): token_rows = tokens_all.reshape(req_local * span_total, model_width)  4.49 us
    pallas_call x1, Pallas kernels, pair_partials(): pl.pallas_call(functools.partial(kernel, scaling=HEAD_DIM ** (-0.5)), gri...  4.35 us
  transfers between devices with their start and end apart: 9, of which 7 were waited for; matrix products, arithmetic and copies ran while one was open for 26% of the time, Pallas kernels for 9%

profile of v7, /device:TPU:0, one launch (start us, length us, event | category | flops | bytes accessed | tf_op | source)
XLA Modules:
  0.0 147.7 jit_solution(14249061895419150357)
XLA Ops:
  6.5 1.0 broadcast_select_fusion.7
  7.5 1.2 broadcast_select_fusion.5
  8.8 3.0 %collective-permute-start.1 = (bf16[256,768]{1,0:T(8,128)(2,1)S(1)}, bf16[256,768]{1,0:T(8,128)(2,1)S(1)}, u32[]{:S(2)}, u32[]{:S(2)}) collective-permute-start(bf16[256,768]{1,0:T(8,128)(2,1)S(1)} %pad_maximum_fusion.1), channel_id=1, source_target_pairs={{0,4},{4,0},{1,5},{5,1},{2,6},{6,2},{3,7},{7,3},{8,12},{12,8},{9,1... | collective-permute-start | bytes 1179656 | tf_op jit(solution)/shard_map/ppermute | solution.py:452
  11.8 9.1 %collective-permute-done.1 = bf16[256,768]{1,0:T(8,128)(2,1)S(1)} collective-permute-done((bf16[256,768]{1,0:T(8,128)(2,1)S(1)}, bf16[256,768]{1,0:T(8,128)(2,1)S(1)}, u32[]{:S(2)}, u32[]{:S(2)}) %collective-permute-start.1) | collective-permute-done | bytes 393248 | tf_op jit(solution)/shard_map/ppermute | solution.py:452
  20.9 0.9 pad_maximum_fusion
  21.9 1.8 %collective-permute-start = (bf16[2,128,2048]{2,1,0:T(8,128)(2,1)S(1)}, bf16[2,128,2048]{2,1,0:T(8,128)(2,1)S(1)}, u32[]{:S(2)}, u32[]{:S(2)}) collective-permute-start(bf16[2,128,2048]{2,1,0:T(8,128)(2,1)S(1)} %copy-done.2), channel_id=1, source_target_pairs={{0,4},{4,0},{1,5},{5,1},{2,6},{6,2},{3,7},{7,3},{8,12},{12,8},{9,1... | collective-permute-start | bytes 3145736 | tf_op jit(solution)/shard_map/ppermute | solution.py:452
  23.7 0.8 concatenate.29
  24.6 21.7 %collective-permute-done = bf16[2,128,2048]{2,1,0:T(8,128)(2,1)S(1)} collective-permute-done((bf16[2,128,2048]{2,1,0:T(8,128)(2,1)S(1)}, bf16[2,128,2048]{2,1,0:T(8,128)(2,1)S(1)}, u32[]{:S(2)}, u32[]{:S(2)}) %collective-permute-start) | collective-permute-done | bytes 1048608 | tf_op jit(solution)/shard_map/ppermute | solution.py:452
  46.3 1.6 %concatenate.30 = bf16[2,128,4,2,256]{4,3,2,1,0:T(2,128)(2,1)} reshape(bf16[2,128,2048]{2,1,0:T(8,128)(2,1)S(1)} %collective-permute-done) | data formatting | bytes 2097152 | tf_op jit(solution)/shard_map/concatenate | solution.py:492
  47.9 5.7 %broadcast_select_fusion.1 = bf16[2,256,4,2,256]{4,3,2,1,0:T(2,128)(2,1)S(1)} fusion(pred[]{:T(512)S(6)} %eq.3, bf16[2,128,4,2,256]{4,3,2,1,0:T(2,128)(2,1)} %concatenate.30, bf16[2,128,4,2,256]{4,3,2,1,0:T(2,128)(2,1)S(1)} %concatenate.29), kind=kLoop, calls=%fused_computation.1 | loop fusion | flops 3145728 | bytes 4194305 | tf_op jit(solution)/shard_map/jit(_where)/select_n | solution.py:490
  53.6 15.3 %rev.3 = bf16[2,256,4,2,256]{4,3,2,1,0:T(2,128)(2,1)} reverse(bf16[2,256,4,2,256]{4,3,2,1,0:T(2,128)(2,1)S(1)} %broadcast_select_fusion.1), dimensions={3} | reverse | bytes 4194304 | tf_op jit(solution)/shard_map/rev | solution.py:497
  69.0 1.6 %broadcast_select_fusion = bf16[2,256,1,8,256]{4,3,2,1,0:T(8,128)(2,1)} fusion(bf16[2,256,1,8,256]{4,3,2,1,0:T(8,128)(2,1)S(1)} %bitcast.23, bf16[2,256,1,8,256]{4,3,2,1,0:T(8,128)(2,1)} %bitcast.25, pred[]{:T(512)S(6)} %eq.3), kind=kLoop, calls=%fused_computation | loop fusion | flops 1048576 | bytes 6291457 | tf_op jit(solution)/shard_map/jit(_where)/select_n | solution.py:497
  70.5 4.5 %reshape_reshape.3 = bf16[512,2048]{1,0:T(8,128)(2,1)} reshape(bf16[2,256,4,2,256]{4,3,2,1,0:T(2,128)(2,1)} %bitcast.24) | data formatting | bytes 4194304 | tf_op jit(solution)/shard_map/reshape;reshape | solution.py:498
  75.0 12.0 %all-gather.2.cloned.1.call-done = bf16[2048,768]{1,0:T(8,128)(2,1)} async-done(((bf16[512,768]{1,0:T(8,128)(2,1)}), bf16[2048,768]{1,0:T(8,128)(2,1)}) %all-gather.2.cloned.1.call-update) | async-done | bytes 3145744 | tf_op jit(solution)/shard_map/all_gather | solution.py:488
  87.0 4.3 %fusion.10 = f32[512,768]{1,0:T(8,128)S(1)} fusion(bf16[512,2048]{1,0:T(8,128)(2,1)} %reshape_reshape.3, bf16[2048,768]{1,0:T(8,128)(2,1)} %all-gather.2.cloned.1.call-done), kind=kOutput, calls=%fused_computation.48 | convolution fusion | flops 1610612736 | bytes 6815744 | tf_op jit(solution)/shard_map/dot_general | solution.py:499
  91.4 0.2 multiply_reduce_fusion.1
  91.7 1.1 collective-permute-done.2
  92.8 1.5 %collective-permute-start.3 = (f32[2,512]{1,0:T(2,128)S(1)}, f32[2,512]{1,0:T(2,128)S(1)}, u32[]{:S(2)}, u32[]{:S(2)}) collective-permute-start(f32[2,512]{1,0:T(2,128)S(1)} %fusion.9), channel_id=1, source_target_pairs={{0,2},{1,3},{2,0},{3,1},{4,6},{5,7},{6,4},{7,5},{8,10},{9,11},{10,... | collective-permute-start | bytes 12296 | tf_op jit(solution)/shard_map/ppermute | solution.py:222
  94.4 1.7 %multiply_cosine_fusion = (f32[512,64]{1,0:T(8,128)S(1)}, f32[512,64]{1,0:T(8,128)}) fusion(f32[64]{0:T(128)S(1)} %negate_power_fusion, f32[512]{0:T(512)S(1)} %bitcast.33), kind=kLoop, calls=%fused_computation.19 | loop fusion | flops 32768 | bytes 264448 | tf_op jit(solution)/shard_map/cos | solution.py:26
  96.1 0.4 collective-permute-done.3
  96.5 1.5 %collective-permute-start.4 = (f32[2,512]{1,0:T(2,128)S(1)}, f32[2,512]{1,0:T(2,128)S(1)}, u32[]{:S(2)}, u32[]{:S(2)}) collective-permute-start(f32[2,512]{1,0:T(2,128)S(1)} %fusion.13), channel_id=1, source_target_pairs={{0,4},{4,0},{1,5},{5,1},{2,6},{6,2},{3,7},{7,3},{8,12},{12,8},{9,1... | collective-permute-start | bytes 12296 | tf_op jit(solution)/shard_map/ppermute | solution.py:452
  98.2 2.0 %collective-permute-done.4 = f32[2,512]{1,0:T(2,128)S(1)} collective-permute-done((f32[2,512]{1,0:T(2,128)S(1)}, f32[2,512]{1,0:T(2,128)S(1)}, u32[]{:S(2)}, u32[]{:S(2)}) %collective-permute-start.4) | collective-permute-done | bytes 4128 | tf_op jit(solution)/shard_map/ppermute | solution.py:452
  100.2 0.2 multiply_multiply_fusion
  100.4 0.3 reshape.164
  100.7 0.3 reshape.163
  101.0 2.5 %subtract_convert_fusion = (bf16[512,2,64]{2,1,0:T(2,128)(2,1)S(1)}, bf16[512,2,64]{2,1,0:T(2,128)(2,1)S(1)}, bf16[512,2,64]{2,1,0:T(2,128)(2,1)S(1)}, bf16[512,2,64]{2,1,0:T(2,128)(2,1)S(1)}) fusion(f32[512,2,128]{2,1,0:T(2,128)S(1)} %reshape.164, f32[512,64]{1,0:T(8,128)} %get-tuple-element.45, f32[512,64]{1,0:T(8,128)S(1)} %get-tuple-element.44, ...), kind=kLoop, calls=%fused_computation.10 | loop fusion | flops 1048576 | bytes 1835008 | tf_op jit(solution)/shard_map/convert.1
  103.5 0.7 pad_maximum_fusion.2
  104.2 0.2 convert_element_type.31.q_ref.qa_ref
  104.4 1.5 %collective-permute-start.5 = (bf16[2,256,256]{2,1,0:T(8,128)(2,1)S(1)}, bf16[2,256,256]{2,1,0:T(8,128)(2,1)S(1)}, u32[]{:S(2)}, u32[]{:S(2)}) collective-permute-start(bf16[2,256,256]{2,1,0:T(8,128)(2,1)S(1)} %convert_element_type.31.q_ref.qa_ref), channel_id=1, source_target_pairs={{0,4},{4,0},{1,5},{5,1},{2,6},{6,2},{3,7},{7,3},{8,12},{12,8},{9,1... | collective-permute-start | bytes 786440 | tf_op jit(solution)/shard_map/ppermute | solution.py:452
  106.0 0.8 slice.133
  106.7 0.7 pad_maximum_fusion.3
  107.5 0.9 convert_element_type.32.nk_ref
  108.3 4.4 %shard_map.136 = (f32[2,2,256,128]{3,2,1,0:T(8,128)}, f32[2,2,256,1]{3,2,1,0:T(8,128)}, f32[2,2,256,1]{3,2,1,0:T(8,128)}) custom-call(s32[2]{0:T(128)} %len_ref.5, s32[2]{0:T(128)} %win_ref.5, s32[2,4]{1,0:T(2,128)} %sink_pos_ref.1, s32[1]{0:T(128)} %bitcast.seq_ref.owner_ref, bf16[2,256,256]{2,1,0:T(8,128)(2,1)} %copy-done, ...), custom_call_target="tpu_custom_call" | custom-call | tf_op jit(solution)/shard_map/pallas_call | solution.py:431
  112.7 0.7 copy-done.1
  113.4 8.8 %shard_map.138 = (bf16[2,128,512]{2,1,0:T(8,128)(2,1)}, f32[2,4,128,2]{3,2,1,0:T(8,128)}) custom-call(s32[2]{0:T(128)} %len_ref.5, s32[2]{0:T(128)} %win_ref.5, s32[1]{0:T(128)} %bitcast.seq_ref.owner_ref, s32[1]{0:T(128)} %bitcast.7.first_ref, s32[1]{0:T(128)} %bitcast.8.owner_ref, bf16[2,256,256]{2,1,0:T(8,128)(2,1)} %copy-done, ...), custom_call_target="tpu_custom_call" | custom-call | tf_op jit(solution)/shard_map/pallas_call | solution.py:571
  122.2 0.6 collective-permute-start.6
  122.8 8.9 %shard_map.137 = (f32[2,128,512]{2,1,0:T(8,128)}, f32[2,4,128,2]{3,2,1,0:T(8,128)}) custom-call(s32[2]{0:T(128)} %len_ref.5, s32[2]{0:T(128)} %win_ref.5, s32[1]{0:T(128)} %bitcast.seq_ref.owner_ref, s32[1]{0:T(128)} %bitcast.1.first_ref, s32[1]{0:T(128)} %bitcast.seq_ref.owner_ref, bf16[2,256,256]{2,1,0:T(8,128)(2,1)} %copy-done, ...), custom_call_target="tpu_custom_call" | custom-call | tf_op jit(solution)/shard_map/pallas_call | solution.py:571
  131.7 1.7 %slice_reduce_fusion.3 = (f32[2,4,128]{2,1,0:T(4,128)S(1)}, f32[2,4,128]{2,1,0:T(4,128)S(1)}) fusion(f32[2,4,128,2]{3,2,1,0:T(8,128)} %get-tuple-element.16), kind=kLoop, calls=%fused_computation.8 | loop fusion | bytes 16384 | tf_op jit(solution)/shard_map/slice | solution.py:600
  133.4 1.5 %collective-permute-start.7 = (bf16[2,128,512]{2,1,0:T(8,128)(2,1)S(1)}, bf16[2,128,512]{2,1,0:T(8,128)(2,1)S(1)}, u32[]{:S(2)}, u32[]{:S(2)}) collective-permute-start(bf16[2,128,512]{2,1,0:T(8,128)(2,1)S(1)} %copy-done.7), channel_id=1, source_target_pairs={{0,4},{4,0},{1,5},{5,1},{2,6},{6,2},{3,7},{7,3},{8,12},{12,8},{9,1... | collective-permute-start | bytes 786440 | tf_op jit(solution)/shard_map/ppermute | solution.py:452
  134.9 0.5 slice_reduce_fusion
  135.6 0.3 div.19
  136.0 0.2 div.20
  136.3 0.3 mul.195
  136.7 0.2 mul.196
  137.0 0.3 mul.191
  137.4 0.2 mul.192
  137.6 2.4 %collective-permute-done.7 = bf16[2,128,512]{2,1,0:T(8,128)(2,1)S(1)} collective-permute-done((bf16[2,128,512]{2,1,0:T(8,128)(2,1)S(1)}, bf16[2,128,512]{2,1,0:T(8,128)(2,1)S(1)}, u32[]{:S(2)}, u32[]{:S(2)}) %collective-permute-start.7) | collective-permute-done | bytes 262176 | tf_op jit(solution)/shard_map/ppermute | solution.py:452
  140.0 0.8 select_convert_fusion
  (39 shorter events, 0.9 us)
Async XLA Ops:
  6.5 80.5 %all-gather.2.cloned.1.call-start = ((), (), s32[]{:S(2)}) async-start(), calls=%async_computation | async-start | bytes 3932160 | tf_op jit(solution)/shard_map/all_gather | solution.py:488
  7.5 14.4 %copy-start.2 = (bf16[2,128,2048]{2,1,0:T(8,128)(2,1)S(1)}, bf16[2,128,2048]{2,1,0:T(8,128)(2,1)}, u32[]{:S(2)}) copy-start(bf16[2,128,2048]{2,1,0:T(8,128)(2,1)} %param.14) | copy-start | bytes 3145732
  8.8 12.1 %collective-permute-start.1 = (bf16[256,768]{1,0:T(8,128)(2,1)S(1)}, bf16[256,768]{1,0:T(8,128)(2,1)S(1)}, u32[]{:S(2)}, u32[]{:S(2)}) collective-permute-start(bf16[256,768]{1,0:T(8,128)(2,1)S(1)} %pad_maximum_fusion.1), channel_id=1, source_target_pairs={{0,4},{4,0},{1,5},{5,1},{2,6},{6,2},{3,7},{7,3},{8,12},{12,8},{9,1... | collective-permute-start | bytes 1179656 | tf_op jit(solution)/shard_map/ppermute | solution.py:452
  20.9 3.6 %copy-start.4 = (s32[2]{0:T(128)S(1)}, s32[2]{0:T(128)}, u32[]{:S(2)}) copy-start(s32[2]{0:T(128)} %len_ref.5) | copy-start | bytes 28
  21.9 24.4 %collective-permute-start = (bf16[2,128,2048]{2,1,0:T(8,128)(2,1)S(1)}, bf16[2,128,2048]{2,1,0:T(8,128)(2,1)S(1)}, u32[]{:S(2)}, u32[]{:S(2)}) collective-permute-start(bf16[2,128,2048]{2,1,0:T(8,128)(2,1)S(1)} %copy-done.2), channel_id=1, source_target_pairs={{0,4},{4,0},{1,5},{5,1},{2,6},{6,2},{3,7},{7,3},{8,12},{12,8},{9,1... | collective-permute-start | bytes 3145736 | tf_op jit(solution)/shard_map/ppermute | solution.py:452
  75.0 23.0 %copy-start.5 = (f32[512]{0:T(512)S(1)}, f32[512]{0:T(512)}, u32[]{:S(2)}) copy-start(f32[512]{0:T(512)} %param.19) | copy-start | bytes 6148
  75.0 23.1 %copy-start.6 = (f32[512]{0:T(512)S(1)}, f32[512]{0:T(512)}, u32[]{:S(2)}) copy-start(f32[512]{0:T(512)} %param.18) | copy-start | bytes 6148
  91.6 1.2 collective-permute-start.2
  92.8 3.7 %collective-permute-start.3 = (f32[2,512]{1,0:T(2,128)S(1)}, f32[2,512]{1,0:T(2,128)S(1)}, u32[]{:S(2)}, u32[]{:S(2)}) collective-permute-start(f32[2,512]{1,0:T(2,128)S(1)} %fusion.9), channel_id=1, source_target_pairs={{0,2},{1,3},{2,0},{3,1},{4,6},{5,7},{6,4},{7,5},{8,10},{9,11},{10,... | collective-permute-start | bytes 12296 | tf_op jit(solution)/shard_map/ppermute | solution.py:222
  96.5 3.7 %collective-permute-start.4 = (f32[2,512]{1,0:T(2,128)S(1)}, f32[2,512]{1,0:T(2,128)S(1)}, u32[]{:S(2)}, u32[]{:S(2)}) collective-permute-start(f32[2,512]{1,0:T(2,128)S(1)} %fusion.13), channel_id=1, source_target_pairs={{0,4},{4,0},{1,5},{5,1},{2,6},{6,2},{3,7},{7,3},{8,12},{12,8},{9,1... | collective-permute-start | bytes 12296 | tf_op jit(solution)/shard_map/ppermute | solution.py:452
  101.0 4.9 %copy-start.8 = (s32[2]{0:T(128)S(1)}, s32[2]{0:T(128)}, u32[]{:S(2)}) copy-start(s32[2]{0:T(128)} %param.26) | copy-start | bytes 28
  104.4 4.0 %copy-start = (bf16[2,256,256]{2,1,0:T(8,128)(2,1)}, bf16[2,256,256]{2,1,0:T(8,128)(2,1)S(1)}, u32[]{:S(2)}) copy-start(bf16[2,256,256]{2,1,0:T(8,128)(2,1)S(1)} %convert_element_type.31.q_ref.qa_ref) | copy-start | bytes 786436
  104.4 8.3 %collective-permute-start.5 = (bf16[2,256,256]{2,1,0:T(8,128)(2,1)S(1)}, bf16[2,256,256]{2,1,0:T(8,128)(2,1)S(1)}, u32[]{:S(2)}, u32[]{:S(2)}) collective-permute-start(bf16[2,256,256]{2,1,0:T(8,128)(2,1)S(1)} %convert_element_type.31.q_ref.qa_ref), channel_id=1, source_target_pairs={{0,4},{4,0},{1,5},{5,1},{2,6},{6,2},{3,7},{7,3},{8,12},{12,8},{9,1... | collective-permute-start | bytes 786440 | tf_op jit(solution)/shard_map/ppermute | solution.py:452
  112.7 0.7 copy-start.1
  122.2 12.7 %collective-permute-start.6 = (f32[2,4,128,2]{3,2,1,0:T(8,128)}, f32[2,4,128,2]{3,2,1,0:T(8,128)S(1)}, u32[]{:S(2)}, u32[]{:S(2)}) collective-permute-start(f32[2,4,128,2]{3,2,1,0:T(8,128)} %get-tuple-element.17), channel_id=1, source_target_pairs={{0,4},{4,0},{1,5},{5,1},{2,6},{6,2},{3,7},{7,3},{8,12},{12,8},{9,1... | collective-permute-start | bytes 24584 | tf_op jit(solution)/shard_map/ppermute | solution.py:452
  122.8 10.6 %copy-start.7 = (bf16[2,128,512]{2,1,0:T(8,128)(2,1)S(1)}, bf16[2,128,512]{2,1,0:T(8,128)(2,1)}, u32[]{:S(2)}) copy-start(bf16[2,128,512]{2,1,0:T(8,128)(2,1)} %get-tuple-element.18) | copy-start | bytes 786436
  133.4 6.6 %collective-permute-start.7 = (bf16[2,128,512]{2,1,0:T(8,128)(2,1)S(1)}, bf16[2,128,512]{2,1,0:T(8,128)(2,1)S(1)}, u32[]{:S(2)}, u32[]{:S(2)}) collective-permute-start(bf16[2,128,512]{2,1,0:T(8,128)(2,1)S(1)} %copy-done.7), channel_id=1, source_target_pairs={{0,4},{4,0},{1,5},{5,1},{2,6},{6,2},{3,7},{7,3},{8,12},{12,8},{9,1... | collective-permute-start | bytes 786440 | tf_op jit(solution)/shard_map/ppermute | solution.py:452
  136.2 3.8 %copy-start.3 = (f32[2,128,512]{2,1,0:T(8,128)S(1)}, f32[2,128,512]{2,1,0:T(8,128)}, u32[]{:S(2)}) copy-start(f32[2,128,512]{2,1,0:T(8,128)} %get-tuple-element.15) | copy-start | bytes 1572868
Sparse Core Ops, SparseCore 0:
  22.0 64.9 all-gather.1
